TPU v7x, 32 devices: a whole 2x2x4 slice. The times are simulated.
32 devices in a mesh: year: 8 (over z, x), region: 4 (over y, core).
Axes of the slice: x: 2, y: 2, z: 4, core: 2. Of those that a mesh axis runs over, the one named last changes fastest.
Arguments:
- daily_temps: bfloat16 [8, 22, 512], P('year', None, 'region'), may hold values from -6 to 6
- land_mask: int32 [512], P('region'), may hold values 0 or 1
Outputs:
- coarse_threshold: float32 [8, 512], P('year', 'region')
- refined_threshold: float32 [8, 512], P('year', 'region')
All inputs are finite; a program needn't handle non-finite values. No bound on the sum of `land_mask` on one device may be relied on, other than what follows from the above.
Results may differ from a plain program's by a relative error of at most 0.0013.
Values may be sent and summed in bfloat16 or wider, within the bound.
No kernel may reach another device: no remote copies, remote signals or barrier semaphores. Data moves between devices by JAX's collectives and lax.ppermute only.
A program may use at most 64 MiB of HBM per device.

v0:
```python
import jax
import jax.numpy as jnp
from jax import lax
from jax.sharding import PartitionSpec as P

WIN = 15
BINS = 256


VALUE_RANGE = 12.8
QUANT_LEVEL = 0.9
SHARPNESS = 32.0
KERNEL_SCALE = 0.25
STEP_SIZE = 2.0


def extended_2(array, sides, width):
    for axis, dim in sides:
        devices, length = (lax.axis_size(axis), array.shape[dim])
        up = [(i, (i + 1) % devices) for i in range(devices)]
        down = [(j, i) for i, j in up]
        last = lax.slice_in_dim(array, length - width, length, axis=dim)
        leading = lax.slice_in_dim(array, 0, width, axis=dim)
        before = lax.ppermute(last, axis, up)
        after = lax.ppermute(leading, axis, down)
        array = jnp.concatenate([before, array, after], axis=dim)
    return array


def smooth_field(extended, flags):
    center = extended[..., 1:-1]
    same_west = 1.0 - jnp.abs(flags[1:-1] - flags[:-2])
    same_east = 1.0 - jnp.abs(flags[1:-1] - flags[2:])
    mixed = center + same_west * extended[..., :-2] + same_east * extended[..., 2:]
    return (mixed / (1.0 + same_west + same_east)).astype(jnp.bfloat16)


def bin_weights(year_field, bin_count):
    width = VALUE_RANGE / bin_count
    scaled = jnp.clip(
        (year_field.astype(jnp.float32) + 0.5 * VALUE_RANGE) / width, 0.0, bin_count - 1.0
    )
    centers = jnp.arange(bin_count, dtype=jnp.float32)
    return jnp.maximum(0.0, 1.0 - jnp.abs(scaled[..., None] - centers)).astype(jnp.bfloat16)


def quantile(histogram, count_all, bin_count):
    width = VALUE_RANGE / bin_count
    cumulative = jnp.cumsum(histogram, axis=-1)
    ranks = jnp.clip(0.5 + SHARPNESS * (QUANT_LEVEL - cumulative / count_all), 0.0, 1.0)
    return -0.5 * VALUE_RANGE + width * jnp.sum(ranks, axis=-1)


def day_band(row_count, days_in):
    row_day = lax.broadcasted_iota(jnp.int32, (row_count, days_in), 0)
    column_day = lax.broadcasted_iota(jnp.int32, (row_count, days_in), 1)
    inside = (column_day >= row_day) & (column_day < row_day + WIN)
    return jnp.where(inside, 1.0, 0.0).astype(jnp.bfloat16)


def window_cdf(threshold, year_field):
    cal_days = threshold.shape[0]
    samples = year_field.astype(jnp.float32)
    running = jnp.zeros(threshold.shape, jnp.float32)
    for offset in range(WIN):
        window = samples[:, offset : offset + cal_days, :]
        running = running + jnp.sum(
            jax.nn.sigmoid((threshold[None] - window) / KERNEL_SCALE), axis=0
        )
    return running


def shards(daily_temps, land_mask):
    days_in = daily_temps.shape[1]
    lon_cells = daily_temps.shape[2]
    year_count = lax.axis_size("year")
    cal_days = days_in - WIN + 1
    cal_own = cal_days // year_count
    count_all = float(year_count * WIN)
    flag_row = land_mask.astype(jnp.bfloat16)[None, :]
    stacked = jnp.concatenate([daily_temps[0], flag_row], axis=0)
    extended = extended_2(stacked, (("region", 1),), 1)
    smoothed = smooth_field(
        extended[:days_in].astype(jnp.float32), extended[days_in].astype(jnp.float32)
    )
    weights = bin_weights(smoothed, BINS).reshape(days_in, lon_cells * BINS)
    own_rows = lax.psum_scatter(
        jnp.dot(
            day_band(cal_own * lax.axis_size("year"), days_in),
            weights,
            preferred_element_type=jnp.float32,
        ),
        "year",
        scatter_dimension=0,
        tiled=True,
    )
    coarse = quantile(own_rows.reshape(cal_own, lon_cells, BINS), count_all, BINS)
    coarse_all = lax.all_gather(coarse, "year", axis=0, tiled=True)
    partial_cdf = window_cdf(coarse_all, smoothed[None])
    cdf_whole = lax.psum(partial_cdf, "year")
    own_cdf = lax.dynamic_slice_in_dim(cdf_whole, lax.axis_index("year") * cal_own, cal_own, 0)
    refined = coarse - STEP_SIZE * (own_cdf / count_all - QUANT_LEVEL)
    return (coarse, refined)


def solution(mesh):
    return jax.shard_map(
        shards,
        mesh=mesh,
        in_specs=(P("year", None, "region"), P("region")),
        out_specs=(P("year", "region"), P("year", "region")),
        check_vma=False,
    )
```

profile of v0, /device:TPU:0, one launch (start us, length us, event | category | flops | bytes accessed | tf_op | source)
XLA Modules:
  0.0 145.1 jit_solution(3068982300265254493)
XLA Ops:
  7.2 0.7 convert_bitcast_fusion.1
  7.9 0.8 slice_maximum_fusion
  8.7 2.4 %collective-permute-start.1 = (bf16[23,1]{1,0:T(8,128)(2,1)S(1)}, bf16[23,1]{1,0:T(8,128)(2,1)S(1)}, u32[]{:S(2)}, u32[]{:S(2)}) collective-permute-start(bf16[23,1]{1,0:T(8,128)(2,1)S(1)} %get-tuple-element.9), channel_id=1, source_target_pairs={{1,0},{2,1},{3,2},{0,3},{5,4},{6,5},{7,6},{4,7},{9,8},{10,9},{11,1... | collective-permute-start | bytes 146 | tf_op jit(solution)/shard_map/ppermute | solution.py:25
  11.2 0.1 copy.8
  11.2 1.2 collective-permute-done.1
  12.5 1.7 %collective-permute-done = bf16[23,1]{1,0:T(8,128)(2,1)S(1)} collective-permute-done((bf16[23,1]{1,0:T(8,128)(2,1)S(1)}, bf16[23,1]{1,0:T(8,128)(2,1)S(1)}, u32[]{:S(2)}, u32[]{:S(2)}) %collective-permute-start) | collective-permute-done | bytes 78 | tf_op jit(solution)/shard_map/ppermute | solution.py:24
  14.2 0.8 maximum_convert_fusion.2
  14.9 0.1 bitcast_add_fusion
  15.0 0.1 subtract_bitcast_fusion.1
  15.1 0.8 pad_maximum_fusion
  15.9 0.1 convert_bitcast_fusion
  16.0 0.4 sub.122
  16.4 0.3 pad.12
  16.8 1.8 %copy.7 = f32[3,8,128,256]{3,1,2,0:T(8,128)S(1)} copy(f32[3,8,128,256]{3,2,1,0:T(8,128)S(1)} %bitcast.36) | data formatting | bytes 6291456
  18.6 1.8 %fusion = f32[8,32768]{1,0:T(8,128)} fusion(f32[22,32768]{1,0:T(8,128)S(1)} %bitcast.35, f32[32768]{0:T(1024)S(1)} %bitcast.37, s32[8]{0:T(128)S(1)} %iota_add_fusion), kind=kOutput, calls=%fused_computation.1 | convolution fusion | flops 15139696 | bytes 4063264 | tf_op jit(solution)/shard_map/dot_general | solution.py:88
  20.5 0.6 dynamic-slice
  21.1 77.9 %all-reduce.3.cloned.1.call-done = f32[8,32768]{1,0:T(8,128)} async-done(((f32[8,32768]{1,0:T(8,128)}), f32[8,32768]{1,0:T(8,128)}) %all-reduce.3.cloned.1.call-update) | async-done | bytes 1048592
  99.0 2.0 %constant_dynamic-slice_fusion = f32[1,32768]{1,0:T(1,128)S(1)} fusion(f32[8,32768]{1,0:T(8,128)} %all-reduce.3.cloned.1.call-done, u32[]{:T(128)} %bitcast.13), kind=kLoop, calls=%fused_computation.140 | loop fusion | bytes 262148
  101.0 0.1 copy.6
  101.1 0.1 fusion.112
  101.3 0.2 clamp_reduce_fusion
  101.4 19.1 %all-gather.1 = f32[8,1,128]{2,1,0:T(1,128)S(1)} all-gather(f32[1,1,128]{2,1,0:T(1,128)S(1)} %fusion.106), channel_id=2, replica_groups=mesh['year'=8,'region'=4] {'year'}, dimensions={0}, use_global_device_ids=true | all-gather | bytes 4608 | tf_op jit(solution)/shard_map/all_gather | solution.py:98
  120.5 17.1 %psum.7 = f32[8,128]{1,0:T(8,128)S(1)} all-reduce(f32[8,128]{1,0:T(8,128)S(1)} %fusion.16), channel_id=1, replica_groups=mesh['year'=8,'region'=4] {'year'}, use_global_device_ids=true, to_apply=%region_4.5 | all-reduce | flops 1024 | bytes 8192 | tf_op jit(solution)/shard_map/psum | solution.py:100
  137.7 0.5 multiply_subtract_fusion
  (14 shorter events, 0.2 us)
Async XLA Ops:
  7.2 91.8 %all-reduce.3.cloned.1.call-start = ((), (), s32[]{:S(2)}) async-start(), calls=%async_computation | async-start | bytes 2097152
  8.7 3.8 %collective-permute-start.1 = (bf16[23,1]{1,0:T(8,128)(2,1)S(1)}, bf16[23,1]{1,0:T(8,128)(2,1)S(1)}, u32[]{:S(2)}, u32[]{:S(2)}) collective-permute-start(bf16[23,1]{1,0:T(8,128)(2,1)S(1)} %get-tuple-element.9), channel_id=1, source_target_pairs={{1,0},{2,1},{3,2},{0,3},{5,4},{6,5},{7,6},{4,7},{9,8},{10,9},{11,1... | collective-permute-start | bytes 146 | tf_op jit(solution)/shard_map/ppermute | solution.py:25
  11.1 3.1 %collective-permute-start = (bf16[23,1]{1,0:T(8,128)(2,1)S(1)}, bf16[23,1]{1,0:T(8,128)(2,1)S(1)}, u32[]{:S(2)}, u32[]{:S(2)}) collective-permute-start(bf16[23,1]{1,0:T(8,128)(2,1)S(1)} %get-tuple-element.8), channel_id=1, source_target_pairs={{0,1},{1,2},{2,3},{3,0},{4,5},{5,6},{6,7},{7,4},{8,9},{9,10},{10,1... | collective-permute-start | bytes 146 | tf_op jit(solution)/shard_map/ppermute | solution.py:24
  18.6 1.9 %copy-start = (u32[32]{0:T(128)S(1)}, u32[32]{0:T(128)}, u32[]{:S(2)}) copy-start(u32[32]{0:T(128)} %constant.71) | copy-start | bytes 388
Sparse Core Ops, SparseCore 0:
  20.6 78.3 all-reduce.2
where the time goes:
time: 145 us
  waiting for transfers between devices  80.9 us (56%)
  blocking collectives  36.2 us (25%)
  between operations  14.1 us (10%)
  local copies, waits for them, and re-layouts  5.36 us (4%)
  other arithmetic  4.19 us (3%)
  starting transfers between devices  2.45 us (2%)
  matrix products  1.83 us (1%)
    unnamed x2, waiting for transfers between devices  78 us
    all_gather x1, blocking collectives, shards(): coarse_all = lax.all_gather(coarse, 'year', axis=0, tiled=True)  19.1 us
    psum x1, blocking collectives, shards(): cdf_whole = lax.psum(partial_cdf, 'year')  17.1 us
    unnamed x8, local copies, waits for them, and re-layouts  4.8 us
  transfers between devices with their start and end apart: 3, of which 3 were waited for; matrix products, arithmetic and copies ran while one was open for 0% of the time, Pallas kernels for 0%

commit v1 on v0

v1 whole, which is shorter than its diff:
```python
import jax
import jax.numpy as jnp
from jax import lax
from jax.sharding import PartitionSpec as P

WIN = 15
BINS = 256


VALUE_RANGE = 12.8
QUANT_LEVEL = 0.9
SHARPNESS = 32.0
KERNEL_SCALE = 0.25
STEP_SIZE = 2.0


def extended_2(array, sides, width):
    for axis, dim in sides:
        devices, length = (lax.axis_size(axis), array.shape[dim])
        up = [(i, (i + 1) % devices) for i in range(devices)]
        down = [(j, i) for i, j in up]
        last = lax.slice_in_dim(array, length - width, length, axis=dim)
        leading = lax.slice_in_dim(array, 0, width, axis=dim)
        before = lax.ppermute(last, axis, up)
        after = lax.ppermute(leading, axis, down)
        array = jnp.concatenate([before, array, after], axis=dim)
    return array


def smooth_field(extended, flags):
    center = extended[..., 1:-1]
    same_west = 1.0 - jnp.abs(flags[1:-1] - flags[:-2])
    same_east = 1.0 - jnp.abs(flags[1:-1] - flags[2:])
    mixed = center + same_west * extended[..., :-2] + same_east * extended[..., 2:]
    return (mixed / (1.0 + same_west + same_east)).astype(jnp.bfloat16)


def gather_years(block, axis):
    devices = lax.axis_size(axis)
    pieces = [block]
    for shift in range(1, devices):
        pairs = [(i, (i + shift) % devices) for i in range(devices)]
        pieces.append(lax.ppermute(block, axis, pairs))
    return jnp.stack(pieces, axis=0)


def coarse_from_samples(samples, count_all, bin_count):
    width = VALUE_RANGE / bin_count
    scaled = jnp.clip((samples + 0.5 * VALUE_RANGE) / width, 0.0, bin_count - 1.0)
    upper = lax.broadcasted_iota(jnp.float32, (bin_count, 1), 0) + 1.0
    cumulative = jnp.sum(jnp.clip(upper[None] - scaled[:, None, :], 0.0, 1.0), axis=0)
    ranks = jnp.clip(0.5 + SHARPNESS * (QUANT_LEVEL - cumulative / count_all), 0.0, 1.0)
    return -0.5 * VALUE_RANGE + width * jnp.sum(ranks, axis=0)


def shards(daily_temps, land_mask):
    days_in = daily_temps.shape[1]
    year_count = lax.axis_size("year")
    cal_days = days_in - WIN + 1
    cal_own = cal_days // year_count
    count_all = float(year_count * WIN)
    flag_row = land_mask.astype(jnp.bfloat16)[None, :]
    stacked = jnp.concatenate([daily_temps[0], flag_row], axis=0)
    extended = extended_2(stacked, (("region", 1),), 1)
    smoothed = smooth_field(
        extended[:days_in].astype(jnp.float32), extended[days_in].astype(jnp.float32)
    )
    every_year = gather_years(smoothed, "year").astype(jnp.float32)
    first_day = lax.axis_index("year") * cal_own
    coarse_rows = []
    refined_rows = []
    for j in range(cal_own):
        window = lax.dynamic_slice_in_dim(every_year, first_day + j, WIN, axis=1)
        samples = window.reshape(-1, window.shape[-1])
        coarse = coarse_from_samples(samples, count_all, BINS)
        cdf = jnp.sum(jax.nn.sigmoid((coarse[None] - samples) / KERNEL_SCALE), axis=0)
        refined = coarse - STEP_SIZE * (cdf / count_all - QUANT_LEVEL)
        coarse_rows.append(coarse)
        refined_rows.append(refined)
    return (jnp.stack(coarse_rows, axis=0), jnp.stack(refined_rows, axis=0))


def solution(mesh):
    return jax.shard_map(
        shards,
        mesh=mesh,
        in_specs=(P("year", None, "region"), P("region")),
        out_specs=(P("year", "region"), P("year", "region")),
        check_vma=False,
    )
```

time: 145 us -> 28.2 us (0.19)
  waiting for transfers between devices: 80.9 us -> 7.36 us
  blocking collectives: 36.2 us -> 0 us
  between operations: 14.1 us -> 0.68 us
  starting transfers between devices: 2.45 us -> 14.2 us
  local copies, waits for them, and re-layouts: 5.36 us -> 0.06 us
  matrix products: 1.83 us -> 0 us
    unnamed x2 -> x0, waiting for transfers between devices: 78 us -> none
    all_gather x1 -> x0, blocking collectives: 19.1 us -> none  [shards(): coarse_all = lax.all_gather(coarse, 'year', axis=0, tiled=True)]
    psum x1 -> x0, blocking collectives: 17.1 us -> none  [shards(): cdf_whole = lax.psum(partial_cdf, 'year')]
    ppermute x0 -> x7, starting transfers between devices: none -> 11.7 us  [gather_years(): pieces.append(lax.ppermute(block, axis, pairs))]
    ppermute x0 -> x7, waiting for transfers between devices: none -> 6.01 us  [gather_years(): pieces.append(lax.ppermute(block, axis, pairs))]
    unnamed x8 -> x6, local copies, waits for them, and re-layouts: 4.8 us -> 0.05 us
    dot_general x1 -> x0, matrix products: 1.83 us -> none  [shards(): jnp.dot(day_band(cal_own * lax.axis_size('year'), days_in), weights, pref...]
    reduce_sum x1 -> x3, other arithmetic: 0.16 us -> 1.78 us  [the longest x1 1.66 us: coarse_from_samples(): jnp.sum(jnp.clip(upper[None] - scaled[:, None, :], 0.0, 1.0), axis=0)]
  transfers between devices with their start and end apart: 3 -> 9, of which waited for: 3 -> 4; matrix products, arithmetic and copies ran while one was open for 0% -> 0% of each run, Pallas kernels for 0% -> 0%
where the time goes in v1:
time: 28.2 us; the launch traced here: 27.9 us
  starting transfers between devices  14.2 us (50%)
  waiting for transfers between devices  7.36 us (26%)
  other arithmetic  5.61 us (20%)
  between operations  0.68 us (2%)
    ppermute x7, starting transfers between devices, gather_years(): pieces.append(lax.ppermute(block, axis, pairs))  11.7 us
    ppermute x7, waiting for transfers between devices, gather_years(): pieces.append(lax.ppermute(block, axis, pairs))  6.01 us
    ppermute x1, starting transfers between devices, extended_2(): after = lax.ppermute(leading, axis, down)  2.01 us
    reduce_sum x1, other arithmetic, coarse_from_samples(): jnp.sum(jnp.clip(upper[None] - scaled[:, None, :], 0.0, 1.0), axis=0)  1.66 us
    ppermute x1, waiting for transfers between devices, extended_2(): before = lax.ppermute(last, axis, up)  1.26 us
    concatenate x1, other arithmetic, shards(): stacked = jnp.concatenate([daily_temps[0], flag_row], axis=0)  0.84 us
    concatenate x1, other arithmetic, extended_2(): array = jnp.concatenate([before, array, after], axis=dim)  0.78 us
    convert_element_type x1, other arithmetic, shards(): extended[days_in].astype(jnp.float32)  0.75 us
  transfers between devices with their start and end apart: 9, of which 4 were waited for; matrix products, arithmetic and copies ran while one was open for 0% of the time, Pallas kernels for 0%

profile of v1, /device:TPU:0, one launch (start us, length us, event | category | flops | bytes accessed | tf_op | source)
XLA Modules:
  0.0 27.9 jit_solution(13501689752090335430)
XLA Ops:
  0.6 0.7 %convert_bitcast_fusion = bf16[1,128]{1,0:T(2,128)(2,1)S(1)} fusion(s32[128]{0:T(128)} %param.3), kind=kLoop, calls=%fused_computation.41 | loop fusion | flops 128 | bytes 768 | tf_op jit(solution)/shard_map/broadcast_in_dim | solution.py:62
  1.3 0.8 %slice_maximum_fusion = (bf16[23,1]{1,0:T(8,128)(2,1)S(1)}, bf16[23,1]{1,0:T(8,128)(2,1)S(1)}) fusion(bf16[1,128]{1,0:T(2,128)(2,1)S(1)} %convert_bitcast_fusion, bf16[22,128]{1,0:T(8,128)(2,1)} %bitcast.31), kind=kLoop, calls=%fused_computation.29 | loop fusion | flops 184 | bytes 5980 | tf_op jit(solution)/shard_map/concatenate | solution.py:63
  2.1 0.5 %collective-permute-start = (bf16[23,1]{1,0:T(8,128)(2,1)S(1)}, bf16[23,1]{1,0:T(8,128)(2,1)S(1)}, u32[]{:S(2)}, u32[]{:S(2)}) collective-permute-start(bf16[23,1]{1,0:T(8,128)(2,1)S(1)} %get-tuple-element.8), channel_id=1, source_target_pairs={{0,1},{1,2},{2,3},{3,0},{4,5},{5,6},{6,7},{7,4},{8,9},{9,10},{10,1... | collective-permute-start | bytes 146 | tf_op jit(solution)/shard_map/ppermute | solution.py:24
  2.6 2.0 %collective-permute-start.1 = (bf16[23,1]{1,0:T(8,128)(2,1)S(1)}, bf16[23,1]{1,0:T(8,128)(2,1)S(1)}, u32[]{:S(2)}, u32[]{:S(2)}) collective-permute-start(bf16[23,1]{1,0:T(8,128)(2,1)S(1)} %get-tuple-element.9), channel_id=1, source_target_pairs={{1,0},{2,1},{3,2},{0,3},{5,4},{6,5},{7,6},{4,7},{9,8},{10,9},{11,1... | collective-permute-start | bytes 146 | tf_op jit(solution)/shard_map/ppermute | solution.py:25
  4.6 1.3 %collective-permute-done = bf16[23,1]{1,0:T(8,128)(2,1)S(1)} collective-permute-done((bf16[23,1]{1,0:T(8,128)(2,1)S(1)}, bf16[23,1]{1,0:T(8,128)(2,1)S(1)}, u32[]{:S(2)}, u32[]{:S(2)}) %collective-permute-start) | collective-permute-done | bytes 78 | tf_op jit(solution)/shard_map/ppermute | solution.py:24
  5.9 0.1 collective-permute-done.1
  5.9 0.8 %maximum_convert_fusion = f32[1,130]{1,0:T(1,128)S(1)} fusion(bf16[23,1]{1,0:T(8,128)(2,1)S(1)} %collective-permute-done.1, bf16[23,1]{1,0:T(8,128)(2,1)S(1)} %collective-permute-done, bf16[1,128]{1,0:T(2,128)(2,1)S(1)} %convert_bitcast_fusion, bf16[22,128]{1,0:T(8,128)(2,1)} %bitcast.32), kind=kLoop, calls=%fused_computation.30 | loop fusion | flops 1040 | bytes 6500 | tf_op jit(solution)/shard_map/convert_element_type | solution.py:66
  6.7 0.1 subtract_bitcast_fusion.1
  6.8 0.1 bitcast_add_fusion
  6.9 0.8 %pad_maximum_fusion = bf16[23,130]{1,0:T(8,128)(2,1)S(1)} fusion(bf16[23,1]{1,0:T(8,128)(2,1)S(1)} %collective-permute-done.1, bf16[1,128]{1,0:T(2,128)(2,1)S(1)} %convert_bitcast_fusion, bf16[22,128]{1,0:T(8,128)(2,1)} %bitcast.33, bf16[23,1]{1,0:T(8,128)(2,1)S(1)} %collective-permute-done), kind=kLoop, calls=%fused_computation.26 | loop fusion | flops 23920 | bytes 11960 | tf_op jit(solution)/shard_map/concatenate | solution.py:26
  7.6 0.1 constant_dynamic-update-slice_fusion.7
  7.7 2.2 %collective-permute-start.2 = (bf16[22,128]{1,0:T(8,128)(2,1)S(1)}, bf16[22,128]{1,0:T(8,128)(2,1)S(1)}, u32[]{:S(2)}, u32[]{:S(2)}) collective-permute-start(bf16[22,128]{1,0:T(8,128)(2,1)S(1)} %get-tuple-element.5), channel_id=1, source_target_pairs={{0,4},{4,8},{8,12},{12,16},{16,20},{20,24},{24,28},{28,0},{1,5},{5... | collective-permute-start | bytes 16904 | tf_op jit(solution)/shard_map/ppermute | solution.py:43
  10.0 3.6 %collective-permute-start.7 = (bf16[22,128]{1,0:T(8,128)(2,1)S(1)}, bf16[22,128]{1,0:T(8,128)(2,1)S(1)}, u32[]{:S(2)}, u32[]{:S(2)}) collective-permute-start(bf16[22,128]{1,0:T(8,128)(2,1)S(1)} %get-tuple-element.5), channel_id=1, source_target_pairs={{0,24},{4,28},{8,0},{12,4},{16,8},{20,12},{24,16},{28,20},{1,25},{... | collective-permute-start | bytes 16904 | tf_op jit(solution)/shard_map/ppermute | solution.py:43
  13.6 0.4 %collective-permute-start.6 = (bf16[22,128]{1,0:T(8,128)(2,1)S(1)}, bf16[22,128]{1,0:T(8,128)(2,1)S(1)}, u32[]{:S(2)}, u32[]{:S(2)}) collective-permute-start(bf16[22,128]{1,0:T(8,128)(2,1)S(1)} %get-tuple-element.5), channel_id=1, source_target_pairs={{0,20},{4,24},{8,28},{12,0},{16,4},{20,8},{24,12},{28,16},{1,21},{... | collective-permute-start | bytes 16904 | tf_op jit(solution)/shard_map/ppermute | solution.py:43
  14.0 2.0 %collective-permute-start.5 = (bf16[22,128]{1,0:T(8,128)(2,1)S(1)}, bf16[22,128]{1,0:T(8,128)(2,1)S(1)}, u32[]{:S(2)}, u32[]{:S(2)}) collective-permute-start(bf16[22,128]{1,0:T(8,128)(2,1)S(1)} %get-tuple-element.5), channel_id=1, source_target_pairs={{0,16},{4,20},{8,24},{12,28},{16,0},{20,4},{24,8},{28,12},{1,17},{... | collective-permute-start | bytes 16904 | tf_op jit(solution)/shard_map/ppermute | solution.py:43
  16.0 0.5 %collective-permute-start.4 = (bf16[22,128]{1,0:T(8,128)(2,1)S(1)}, bf16[22,128]{1,0:T(8,128)(2,1)S(1)}, u32[]{:S(2)}, u32[]{:S(2)}) collective-permute-start(bf16[22,128]{1,0:T(8,128)(2,1)S(1)} %get-tuple-element.5), channel_id=1, source_target_pairs={{0,12},{4,16},{8,20},{12,24},{16,28},{20,0},{24,4},{28,8},{1,13},{... | collective-permute-start | bytes 16904 | tf_op jit(solution)/shard_map/ppermute | solution.py:43
  16.5 1.9 %collective-permute-start.3 = (bf16[22,128]{1,0:T(8,128)(2,1)S(1)}, bf16[22,128]{1,0:T(8,128)(2,1)S(1)}, u32[]{:S(2)}, u32[]{:S(2)}) collective-permute-start(bf16[22,128]{1,0:T(8,128)(2,1)S(1)} %get-tuple-element.5), channel_id=1, source_target_pairs={{0,8},{4,12},{8,16},{12,20},{16,24},{20,28},{24,0},{28,4},{1,9},{5... | collective-permute-start | bytes 16904 | tf_op jit(solution)/shard_map/ppermute | solution.py:43
  18.4 3.5 %collective-permute-done.3 = bf16[22,128]{1,0:T(8,128)(2,1)S(1)} collective-permute-done((bf16[22,128]{1,0:T(8,128)(2,1)S(1)}, bf16[22,128]{1,0:T(8,128)(2,1)S(1)}, u32[]{:S(2)}, u32[]{:S(2)}) %collective-permute-start.3) | collective-permute-done | bytes 5664 | tf_op jit(solution)/shard_map/ppermute | solution.py:43
  21.9 1.1 %collective-permute-start.8 = (bf16[22,128]{1,0:T(8,128)(2,1)S(1)}, bf16[22,128]{1,0:T(8,128)(2,1)S(1)}, u32[]{:S(2)}, u32[]{:S(2)}) collective-permute-start(bf16[22,128]{1,0:T(8,128)(2,1)S(1)} %get-tuple-element.5), channel_id=1, source_target_pairs={{0,28},{4,0},{8,4},{12,8},{16,12},{20,16},{24,20},{28,24},{1,29},{... | collective-permute-start | bytes 16904 | tf_op jit(solution)/shard_map/ppermute | solution.py:43
  23.1 2.5 %collective-permute-done.8 = bf16[22,128]{1,0:T(8,128)(2,1)S(1)} collective-permute-done((bf16[22,128]{1,0:T(8,128)(2,1)S(1)}, bf16[22,128]{1,0:T(8,128)(2,1)S(1)}, u32[]{:S(2)}, u32[]{:S(2)}) %collective-permute-start.8) | collective-permute-done | bytes 5664 | tf_op jit(solution)/shard_map/ppermute | solution.py:43
  25.6 1.7 %clamp_reduce_fusion = f32[256,128]{1,0:T(8,128)S(1)} fusion(f32[120,128]{1,0:T(8,128)S(1)} %min.28, f32[256]{0:T(256)S(1)} %iota_add_fusion), kind=kLoop, calls=%fused_computation | loop fusion | flops 11763712 | bytes 193536 | tf_op jit(solution)/shard_map/reduce_sum | solution.py:51
  27.3 0.1 clamp_reduce_fusion.1
  27.3 0.1 fusion.7
  27.4 0.5 %bitcast_subtract_fusion = (f32[1,128]{1,0:T(1,128)}, f32[1,128]{1,0:T(1,128)}) fusion(f32[128]{0:T(128)S(1)} %fusion.7, f32[128]{0:T(128)S(1)} %clamp_reduce_fusion.1), kind=kLoop, calls=%fused_computation.36 | loop fusion | flops 768 | bytes 2048 | tf_op jit(solution)/shard_map/sub | solution.py:77
  (17 shorter events, 0.1 us)
Async XLA Ops:
  2.1 3.7 %collective-permute-start = (bf16[23,1]{1,0:T(8,128)(2,1)S(1)}, bf16[23,1]{1,0:T(8,128)(2,1)S(1)}, u32[]{:S(2)}, u32[]{:S(2)}) collective-permute-start(bf16[23,1]{1,0:T(8,128)(2,1)S(1)} %get-tuple-element.8), channel_id=1, source_target_pairs={{0,1},{1,2},{2,3},{3,0},{4,5},{5,6},{6,7},{7,4},{8,9},{9,10},{10,1... | collective-permute-start | bytes 146 | tf_op jit(solution)/shard_map/ppermute | solution.py:24
  2.6 3.4 %collective-permute-start.1 = (bf16[23,1]{1,0:T(8,128)(2,1)S(1)}, bf16[23,1]{1,0:T(8,128)(2,1)S(1)}, u32[]{:S(2)}, u32[]{:S(2)}) collective-permute-start(bf16[23,1]{1,0:T(8,128)(2,1)S(1)} %get-tuple-element.9), channel_id=1, source_target_pairs={{1,0},{2,1},{3,2},{0,3},{5,4},{6,5},{7,6},{4,7},{9,8},{10,9},{11,1... | collective-permute-start | bytes 146 | tf_op jit(solution)/shard_map/ppermute | solution.py:25
  7.7 8.8 %collective-permute-start.2 = (bf16[22,128]{1,0:T(8,128)(2,1)S(1)}, bf16[22,128]{1,0:T(8,128)(2,1)S(1)}, u32[]{:S(2)}, u32[]{:S(2)}) collective-permute-start(bf16[22,128]{1,0:T(8,128)(2,1)S(1)} %get-tuple-element.5), channel_id=1, source_target_pairs={{0,4},{4,8},{8,12},{12,16},{16,20},{20,24},{24,28},{28,0},{1,5},{5... | collective-permute-start | bytes 16904 | tf_op jit(solution)/shard_map/ppermute | solution.py:43
  10.0 13.1 %collective-permute-start.7 = (bf16[22,128]{1,0:T(8,128)(2,1)S(1)}, bf16[22,128]{1,0:T(8,128)(2,1)S(1)}, u32[]{:S(2)}, u32[]{:S(2)}) collective-permute-start(bf16[22,128]{1,0:T(8,128)(2,1)S(1)} %get-tuple-element.5), channel_id=1, source_target_pairs={{0,24},{4,28},{8,0},{12,4},{16,8},{20,12},{24,16},{28,20},{1,25},{... | collective-permute-start | bytes 16904 | tf_op jit(solution)/shard_map/ppermute | solution.py:43
  13.6 9.5 %collective-permute-start.6 = (bf16[22,128]{1,0:T(8,128)(2,1)S(1)}, bf16[22,128]{1,0:T(8,128)(2,1)S(1)}, u32[]{:S(2)}, u32[]{:S(2)}) collective-permute-start(bf16[22,128]{1,0:T(8,128)(2,1)S(1)} %get-tuple-element.5), channel_id=1, source_target_pairs={{0,20},{4,24},{8,28},{12,0},{16,4},{20,8},{24,12},{28,16},{1,21},{... | collective-permute-start | bytes 16904 | tf_op jit(solution)/shard_map/ppermute | solution.py:43
  14.0 9.0 %collective-permute-start.5 = (bf16[22,128]{1,0:T(8,128)(2,1)S(1)}, bf16[22,128]{1,0:T(8,128)(2,1)S(1)}, u32[]{:S(2)}, u32[]{:S(2)}) collective-permute-start(bf16[22,128]{1,0:T(8,128)(2,1)S(1)} %get-tuple-element.5), channel_id=1, source_target_pairs={{0,16},{4,20},{8,24},{12,28},{16,0},{20,4},{24,8},{28,12},{1,17},{... | collective-permute-start | bytes 16904 | tf_op jit(solution)/shard_map/ppermute | solution.py:43
  16.0 7.0 %collective-permute-start.4 = (bf16[22,128]{1,0:T(8,128)(2,1)S(1)}, bf16[22,128]{1,0:T(8,128)(2,1)S(1)}, u32[]{:S(2)}, u32[]{:S(2)}) collective-permute-start(bf16[22,128]{1,0:T(8,128)(2,1)S(1)} %get-tuple-element.5), channel_id=1, source_target_pairs={{0,12},{4,16},{8,20},{12,24},{16,28},{20,0},{24,4},{28,8},{1,13},{... | collective-permute-start | bytes 16904 | tf_op jit(solution)/shard_map/ppermute | solution.py:43
  16.5 5.4 %collective-permute-start.3 = (bf16[22,128]{1,0:T(8,128)(2,1)S(1)}, bf16[22,128]{1,0:T(8,128)(2,1)S(1)}, u32[]{:S(2)}, u32[]{:S(2)}) collective-permute-start(bf16[22,128]{1,0:T(8,128)(2,1)S(1)} %get-tuple-element.5), channel_id=1, source_target_pairs={{0,8},{4,12},{8,16},{12,20},{16,24},{20,28},{24,0},{28,4},{1,9},{5... | collective-permute-start | bytes 16904 | tf_op jit(solution)/shard_map/ppermute | solution.py:43
  21.9 3.6 %collective-permute-start.8 = (bf16[22,128]{1,0:T(8,128)(2,1)S(1)}, bf16[22,128]{1,0:T(8,128)(2,1)S(1)}, u32[]{:S(2)}, u32[]{:S(2)}) collective-permute-start(bf16[22,128]{1,0:T(8,128)(2,1)S(1)} %get-tuple-element.5), channel_id=1, source_target_pairs={{0,28},{4,0},{8,4},{12,8},{16,12},{20,16},{24,20},{28,24},{1,29},{... | collective-permute-start | bytes 16904 | tf_op jit(solution)/shard_map/ppermute | solution.py:43

commit v2 on v1

--- a/solution.py
+++ b/solution.py
@@ -37,11 +37,8 @@
 
 def gather_years(block, axis):
     devices = lax.axis_size(axis)
-    pieces = [block]
-    for shift in range(1, devices):
-        pairs = [(i, (i + shift) % devices) for i in range(devices)]
-        pieces.append(lax.ppermute(block, axis, pairs))
-    return jnp.stack(pieces, axis=0)
+    tiled = jnp.broadcast_to(block[None], (devices,) + block.shape)
+    return lax.all_to_all(tiled, axis, 0, 0, tiled=True)
 
 
 def coarse_from_samples(samples, count_all, bin_count):

time: 28.2 us -> 24.4 us (0.87)
  starting transfers between devices: 14.2 us -> 9 us
  waiting for transfers between devices: 7.36 us -> 8.13 us
  local copies, waits for them, and re-layouts: 0.06 us -> 0.64 us
    ppermute x7 -> x0, starting transfers between devices: 11.7 us -> none  [gather_years(): pieces.append(lax.ppermute(block, axis, pairs))]
    all_to_all x0 -> x1, waiting for transfers between devices: none -> 6.79 us  [gather_years(): return lax.all_to_all(tiled, axis, 0, 0, tiled=True)]
    all_to_all x0 -> x1, starting transfers between devices: none -> 6.54 us  [gather_years(): return lax.all_to_all(tiled, axis, 0, 0, tiled=True)]
    ppermute x7 -> x0, waiting for transfers between devices: 6.01 us -> none  [gather_years(): pieces.append(lax.ppermute(block, axis, pairs))]
    broadcast_in_dim x0 -> x1, local copies, waits for them, and re-layouts: none -> 0.63 us  [gather_years(): tiled = jnp.broadcast_to(block[None], (devices,) + block.shape)]
  transfers between devices with their start and end apart: 9 -> 3, of which waited for: 4 -> 3; matrix products, arithmetic and copies ran while one was open for 0% -> 0% of each run, Pallas kernels for 0% -> 0%
where the time goes in v2:
time: 24.4 us; the launch traced here: 24 us
  starting transfers between devices  9 us (37%)
  waiting for transfers between devices  8.13 us (33%)
  other arithmetic  5.61 us (23%)
  between operations  0.65 us (3%)
  local copies, waits for them, and re-layouts  0.64 us (3%)
    all_to_all x1, waiting for transfers between devices, gather_years(): return lax.all_to_all(tiled, axis, 0, 0, tiled=True)  6.79 us
    all_to_all x1, starting transfers between devices, gather_years(): return lax.all_to_all(tiled, axis, 0, 0, tiled=True)  6.54 us
    ppermute x1, starting transfers between devices, extended_2(): after = lax.ppermute(leading, axis, down)  2.01 us
    reduce_sum x1, other arithmetic, coarse_from_samples(): jnp.sum(jnp.clip(upper[None] - scaled[:, None, :], 0.0, 1.0), axis=0)  1.66 us
    ppermute x1, waiting for transfers between devices, extended_2(): before = lax.ppermute(last, axis, up)  1.26 us
    concatenate x1, other arithmetic, shards(): stacked = jnp.concatenate([daily_temps[0], flag_row], axis=0)  0.84 us
    concatenate x1, other arithmetic, extended_2(): array = jnp.concatenate([before, array, after], axis=dim)  0.78 us
    convert_element_type x1, other arithmetic, shards(): extended[days_in].astype(jnp.float32)  0.75 us
  transfers between devices with their start and end apart: 3, of which 3 were waited for; matrix products, arithmetic and copies ran while one was open for 0% of the time, Pallas kernels for 0%

profile of v2, /device:TPU:0, one launch (start us, length us, event | category | flops | bytes accessed | tf_op | source)
XLA Modules:
  0.0 24.0 jit_solution(5270585627944360812)
XLA Ops:
  0.6 0.7 %convert_bitcast_fusion = bf16[1,128]{1,0:T(2,128)(2,1)S(1)} fusion(s32[128]{0:T(128)} %param.3), kind=kLoop, calls=%fused_computation.33 | loop fusion | flops 128 | bytes 768 | tf_op jit(solution)/shard_map/broadcast_in_dim | solution.py:59
  1.3 0.8 %slice_maximum_fusion = (bf16[23,1]{1,0:T(8,128)(2,1)S(1)}, bf16[23,1]{1,0:T(8,128)(2,1)S(1)}) fusion(bf16[1,128]{1,0:T(2,128)(2,1)S(1)} %convert_bitcast_fusion, bf16[22,128]{1,0:T(8,128)(2,1)} %bitcast.15), kind=kLoop, calls=%fused_computation.21 | loop fusion | flops 184 | bytes 5980 | tf_op jit(solution)/shard_map/concatenate | solution.py:60
  2.1 0.5 %collective-permute-start = (bf16[23,1]{1,0:T(8,128)(2,1)S(1)}, bf16[23,1]{1,0:T(8,128)(2,1)S(1)}, u32[]{:S(2)}, u32[]{:S(2)}) collective-permute-start(bf16[23,1]{1,0:T(8,128)(2,1)S(1)} %get-tuple-element.6), channel_id=1, source_target_pairs={{0,1},{1,2},{2,3},{3,0},{4,5},{5,6},{6,7},{7,4},{8,9},{9,10},{10,1... | collective-permute-start | bytes 146 | tf_op jit(solution)/shard_map/ppermute | solution.py:24
  2.6 2.0 %collective-permute-start.1 = (bf16[23,1]{1,0:T(8,128)(2,1)S(1)}, bf16[23,1]{1,0:T(8,128)(2,1)S(1)}, u32[]{:S(2)}, u32[]{:S(2)}) collective-permute-start(bf16[23,1]{1,0:T(8,128)(2,1)S(1)} %get-tuple-element.7), channel_id=1, source_target_pairs={{1,0},{2,1},{3,2},{0,3},{5,4},{6,5},{7,6},{4,7},{9,8},{10,9},{11,1... | collective-permute-start | bytes 146 | tf_op jit(solution)/shard_map/ppermute | solution.py:25
  4.6 1.3 %collective-permute-done = bf16[23,1]{1,0:T(8,128)(2,1)S(1)} collective-permute-done((bf16[23,1]{1,0:T(8,128)(2,1)S(1)}, bf16[23,1]{1,0:T(8,128)(2,1)S(1)}, u32[]{:S(2)}, u32[]{:S(2)}) %collective-permute-start) | collective-permute-done | bytes 78 | tf_op jit(solution)/shard_map/ppermute | solution.py:24
  5.9 0.1 collective-permute-done.1
  5.9 0.8 %maximum_convert_fusion = f32[1,130]{1,0:T(1,128)S(1)} fusion(bf16[23,1]{1,0:T(8,128)(2,1)S(1)} %collective-permute-done.1, bf16[23,1]{1,0:T(8,128)(2,1)S(1)} %collective-permute-done, bf16[1,128]{1,0:T(2,128)(2,1)S(1)} %convert_bitcast_fusion, bf16[22,128]{1,0:T(8,128)(2,1)} %bitcast.16), kind=kLoop, calls=%fused_computation.22 | loop fusion | flops 1040 | bytes 6500 | tf_op jit(solution)/shard_map/convert_element_type | solution.py:63
  6.7 0.1 subtract_bitcast_fusion.1
  6.8 0.1 bitcast_add_fusion
  6.9 0.8 %pad_maximum_fusion = bf16[23,130]{1,0:T(8,128)(2,1)S(1)} fusion(bf16[23,1]{1,0:T(8,128)(2,1)S(1)} %collective-permute-done.1, bf16[1,128]{1,0:T(2,128)(2,1)S(1)} %convert_bitcast_fusion, bf16[22,128]{1,0:T(8,128)(2,1)} %bitcast.17, bf16[23,1]{1,0:T(8,128)(2,1)S(1)} %collective-permute-done), kind=kLoop, calls=%fused_computation.18 | loop fusion | flops 23920 | bytes 11960 | tf_op jit(solution)/shard_map/concatenate | solution.py:26
  7.6 0.1 fusion.11
  7.7 0.6 %broadcast_in_dim.5 = bf16[8,22,128]{2,1,0:T(8,128)(2,1)} broadcast(bf16[22,128]{1,0:T(8,128)(2,1)S(1)} %fusion.11), dimensions={1,2} | broadcast | bytes 50688 | tf_op jit(solution)/shard_map/broadcast_in_dim | solution.py:40
  8.4 6.5 %all-to-all-start = ((bf16[8,22,128]{2,1,0:T(8,128)(2,1)}), bf16[8,22,128]{2,1,0:T(8,128)(2,1)S(1)}, u32[]{:S(2)}, u32[]{:S(2)}) async-start(bf16[8,22,128]{2,1,0:T(8,128)(2,1)} %broadcast_in_dim.5), calls=%async_computation | async-start | bytes 98304 | tf_op jit(solution)/shard_map/all_to_all | solution.py:41
  14.9 6.8 %all-to-all-done = bf16[8,22,128]{2,1,0:T(8,128)(2,1)S(1)} async-done(((bf16[8,22,128]{2,1,0:T(8,128)(2,1)}), bf16[8,22,128]{2,1,0:T(8,128)(2,1)S(1)}, u32[]{:S(2)}, u32[]{:S(2)}) %all-to-all-start) | async-done | bytes 45088 | tf_op jit(solution)/shard_map/all_to_all | solution.py:41
  21.7 1.7 %clamp_reduce_fusion = f32[256,128]{1,0:T(8,128)S(1)} fusion(f32[120,128]{1,0:T(8,128)S(1)} %min.28, f32[256]{0:T(256)S(1)} %iota_add_fusion), kind=kLoop, calls=%fused_computation | loop fusion | flops 11763712 | bytes 193536 | tf_op jit(solution)/shard_map/reduce_sum | solution.py:48
  23.4 0.1 clamp_reduce_fusion.1
  23.5 0.1 fusion.7
  23.5 0.5 %bitcast_subtract_fusion = (f32[1,128]{1,0:T(1,128)}, f32[1,128]{1,0:T(1,128)}) fusion(f32[128]{0:T(128)S(1)} %fusion.7, f32[128]{0:T(128)S(1)} %clamp_reduce_fusion.1), kind=kLoop, calls=%fused_computation.28 | loop fusion | flops 768 | bytes 2048 | tf_op jit(solution)/shard_map/sub | solution.py:74
  (5 shorter events, 0.0 us)
Async XLA Ops:
  2.1 3.7 %collective-permute-start = (bf16[23,1]{1,0:T(8,128)(2,1)S(1)}, bf16[23,1]{1,0:T(8,128)(2,1)S(1)}, u32[]{:S(2)}, u32[]{:S(2)}) collective-permute-start(bf16[23,1]{1,0:T(8,128)(2,1)S(1)} %get-tuple-element.6), channel_id=1, source_target_pairs={{0,1},{1,2},{2,3},{3,0},{4,5},{5,6},{6,7},{7,4},{8,9},{9,10},{10,1... | collective-permute-start | bytes 146 | tf_op jit(solution)/shard_map/ppermute | solution.py:24
  2.6 3.4 %collective-permute-start.1 = (bf16[23,1]{1,0:T(8,128)(2,1)S(1)}, bf16[23,1]{1,0:T(8,128)(2,1)S(1)}, u32[]{:S(2)}, u32[]{:S(2)}) collective-permute-start(bf16[23,1]{1,0:T(8,128)(2,1)S(1)} %get-tuple-element.7), channel_id=1, source_target_pairs={{1,0},{2,1},{3,2},{0,3},{5,4},{6,5},{7,6},{4,7},{9,8},{10,9},{11,1... | collective-permute-start | bytes 146 | tf_op jit(solution)/shard_map/ppermute | solution.py:25
  8.4 13.3 %all-to-all-start = ((bf16[8,22,128]{2,1,0:T(8,128)(2,1)}), bf16[8,22,128]{2,1,0:T(8,128)(2,1)S(1)}, u32[]{:S(2)}, u32[]{:S(2)}) async-start(bf16[8,22,128]{2,1,0:T(8,128)(2,1)} %broadcast_in_dim.5), calls=%async_computation | async-start | bytes 98304 | tf_op jit(solution)/shard_map/all_to_all | solution.py:41

commit v3 on v2

--- a/solution.py
+++ b/solution.py
@@ -37,8 +37,14 @@
 
 def gather_years(block, axis):
     devices = lax.axis_size(axis)
-    tiled = jnp.broadcast_to(block[None], (devices,) + block.shape)
-    return lax.all_to_all(tiled, axis, 0, 0, tiled=True)
+    held = block[None]
+    have = 1
+    while have < devices:
+        take = min(have, devices - have)
+        pairs = [(i, (i + have) % devices) for i in range(devices)]
+        held = jnp.concatenate([held, lax.ppermute(held[:take], axis, pairs)], axis=0)
+        have += take
+    return held
 
 
 def coarse_from_samples(samples, count_all, bin_count):

time: 24.4 us -> 27.6 us (1.13)
  waiting for transfers between devices: 8.13 us -> 16.2 us
  starting transfers between devices: 9 us -> 4.76 us
  local copies, waits for them, and re-layouts: 0.64 us -> 0.01 us
    ppermute x0 -> x3, waiting for transfers between devices: none -> 14.8 us  [gather_years(): lax.ppermute(held[:take], axis, pairs)]
    all_to_all x1 -> x0, waiting for transfers between devices: 6.79 us -> none  [gather_years(): return lax.all_to_all(tiled, axis, 0, 0, tiled=True)]
    all_to_all x1 -> x0, starting transfers between devices: 6.54 us -> none  [gather_years(): return lax.all_to_all(tiled, axis, 0, 0, tiled=True)]
    ppermute x0 -> x3, starting transfers between devices: none -> 2.3 us  [gather_years(): lax.ppermute(held[:take], axis, pairs)]
    broadcast_in_dim x1 -> x0, local copies, waits for them, and re-layouts: 0.63 us -> none  [gather_years(): tiled = jnp.broadcast_to(block[None], (devices,) + block.shape)]
  transfers between devices with their start and end apart: 3 -> 5, of which waited for: 3 -> 5; matrix products, arithmetic and copies ran while one was open for 0% -> 0% of each run, Pallas kernels for 0% -> 0%
where the time goes in v3:
time: 27.6 us; the launch traced here: 27.2 us
  waiting for transfers between devices  16.2 us (59%)
  other arithmetic  5.64 us (20%)
  starting transfers between devices  4.76 us (17%)
  between operations  0.68 us (2%)
    ppermute x3, waiting for transfers between devices, gather_years(): lax.ppermute(held[:take], axis, pairs)  14.8 us
    ppermute x3, starting transfers between devices, gather_years(): lax.ppermute(held[:take], axis, pairs)  2.3 us
    ppermute x1, starting transfers between devices, extended_2(): after = lax.ppermute(leading, axis, down)  2.01 us
    reduce_sum x1, other arithmetic, coarse_from_samples(): jnp.sum(jnp.clip(upper[None] - scaled[:, None, :], 0.0, 1.0), axis=0)  1.66 us
    ppermute x1, waiting for transfers between devices, extended_2(): before = lax.ppermute(last, axis, up)  1.26 us
    concatenate x1, other arithmetic, shards(): stacked = jnp.concatenate([daily_temps[0], flag_row], axis=0)  0.84 us
    concatenate x1, other arithmetic, extended_2(): array = jnp.concatenate([before, array, after], axis=dim)  0.78 us
    convert_element_type x1, other arithmetic, shards(): extended[days_in].astype(jnp.float32)  0.75 us
  transfers between devices with their start and end apart: 5, of which 5 were waited for; matrix products, arithmetic and copies ran while one was open for 0% of the time, Pallas kernels for 0%

profile of v3, /device:TPU:0, one launch (start us, length us, event | category | flops | bytes accessed | tf_op | source)
XLA Modules:
  0.0 27.2 jit_solution(2865014873362903897)
XLA Ops:
  0.6 0.7 %convert_bitcast_fusion = bf16[1,128]{1,0:T(2,128)(2,1)S(1)} fusion(s32[128]{0:T(128)} %param.3), kind=kLoop, calls=%fused_computation.43 | loop fusion | flops 128 | bytes 768 | tf_op jit(solution)/shard_map/broadcast_in_dim | solution.py:65
  1.3 0.8 %slice_maximum_fusion = (bf16[23,1]{1,0:T(8,128)(2,1)S(1)}, bf16[23,1]{1,0:T(8,128)(2,1)S(1)}) fusion(bf16[1,128]{1,0:T(2,128)(2,1)S(1)} %convert_bitcast_fusion, bf16[22,128]{1,0:T(8,128)(2,1)} %bitcast.17), kind=kLoop, calls=%fused_computation.30 | loop fusion | flops 184 | bytes 5980 | tf_op jit(solution)/shard_map/concatenate | solution.py:66
  2.1 0.5 %collective-permute-start = (bf16[23,1]{1,0:T(8,128)(2,1)S(1)}, bf16[23,1]{1,0:T(8,128)(2,1)S(1)}, u32[]{:S(2)}, u32[]{:S(2)}) collective-permute-start(bf16[23,1]{1,0:T(8,128)(2,1)S(1)} %get-tuple-element.8), channel_id=1, source_target_pairs={{0,1},{1,2},{2,3},{3,0},{4,5},{5,6},{6,7},{7,4},{8,9},{9,10},{10,1... | collective-permute-start | bytes 146 | tf_op jit(solution)/shard_map/ppermute | solution.py:24
  2.6 2.0 %collective-permute-start.1 = (bf16[23,1]{1,0:T(8,128)(2,1)S(1)}, bf16[23,1]{1,0:T(8,128)(2,1)S(1)}, u32[]{:S(2)}, u32[]{:S(2)}) collective-permute-start(bf16[23,1]{1,0:T(8,128)(2,1)S(1)} %get-tuple-element.9), channel_id=1, source_target_pairs={{1,0},{2,1},{3,2},{0,3},{5,4},{6,5},{7,6},{4,7},{9,8},{10,9},{11,1... | collective-permute-start | bytes 146 | tf_op jit(solution)/shard_map/ppermute | solution.py:25
  4.6 1.3 %collective-permute-done = bf16[23,1]{1,0:T(8,128)(2,1)S(1)} collective-permute-done((bf16[23,1]{1,0:T(8,128)(2,1)S(1)}, bf16[23,1]{1,0:T(8,128)(2,1)S(1)}, u32[]{:S(2)}, u32[]{:S(2)}) %collective-permute-start) | collective-permute-done | bytes 78 | tf_op jit(solution)/shard_map/ppermute | solution.py:24
  5.9 0.1 collective-permute-done.1
  5.9 0.8 %maximum_convert_fusion = f32[1,130]{1,0:T(1,128)S(1)} fusion(bf16[23,1]{1,0:T(8,128)(2,1)S(1)} %collective-permute-done.1, bf16[23,1]{1,0:T(8,128)(2,1)S(1)} %collective-permute-done, bf16[1,128]{1,0:T(2,128)(2,1)S(1)} %convert_bitcast_fusion, bf16[22,128]{1,0:T(8,128)(2,1)} %bitcast.18), kind=kLoop, calls=%fused_computation.32 | loop fusion | flops 1040 | bytes 6500 | tf_op jit(solution)/shard_map/convert_element_type | solution.py:69
  6.7 0.1 subtract_bitcast_fusion.1
  6.8 0.1 bitcast_add_fusion
  6.9 0.8 %pad_maximum_fusion.1 = bf16[23,130]{1,0:T(8,128)(2,1)S(1)} fusion(bf16[23,1]{1,0:T(8,128)(2,1)S(1)} %collective-permute-done.1, bf16[1,128]{1,0:T(2,128)(2,1)S(1)} %convert_bitcast_fusion, bf16[22,128]{1,0:T(8,128)(2,1)} %bitcast.19, bf16[23,1]{1,0:T(8,128)(2,1)S(1)} %collective-permute-done), kind=kLoop, calls=%fused_computation.26 | loop fusion | flops 23920 | bytes 11960 | tf_op jit(solution)/shard_map/concatenate | solution.py:26
  7.6 0.1 fusion.15
  7.7 2.2 %collective-permute-start.2 = (bf16[1,22,128]{2,1,0:T(8,128)(2,1)S(1)}, bf16[1,22,128]{2,1,0:T(8,128)(2,1)S(1)}, u32[]{:S(2)}, u32[]{:S(2)}) collective-permute-start(bf16[1,22,128]{2,1,0:T(8,128)(2,1)S(1)} %fusion.15), channel_id=1, source_target_pairs={{0,4},{4,8},{8,12},{12,16},{16,20},{20,24},{24,28},{28,0},{1,5},{5... | collective-permute-start | bytes 16904 | tf_op jit(solution)/shard_map/ppermute | solution.py:45
  9.9 4.6 %collective-permute-done.2 = bf16[1,22,128]{2,1,0:T(8,128)(2,1)S(1)} collective-permute-done((bf16[1,22,128]{2,1,0:T(8,128)(2,1)S(1)}, bf16[1,22,128]{2,1,0:T(8,128)(2,1)S(1)}, u32[]{:S(2)}, u32[]{:S(2)}) %collective-permute-start.2) | collective-permute-done | bytes 5664 | tf_op jit(solution)/shard_map/ppermute | solution.py:45
  14.6 0.0 collective-permute-start.3
  14.6 5.5 %collective-permute-done.3 = bf16[2,22,128]{2,1,0:T(8,128)(2,1)S(1)} collective-permute-done((bf16[2,22,128]{2,1,0:T(8,128)(2,1)S(1)}, bf16[2,22,128]{2,1,0:T(8,128)(2,1)S(1)}, u32[]{:S(2)}, u32[]{:S(2)}) %collective-permute-start.3) | collective-permute-done | bytes 11296 | tf_op jit(solution)/shard_map/ppermute | solution.py:45
  20.1 0.1 collective-permute-start.4
  20.2 4.7 %collective-permute-done.4 = bf16[4,22,128]{2,1,0:T(8,128)(2,1)S(1)} collective-permute-done((bf16[4,22,128]{2,1,0:T(8,128)(2,1)S(1)}, bf16[4,22,128]{2,1,0:T(8,128)(2,1)S(1)}, u32[]{:S(2)}, u32[]{:S(2)}) %collective-permute-start.4) | collective-permute-done | bytes 22560 | tf_op jit(solution)/shard_map/ppermute | solution.py:45
  24.9 1.7 %clamp_reduce_fusion = f32[256,128]{1,0:T(8,128)S(1)} fusion(f32[120,128]{1,0:T(8,128)S(1)} %min.28, f32[256]{0:T(256)S(1)} %iota_add_fusion), kind=kLoop, calls=%fused_computation | loop fusion | flops 11763712 | bytes 193536 | tf_op jit(solution)/shard_map/reduce_sum | solution.py:54
  26.6 0.1 clamp_reduce_fusion.1
  26.7 0.1 fusion.7
  26.7 0.5 %bitcast_subtract_fusion = (f32[1,128]{1,0:T(1,128)}, f32[1,128]{1,0:T(1,128)}) fusion(f32[128]{0:T(128)S(1)} %fusion.7, f32[128]{0:T(128)S(1)} %clamp_reduce_fusion.1), kind=kLoop, calls=%fused_computation.38 | loop fusion | flops 768 | bytes 2048 | tf_op jit(solution)/shard_map/sub | solution.py:80
  (7 shorter events, 0.1 us)
Async XLA Ops:
  2.1 3.7 %collective-permute-start = (bf16[23,1]{1,0:T(8,128)(2,1)S(1)}, bf16[23,1]{1,0:T(8,128)(2,1)S(1)}, u32[]{:S(2)}, u32[]{:S(2)}) collective-permute-start(bf16[23,1]{1,0:T(8,128)(2,1)S(1)} %get-tuple-element.8), channel_id=1, source_target_pairs={{0,1},{1,2},{2,3},{3,0},{4,5},{5,6},{6,7},{7,4},{8,9},{9,10},{10,1... | collective-permute-start | bytes 146 | tf_op jit(solution)/shard_map/ppermute | solution.py:24
  2.6 3.4 %collective-permute-start.1 = (bf16[23,1]{1,0:T(8,128)(2,1)S(1)}, bf16[23,1]{1,0:T(8,128)(2,1)S(1)}, u32[]{:S(2)}, u32[]{:S(2)}) collective-permute-start(bf16[23,1]{1,0:T(8,128)(2,1)S(1)} %get-tuple-element.9), channel_id=1, source_target_pairs={{1,0},{2,1},{3,2},{0,3},{5,4},{6,5},{7,6},{4,7},{9,8},{10,9},{11,1... | collective-permute-start | bytes 146 | tf_op jit(solution)/shard_map/ppermute | solution.py:25
  7.7 6.9 %collective-permute-start.2 = (bf16[1,22,128]{2,1,0:T(8,128)(2,1)S(1)}, bf16[1,22,128]{2,1,0:T(8,128)(2,1)S(1)}, u32[]{:S(2)}, u32[]{:S(2)}) collective-permute-start(bf16[1,22,128]{2,1,0:T(8,128)(2,1)S(1)} %fusion.15), channel_id=1, source_target_pairs={{0,4},{4,8},{8,12},{12,16},{16,20},{20,24},{24,28},{28,0},{1,5},{5... | collective-permute-start | bytes 16904 | tf_op jit(solution)/shard_map/ppermute | solution.py:45
  14.6 5.5 %collective-permute-start.3 = (bf16[2,22,128]{2,1,0:T(8,128)(2,1)S(1)}, bf16[2,22,128]{2,1,0:T(8,128)(2,1)S(1)}, u32[]{:S(2)}, u32[]{:S(2)}) collective-permute-start(bf16[2,22,128]{2,1,0:T(8,128)(2,1)S(1)} %pad_maximum_fusion.2), channel_id=1, source_target_pairs={{0,8},{4,12},{8,16},{12,20},{16,24},{20,28},{24,0},{28,4},{1,9},{5... | collective-permute-start | bytes 33800 | tf_op jit(solution)/shard_map/ppermute | solution.py:45
  20.1 4.8 %collective-permute-start.4 = (bf16[4,22,128]{2,1,0:T(8,128)(2,1)S(1)}, bf16[4,22,128]{2,1,0:T(8,128)(2,1)S(1)}, u32[]{:S(2)}, u32[]{:S(2)}) collective-permute-start(bf16[4,22,128]{2,1,0:T(8,128)(2,1)S(1)} %pad_maximum_fusion), channel_id=1, source_target_pairs={{0,16},{4,20},{8,24},{12,28},{16,0},{20,4},{24,8},{28,12},{1,17},{... | collective-permute-start | bytes 67592 | tf_op jit(solution)/shard_map/ppermute | solution.py:45

commit v4 on v2

--- a/solution.py
+++ b/solution.py
@@ -14,19 +14,6 @@
 STEP_SIZE = 2.0
 
 
-def extended_2(array, sides, width):
-    for axis, dim in sides:
-        devices, length = (lax.axis_size(axis), array.shape[dim])
-        up = [(i, (i + 1) % devices) for i in range(devices)]
-        down = [(j, i) for i, j in up]
-        last = lax.slice_in_dim(array, length - width, length, axis=dim)
-        leading = lax.slice_in_dim(array, 0, width, axis=dim)
-        before = lax.ppermute(last, axis, up)
-        after = lax.ppermute(leading, axis, down)
-        array = jnp.concatenate([before, array, after], axis=dim)
-    return array
-
-
 def smooth_field(extended, flags):
     center = extended[..., 1:-1]
     same_west = 1.0 - jnp.abs(flags[1:-1] - flags[:-2])
@@ -35,10 +22,10 @@
     return (mixed / (1.0 + same_west + same_east)).astype(jnp.bfloat16)
 
 
-def gather_years(block, axis):
-    devices = lax.axis_size(axis)
+def gather_everything(block):
+    devices = lax.axis_size("year") * lax.axis_size("region")
     tiled = jnp.broadcast_to(block[None], (devices,) + block.shape)
-    return lax.all_to_all(tiled, axis, 0, 0, tiled=True)
+    return lax.all_to_all(tiled, ("year", "region"), 0, 0, tiled=True)
 
 
 def coarse_from_samples(samples, count_all, bin_count):
@@ -52,17 +39,20 @@
 
 def shards(daily_temps, land_mask):
     days_in = daily_temps.shape[1]
+    lon_own = daily_temps.shape[2]
     year_count = lax.axis_size("year")
+    region_count = lax.axis_size("region")
     cal_days = days_in - WIN + 1
     cal_own = cal_days // year_count
     count_all = float(year_count * WIN)
     flag_row = land_mask.astype(jnp.bfloat16)[None, :]
     stacked = jnp.concatenate([daily_temps[0], flag_row], axis=0)
-    extended = extended_2(stacked, (("region", 1),), 1)
-    smoothed = smooth_field(
-        extended[:days_in].astype(jnp.float32), extended[days_in].astype(jnp.float32)
-    )
-    every_year = gather_years(smoothed, "year").astype(jnp.float32)
+    everything = gather_everything(stacked).reshape(year_count, region_count, days_in + 1, lon_own)
+    row = jnp.moveaxis(everything, 1, 2).reshape(year_count, days_in + 1, region_count * lon_own)
+    ring = jnp.concatenate([row[..., -1:], row, row[..., :1]], axis=-1)
+    extended = lax.dynamic_slice_in_dim(ring, lax.axis_index("region") * lon_own, lon_own + 2, axis=2)
+    extended = extended.astype(jnp.float32)
+    every_year = smooth_field(extended[:, :days_in], extended[0, days_in]).astype(jnp.float32)
     first_day = lax.axis_index("year") * cal_own
     coarse_rows = []
     refined_rows = []

time: 24.4 us -> 22.2 us (0.910)
  starting transfers between devices: 9 us -> 7.3 us
  other arithmetic: 5.61 us -> 3.94 us
  waiting for transfers between devices: 8.13 us -> 8.87 us
  local copies, waits for them, and re-layouts: 0.64 us -> 1.01 us
    ppermute x2 -> x0, starting transfers between devices: 2.46 us -> none  [the longest x1 2.01 us: extended_2(): after = lax.ppermute(leading, axis, down)]
    all_to_all x1, waiting for transfers between devices: 6.79 us -> 8.87 us  [gather_everything(): return lax.all_to_all(tiled, ('year', 'region'), 0, 0, tiled=True)]
    ppermute x2 -> x0, waiting for transfers between devices: 1.35 us -> none  [the longest x1 1.26 us: extended_2(): before = lax.ppermute(last, axis, up)]
    concatenate x1 -> x0, other arithmetic: 0.78 us -> none  [extended_2(): array = jnp.concatenate([before, array, after], axis=dim)]
    all_to_all x1, starting transfers between devices: 6.54 us -> 7.3 us  [gather_everything(): return lax.all_to_all(tiled, ('year', 'region'), 0, 0, tiled=True)]
    convert_element_type x3 -> x1, other arithmetic: 0.84 us -> 0.16 us  [shards(): extended = extended.astype(jnp.float32)]
  transfers between devices with their start and end apart: 3 -> 1, of which waited for: 3 -> 1; matrix products, arithmetic and copies ran while one was open for 0% -> 0% of each run, Pallas kernels for 0% -> 0%
where the time goes in v4:
time: 22.2 us; the launch traced here: 21.8 us
  waiting for transfers between devices  8.87 us (40%)
  starting transfers between devices  7.3 us (33%)
  other arithmetic  3.94 us (18%)
  local copies, waits for them, and re-layouts  1.01 us (5%)
  between operations  0.7 us (3%)
    all_to_all x1, waiting for transfers between devices, gather_everything(): return lax.all_to_all(tiled, ('year', 'region'), 0, 0, tiled=True)  8.87 us
    all_to_all x1, starting transfers between devices, gather_everything(): return lax.all_to_all(tiled, ('year', 'region'), 0, 0, tiled=True)  7.3 us
    reduce_sum x1, other arithmetic, coarse_from_samples(): jnp.sum(jnp.clip(upper[None] - scaled[:, None, :], 0.0, 1.0), axis=0)  1.66 us
    concatenate x1, other arithmetic, shards(): stacked = jnp.concatenate([daily_temps[0], flag_row], axis=0)  0.7 us
    broadcast_in_dim x1, local copies, waits for them, and re-layouts, gather_everything(): tiled = jnp.broadcast_to(block[None], (devices,) + block.shape)  0.7 us
    broadcast_in_dim x1, other arithmetic, shards(): flag_row = land_mask.astype(jnp.bfloat16)[None, :]  0.66 us
    sub x1, other arithmetic, shards(): refined = coarse - STEP_SIZE * (cdf / count_all - QUANT_LEVEL)  0.52 us
  transfers between devices with their start and end apart: 1, of which 1 were waited for; matrix products, arithmetic and copies ran while one was open for 0% of the time, Pallas kernels for 0%

profile of v4, /device:TPU:0, one launch (start us, length us, event | category | flops | bytes accessed | tf_op | source)
XLA Modules:
  0.0 21.8 jit_solution(18038595526625934817)
XLA Ops:
  0.6 0.7 %convert_bitcast_fusion = bf16[1,128]{1,0:T(2,128)(2,1)S(1)} fusion(s32[128]{0:T(128)} %param.3), kind=kLoop, calls=%fused_computation.34 | loop fusion | flops 128 | bytes 768 | tf_op jit(solution)/shard_map/broadcast_in_dim | solution.py:48
  1.3 0.7 %pad_maximum_fusion = bf16[23,128]{1,0:T(8,128)(2,1)S(1)} fusion(bf16[1,128]{1,0:T(2,128)(2,1)S(1)} %convert_bitcast_fusion, bf16[22,128]{1,0:T(8,128)(2,1)} %bitcast.19), kind=kLoop, calls=%fused_computation.24 | loop fusion | flops 11776 | bytes 11776 | tf_op jit(solution)/shard_map/concatenate | solution.py:49
  2.0 0.7 %broadcast_in_dim.5 = bf16[32,23,128]{2,1,0:T(8,128)(2,1)} broadcast(bf16[23,128]{1,0:T(8,128)(2,1)S(1)} %pad_maximum_fusion), dimensions={1,2} | broadcast | bytes 194304 | tf_op jit(solution)/shard_map/broadcast_in_dim | solution.py:27
  2.7 7.3 %all-to-all-start = ((bf16[32,23,128]{2,1,0:T(8,128)(2,1)}), bf16[32,23,128]{2,1,0:T(8,128)(2,1)S(1)}, u32[]{:S(2)}, u32[]{:S(2)}) async-start(bf16[32,23,128]{2,1,0:T(8,128)(2,1)} %broadcast_in_dim.5), calls=%async_computation | async-start | bytes 393216 | tf_op jit(solution)/shard_map/all_to_all | solution.py:28
  10.0 8.9 %all-to-all-done = bf16[32,23,128]{2,1,0:T(8,128)(2,1)S(1)} async-done(((bf16[32,23,128]{2,1,0:T(8,128)(2,1)}), bf16[32,23,128]{2,1,0:T(8,128)(2,1)S(1)}, u32[]{:S(2)}, u32[]{:S(2)}) %all-to-all-start) | async-done | bytes 188448 | tf_op jit(solution)/shard_map/all_to_all | solution.py:28
  18.9 0.1 reshape.81
  19.0 0.1 fusion.22
  19.1 0.2 fusion.2
  19.2 0.1 fusion.21
  19.4 0.1 add_bitcast_fusion
  19.5 1.7 %clamp_reduce_fusion = f32[256,128]{1,0:T(8,128)S(1)} fusion(f32[120,128]{1,0:T(8,128)S(1)} %min.28, f32[256]{0:T(256)S(1)} %iota_add_fusion), kind=kLoop, calls=%fused_computation | loop fusion | flops 11763712 | bytes 193536 | tf_op jit(solution)/shard_map/reduce_sum | solution.py:35
  21.2 0.1 clamp_reduce_fusion.1
  21.2 0.1 fusion.12
  21.3 0.5 %bitcast_subtract_fusion = (f32[1,128]{1,0:T(1,128)}, f32[1,128]{1,0:T(1,128)}) fusion(f32[128]{0:T(128)S(1)} %fusion.12, f32[128]{0:T(128)S(1)} %clamp_reduce_fusion.1), kind=kLoop, calls=%fused_computation.30 | loop fusion | flops 768 | bytes 2048 | tf_op jit(solution)/shard_map/sub | solution.py:64
  (6 shorter events, 0.1 us)
Async XLA Ops:
  2.7 16.2 %all-to-all-start = ((bf16[32,23,128]{2,1,0:T(8,128)(2,1)}), bf16[32,23,128]{2,1,0:T(8,128)(2,1)S(1)}, u32[]{:S(2)}, u32[]{:S(2)}) async-start(bf16[32,23,128]{2,1,0:T(8,128)(2,1)} %broadcast_in_dim.5), calls=%async_computation | async-start | bytes 393216 | tf_op jit(solution)/shard_map/all_to_all | solution.py:28

commit v5 on v4

--- a/solution.py
+++ b/solution.py
@@ -19,13 +19,23 @@
     same_west = 1.0 - jnp.abs(flags[1:-1] - flags[:-2])
     same_east = 1.0 - jnp.abs(flags[1:-1] - flags[2:])
     mixed = center + same_west * extended[..., :-2] + same_east * extended[..., 2:]
-    return (mixed / (1.0 + same_west + same_east)).astype(jnp.bfloat16)
+    return lax.reduce_precision(mixed / (1.0 + same_west + same_east), exponent_bits=8, mantissa_bits=7)
 
 
-def gather_everything(block):
-    devices = lax.axis_size("year") * lax.axis_size("region")
-    tiled = jnp.broadcast_to(block[None], (devices,) + block.shape)
-    return lax.all_to_all(tiled, ("year", "region"), 0, 0, tiled=True)
+def gather_windows(temps, flags, span, cal_own):
+    year_count, region_count = lax.axis_size("year"), lax.axis_size("region")
+    chunk_rows = span + 1
+    total = year_count * region_count * chunk_rows
+    out_row = lax.broadcasted_iota(jnp.int32, (total, temps.shape[0]), 0)
+    day = lax.broadcasted_iota(jnp.int32, (total, temps.shape[0]), 1)
+    offset = out_row % chunk_rows
+    first = (out_row // (chunk_rows * region_count)) * cal_own
+    select = jnp.where((offset < span) & (day == first + offset), 1.0, 0.0).astype(temps.dtype)
+    picked = jnp.dot(select, temps, preferred_element_type=jnp.float32)
+    is_flag = (lax.broadcasted_iota(jnp.int32, (total, 1), 0) % chunk_rows) == span
+    rows = jnp.where(is_flag, flags.astype(jnp.float32)[None, :], picked).astype(temps.dtype)
+    rows = rows.reshape(year_count * region_count, chunk_rows, temps.shape[1])
+    return lax.all_to_all(rows, ("year", "region"), 0, 0, tiled=True)
 
 
 def coarse_from_samples(samples, count_all, bin_count):
@@ -44,21 +54,19 @@
     region_count = lax.axis_size("region")
     cal_days = days_in - WIN + 1
     cal_own = cal_days // year_count
+    span = WIN + cal_own - 1
     count_all = float(year_count * WIN)
-    flag_row = land_mask.astype(jnp.bfloat16)[None, :]
-    stacked = jnp.concatenate([daily_temps[0], flag_row], axis=0)
-    everything = gather_everything(stacked).reshape(year_count, region_count, days_in + 1, lon_own)
-    row = jnp.moveaxis(everything, 1, 2).reshape(year_count, days_in + 1, region_count * lon_own)
+    received = gather_windows(daily_temps[0], land_mask, span, cal_own)
+    received = received.reshape(year_count, region_count, span + 1, lon_own)
+    row = jnp.moveaxis(received, 1, 2).reshape(year_count, span + 1, region_count * lon_own)
     ring = jnp.concatenate([row[..., -1:], row, row[..., :1]], axis=-1)
     extended = lax.dynamic_slice_in_dim(ring, lax.axis_index("region") * lon_own, lon_own + 2, axis=2)
     extended = extended.astype(jnp.float32)
-    every_year = smooth_field(extended[:, :days_in], extended[0, days_in]).astype(jnp.float32)
-    first_day = lax.axis_index("year") * cal_own
+    every_year = smooth_field(extended[:, :span], extended[0, span])
     coarse_rows = []
     refined_rows = []
     for j in range(cal_own):
-        window = lax.dynamic_slice_in_dim(every_year, first_day + j, WIN, axis=1)
-        samples = window.reshape(-1, window.shape[-1])
+        samples = every_year[:, j : j + WIN].reshape(-1, lon_own)
         coarse = coarse_from_samples(samples, count_all, BINS)
         cdf = jnp.sum(jax.nn.sigmoid((coarse[None] - samples) / KERNEL_SCALE), axis=0)
         refined = coarse - STEP_SIZE * (cdf / count_all - QUANT_LEVEL)

time: 22.2 us -> 21.6 us (0.973)
  matrix products: 0 us -> 1.48 us
  local copies, waits for them, and re-layouts: 1.01 us -> 0.21 us
  waiting for transfers between devices: 8.87 us -> 8.21 us
  other arithmetic: 3.94 us -> 3.41 us
    dot_general x0 -> x1, matrix products: none -> 1.48 us  [gather_windows(): picked = jnp.dot(select, temps, preferred_element_type=jnp.float32)]
    concatenate x1 -> x0, other arithmetic: 0.7 us -> none  [shards(): stacked = jnp.concatenate([daily_temps[0], flag_row], axis=0)]
    broadcast_in_dim x1 -> x0, local copies, waits for them, and re-layouts: 0.7 us -> none  [gather_everything(): tiled = jnp.broadcast_to(block[None], (devices,) + block.shape)]
    convert_element_type x0 -> x1, other arithmetic: none -> 0.66 us  [gather_windows(): flags.astype(jnp.float32)[None, :]]
    broadcast_in_dim x1 -> x0, other arithmetic: 0.66 us -> none  [shards(): flag_row = land_mask.astype(jnp.bfloat16)[None, :]]
    all_to_all x1, waiting for transfers between devices: 8.87 us -> 8.21 us  [gather_windows(): return lax.all_to_all(rows, ('year', 'region'), 0, 0, tiled=True)]
where the time goes in v5:
time: 21.6 us; the launch traced here: 21.3 us
  waiting for transfers between devices  8.21 us (38%)
  starting transfers between devices  7.3 us (34%)
  other arithmetic  3.41 us (16%)
  matrix products  1.48 us (7%)
  between operations  0.72 us (3%)
    all_to_all x1, waiting for transfers between devices, gather_windows(): return lax.all_to_all(rows, ('year', 'region'), 0, 0, tiled=True)  8.21 us
    all_to_all x1, starting transfers between devices, gather_windows(): return lax.all_to_all(rows, ('year', 'region'), 0, 0, tiled=True)  7.3 us
    reduce_sum x1, other arithmetic, coarse_from_samples(): jnp.sum(jnp.clip(upper[None] - scaled[:, None, :], 0.0, 1.0), axis=0)  1.76 us
    dot_general x1, matrix products, gather_windows(): picked = jnp.dot(select, temps, preferred_element_type=jnp.float32)  1.48 us
    convert_element_type x1, other arithmetic, gather_windows(): flags.astype(jnp.float32)[None, :]  0.66 us
    sub x1, other arithmetic, shards(): refined = coarse - STEP_SIZE * (cdf / count_all - QUANT_LEVEL)  0.52 us
  transfers between devices with their start and end apart: 1, of which 1 were waited for; matrix products, arithmetic and copies ran while one was open for 0% of the time, Pallas kernels for 0%

profile of v5, /device:TPU:0, one launch (start us, length us, event | category | flops | bytes accessed | tf_op | source)
XLA Modules:
  0.0 21.3 jit_solution(9785214341323302306)
XLA Ops:
  0.6 0.0 copy-start
  0.7 0.7 %convert_element_type.12 = bf16[128]{0:T(256)(128)(2,1)S(1)} convert(s32[128]{0:T(128)} %param.3) | non-fusion elementwise | flops 128 | bytes 768 | tf_op jit(solution)/shard_map/convert_element_type | solution.py:36
  1.4 0.0 copy-done
  1.4 1.5 %fusion = bf16[512,128]{1,0:T(8,128)(2,1)} fusion(s32[512]{0:T(512)S(1)} %get-tuple-element.11, s32[512]{0:T(512)S(1)} %get-tuple-element.16, s32[512]{0:T(512)S(1)} %get-tuple-element.12, s32[512]{0:T(512)S(1)} %get-tuple-element.15, bf16[128]{0:T(256)(128)(2,1)S(1)} %convert_element_type.12, pred[512]{0:T(512)(128)(4,1)S(1)} %fusion.27, ...), kind=kOutput, calls=%fused_computation.2 | convolution fusion | flops 3039232 | bytes 146688 | tf_op jit(solution)/shard_map/dot_general | solution.py:34
  2.8 7.3 %all-to-all-start = ((bf16[32,16,128]{2,1,0:T(8,128)(2,1)}), bf16[32,16,128]{2,1,0:T(8,128)(2,1)S(1)}, u32[]{:S(2)}, u32[]{:S(2)}) async-start(bf16[32,16,128]{2,1,0:T(8,128)(2,1)} %bitcast.1), calls=%async_computation | async-start | bytes 262144 | tf_op jit(solution)/shard_map/all_to_all | solution.py:38
  10.2 8.2 %all-to-all-done = bf16[32,16,128]{2,1,0:T(8,128)(2,1)S(1)} async-done(((bf16[32,16,128]{2,1,0:T(8,128)(2,1)}), bf16[32,16,128]{2,1,0:T(8,128)(2,1)S(1)}, u32[]{:S(2)}, u32[]{:S(2)}) %all-to-all-start) | async-done | bytes 131104 | tf_op jit(solution)/shard_map/all_to_all | solution.py:38
  18.4 0.1 copy.8
  18.4 0.1 reshape.102
  18.5 0.1 fusion.38
  18.6 0.1 fusion.14
  18.7 0.1 add_bitcast_fusion
  18.8 0.1 multiply_clamp_fusion
  18.9 1.8 %clamp_reduce_fusion = f32[256,128]{1,0:T(8,128)S(1)} fusion(f32[120,128]{1,0:T(8,128)S(1)} %min.28, f32[256]{0:T(256)S(1)} %iota_add_fusion), kind=kLoop, calls=%fused_computation | loop fusion | flops 11763712 | bytes 193536 | tf_op jit(solution)/shard_map/reduce_sum | solution.py:45
  20.7 0.1 clamp_reduce_fusion.1
  20.7 0.1 fusion.19
  20.8 0.5 %bitcast_subtract_fusion = (f32[1,128]{1,0:T(1,128)}, f32[1,128]{1,0:T(1,128)}) fusion(f32[128]{0:T(128)S(1)} %fusion.19, f32[128]{0:T(128)S(1)} %clamp_reduce_fusion.1), kind=kLoop, calls=%fused_computation.53 | loop fusion | flops 768 | bytes 2048 | tf_op jit(solution)/shard_map/sub | solution.py:72
  (7 shorter events, 0.0 us)
Async XLA Ops:
  0.6 0.7 %copy-start = (bf16[1,22,128]{2,1,0:T(8,128)(2,1)S(1)}, bf16[1,22,128]{2,1,0:T(8,128)(2,1)}, u32[]{:S(2)}) copy-start(bf16[1,22,128]{2,1,0:T(8,128)(2,1)} %param.2) | copy-start | bytes 16900
  2.8 15.5 %all-to-all-start = ((bf16[32,16,128]{2,1,0:T(8,128)(2,1)}), bf16[32,16,128]{2,1,0:T(8,128)(2,1)S(1)}, u32[]{:S(2)}, u32[]{:S(2)}) async-start(bf16[32,16,128]{2,1,0:T(8,128)(2,1)} %bitcast.1), calls=%async_computation | async-start | bytes 262144 | tf_op jit(solution)/shard_map/all_to_all | solution.py:38

commit v6 on v5

--- a/solution.py
+++ b/solution.py
@@ -25,15 +25,15 @@
 def gather_windows(temps, flags, span, cal_own):
     year_count, region_count = lax.axis_size("year"), lax.axis_size("region")
     chunk_rows = span + 1
-    total = year_count * region_count * chunk_rows
-    out_row = lax.broadcasted_iota(jnp.int32, (total, temps.shape[0]), 0)
-    day = lax.broadcasted_iota(jnp.int32, (total, temps.shape[0]), 1)
-    offset = out_row % chunk_rows
-    first = (out_row // (chunk_rows * region_count)) * cal_own
-    select = jnp.where((offset < span) & (day == first + offset), 1.0, 0.0).astype(temps.dtype)
-    picked = jnp.dot(select, temps, preferred_element_type=jnp.float32)
-    is_flag = (lax.broadcasted_iota(jnp.int32, (total, 1), 0) % chunk_rows) == span
-    rows = jnp.where(is_flag, flags.astype(jnp.float32)[None, :], picked).astype(temps.dtype)
+    shape = (year_count, region_count, chunk_rows, temps.shape[0] + 1)
+    year = lax.broadcasted_iota(jnp.int32, shape, 0)
+    offset = lax.broadcasted_iota(jnp.int32, shape, 2)
+    day = lax.broadcasted_iota(jnp.int32, shape, 3)
+    wanted = jnp.where(offset < span, year * cal_own + offset, temps.shape[0])
+    select = jnp.where(day == wanted, 1.0, 0.0).astype(temps.dtype)
+    select = select.reshape(year_count * region_count * chunk_rows, temps.shape[0] + 1)
+    source = jnp.concatenate([temps, flags.astype(temps.dtype)[None, :]], axis=0)
+    rows = jnp.dot(select, source, preferred_element_type=jnp.float32).astype(temps.dtype)
     rows = rows.reshape(year_count * region_count, chunk_rows, temps.shape[1])
     return lax.all_to_all(rows, ("year", "region"), 0, 0, tiled=True)
 

time: 21.6 us -> 21.8 us (level)
    broadcast_in_dim x0 -> x1, other arithmetic: none -> 0.66 us  [gather_windows(): flags.astype(temps.dtype)[None, :]]
    convert_element_type x1 -> x0, other arithmetic: 0.66 us -> none  [gather_windows(): flags.astype(jnp.float32)[None, :]]
where the time goes in v6:
time: 21.8 us; the launch traced here: 21.5 us
  waiting for transfers between devices  8.21 us (38%)
  starting transfers between devices  7.3 us (33%)
  other arithmetic  3.31 us (15%)
  matrix products  1.65 us (8%)
  between operations  0.7 us (3%)
  local copies, waits for them, and re-layouts  0.38 us (2%)
    all_to_all x1, waiting for transfers between devices, gather_windows(): return lax.all_to_all(rows, ('year', 'region'), 0, 0, tiled=True)  8.21 us
    all_to_all x1, starting transfers between devices, gather_windows(): return lax.all_to_all(rows, ('year', 'region'), 0, 0, tiled=True)  7.3 us
    reduce_sum x1, other arithmetic, coarse_from_samples(): jnp.sum(jnp.clip(upper[None] - scaled[:, None, :], 0.0, 1.0), axis=0)  1.66 us
    dot_general x1, matrix products, gather_windows(): jnp.dot(select, source, preferred_element_type=jnp.float32)  1.65 us
    broadcast_in_dim x1, other arithmetic, gather_windows(): flags.astype(temps.dtype)[None, :]  0.66 us
    sub x1, other arithmetic, shards(): refined = coarse - STEP_SIZE * (cdf / count_all - QUANT_LEVEL)  0.52 us
  transfers between devices with their start and end apart: 1, of which 1 were waited for; matrix products, arithmetic and copies ran while one was open for 0% of the time, Pallas kernels for 0%

profile of v6, /device:TPU:0, one launch (start us, length us, event | category | flops | bytes accessed | tf_op | source)
XLA Modules:
  0.0 21.5 jit_solution(9664424284696068585)
XLA Ops:
  0.7 0.1 add.93
  0.7 0.1 iota.39
  0.8 0.7 %convert_bitcast_fusion = bf16[1,128]{1,0:T(2,128)(2,1)S(1)} fusion(s32[128]{0:T(128)} %param.3), kind=kLoop, calls=%fused_computation.39 | loop fusion | flops 128 | bytes 768 | tf_op jit(solution)/shard_map/broadcast_in_dim | solution.py:35
  1.5 1.7 %convolution_convert_fusion = bf16[512,128]{1,0:T(8,128)(2,1)} fusion(s32[512]{0:T(512)S(1)} %add.93, pred[512]{0:T(512)(128)(4,1)S(1)} %iota.39, bf16[1,128]{1,0:T(2,128)(2,1)S(1)} %convert_bitcast_fusion, bf16[22,128]{1,0:T(8,128)(2,1)} %bitcast.21), kind=kOutput, calls=%fused_computation.1 | convolution fusion | flops 3139072 | bytes 139520 | tf_op jit(solution)/shard_map/dot_general | solution.py:36
  3.2 7.3 %all-to-all-start = ((bf16[32,16,128]{2,1,0:T(8,128)(2,1)}), bf16[32,16,128]{2,1,0:T(8,128)(2,1)S(1)}, u32[]{:S(2)}, u32[]{:S(2)}) async-start(bf16[32,16,128]{2,1,0:T(8,128)(2,1)} %bitcast.2), calls=%async_computation | async-start | bytes 262144 | tf_op jit(solution)/shard_map/all_to_all | solution.py:38
  10.5 8.2 %all-to-all-done = bf16[32,16,128]{2,1,0:T(8,128)(2,1)S(1)} async-done(((bf16[32,16,128]{2,1,0:T(8,128)(2,1)}), bf16[32,16,128]{2,1,0:T(8,128)(2,1)S(1)}, u32[]{:S(2)}, u32[]{:S(2)}) %all-to-all-start) | async-done | bytes 131104 | tf_op jit(solution)/shard_map/all_to_all | solution.py:38
  18.7 0.1 copy.8
  18.7 0.1 reshape.90
  18.8 0.1 fusion.27
  18.9 0.1 fusion.7
  19.0 0.1 add_bitcast_fusion
  19.1 0.1 multiply_clamp_fusion
  19.2 1.7 %clamp_reduce_fusion = f32[256,128]{1,0:T(8,128)S(1)} fusion(f32[120,128]{1,0:T(8,128)S(1)} %min.28, f32[256]{0:T(256)S(1)} %iota_add_fusion.1), kind=kLoop, calls=%fused_computation | loop fusion | flops 11763712 | bytes 193536 | tf_op jit(solution)/shard_map/reduce_sum | solution.py:45
  20.9 0.1 clamp_reduce_fusion.1
  21.0 0.1 fusion.12
  21.0 0.5 %bitcast_subtract_fusion = (f32[1,128]{1,0:T(1,128)}, f32[1,128]{1,0:T(1,128)}) fusion(f32[128]{0:T(128)S(1)} %fusion.12, f32[128]{0:T(128)S(1)} %clamp_reduce_fusion.1), kind=kLoop, calls=%fused_computation.35 | loop fusion | flops 768 | bytes 2048 | tf_op jit(solution)/shard_map/sub | solution.py:72
  (6 shorter events, 0.0 us)
Async XLA Ops:
  3.2 15.5 %all-to-all-start = ((bf16[32,16,128]{2,1,0:T(8,128)(2,1)}), bf16[32,16,128]{2,1,0:T(8,128)(2,1)S(1)}, u32[]{:S(2)}, u32[]{:S(2)}) async-start(bf16[32,16,128]{2,1,0:T(8,128)(2,1)} %bitcast.2), calls=%async_computation | async-start | bytes 262144 | tf_op jit(solution)/shard_map/all_to_all | solution.py:38

commit v7 on v6

--- a/solution.py
+++ b/solution.py
@@ -1,6 +1,10 @@
+import functools
+
 import jax
 import jax.numpy as jnp
 from jax import lax
+from jax.experimental import pallas as pl
+from jax.experimental.pallas import tpu as pltpu
 from jax.sharding import PartitionSpec as P
 
 WIN = 15
@@ -22,19 +26,31 @@
     return lax.reduce_precision(mixed / (1.0 + same_west + same_east), exponent_bits=8, mantissa_bits=7)
 
 
+def chunk_kernel(span, cal_own, year_count, region_count, temps_ref, mask_ref, out_ref, stage_ref):
+    days_in = temps_ref.shape[0]
+    chunk_rows = span + 1
+    stage_ref[0:days_in, :] = temps_ref[...].astype(jnp.float32)
+    flags = mask_ref[...].astype(jnp.float32)
+    stage_ref[days_in : days_in + 1, :] = flags
+    is_flag = lax.broadcasted_iota(jnp.int32, (chunk_rows, out_ref.shape[1]), 0) == span
+    for year in range(year_count):
+        rows = stage_ref[year * cal_own : year * cal_own + chunk_rows, :]
+        tile = jnp.where(is_flag, flags, rows).astype(out_ref.dtype)
+        for region in range(region_count):
+            first = (year * region_count + region) * chunk_rows
+            out_ref[first : first + chunk_rows, :] = tile
+
+
 def gather_windows(temps, flags, span, cal_own):
     year_count, region_count = lax.axis_size("year"), lax.axis_size("region")
     chunk_rows = span + 1
-    shape = (year_count, region_count, chunk_rows, temps.shape[0] + 1)
-    year = lax.broadcasted_iota(jnp.int32, shape, 0)
-    offset = lax.broadcasted_iota(jnp.int32, shape, 2)
-    day = lax.broadcasted_iota(jnp.int32, shape, 3)
-    wanted = jnp.where(offset < span, year * cal_own + offset, temps.shape[0])
-    select = jnp.where(day == wanted, 1.0, 0.0).astype(temps.dtype)
-    select = select.reshape(year_count * region_count * chunk_rows, temps.shape[0] + 1)
-    source = jnp.concatenate([temps, flags.astype(temps.dtype)[None, :]], axis=0)
-    rows = jnp.dot(select, source, preferred_element_type=jnp.float32).astype(temps.dtype)
-    rows = rows.reshape(year_count * region_count, chunk_rows, temps.shape[1])
+    lon_own = temps.shape[1]
+    rows = pl.pallas_call(
+        functools.partial(chunk_kernel, span, cal_own, year_count, region_count),
+        out_shape=jax.ShapeDtypeStruct((year_count * region_count * chunk_rows, lon_own), temps.dtype),
+        scratch_shapes=[pltpu.VMEM((temps.shape[0] + 1, lon_own), jnp.float32)],
+    )(temps, flags.reshape(1, lon_own))
+    rows = rows.reshape(year_count * region_count, chunk_rows, lon_own)
     return lax.all_to_all(rows, ("year", "region"), 0, 0, tiled=True)
 
 

time: 21.8 us -> 20.6 us (0.945)
  matrix products: 1.65 us -> 0 us
  Pallas kernels: 0 us -> 1.35 us
  other arithmetic: 3.31 us -> 2.63 us
    dot_general x1 -> x0, matrix products: 1.65 us -> none  [gather_windows(): jnp.dot(select, source, preferred_element_type=jnp.float32)]
    pallas_call x0 -> x1, Pallas kernels: none -> 1.35 us  [gather_windows(): pl.pallas_call(functools.partial(chunk_kernel, span, cal_own, year_count,...]
    broadcast_in_dim x1 -> x0, other arithmetic: 0.66 us -> none  [gather_windows(): flags.astype(temps.dtype)[None, :]]
where the time goes in v7:
time: 20.6 us; the launch traced here: 20.4 us
  waiting for transfers between devices  8.21 us (40%)
  starting transfers between devices  7.3 us (35%)
  other arithmetic  2.63 us (13%)
  Pallas kernels  1.35 us (7%)
  between operations  0.68 us (3%)
    all_to_all x1, waiting for transfers between devices, gather_windows(): return lax.all_to_all(rows, ('year', 'region'), 0, 0, tiled=True)  8.21 us
    all_to_all x1, starting transfers between devices, gather_windows(): return lax.all_to_all(rows, ('year', 'region'), 0, 0, tiled=True)  7.3 us
    reduce_sum x1, other arithmetic, coarse_from_samples(): jnp.sum(jnp.clip(upper[None] - scaled[:, None, :], 0.0, 1.0), axis=0)  1.66 us
    pallas_call x1, Pallas kernels, gather_windows(): pl.pallas_call(functools.partial(chunk_kernel, span, cal_own, year_count,...  1.35 us
    sub x1, other arithmetic, shards(): refined = coarse - STEP_SIZE * (cdf / count_all - QUANT_LEVEL)  0.52 us
  transfers between devices with their start and end apart: 1, of which 1 were waited for; matrix products, arithmetic and copies ran while one was open for 0% of the time, Pallas kernels for 0%

profile of v7, /device:TPU:0, one launch (start us, length us, event | category | flops | bytes accessed | tf_op | source)
XLA Modules:
  0.0 20.4 jit_solution(13475964797234915189)
XLA Ops:
  0.6 1.3 %shard_map.41 = bf16[512,128]{1,0:T(8,128)(2,1)} custom-call(bf16[22,128]{1,0:T(8,128)(2,1)} %bitcast.20, s32[1,128]{1,0:T(1,128)} %bitcast.22), custom_call_target="tpu_custom_call" | custom-call | tf_op jit(solution)/shard_map/pallas_call | solution.py:48
  2.0 7.3 %all-to-all-start = ((bf16[32,16,128]{2,1,0:T(8,128)(2,1)}), bf16[32,16,128]{2,1,0:T(8,128)(2,1)S(1)}, u32[]{:S(2)}, u32[]{:S(2)}) async-start(bf16[32,16,128]{2,1,0:T(8,128)(2,1)} %bitcast.18), calls=%async_computation | async-start | bytes 262144 | tf_op jit(solution)/shard_map/all_to_all | solution.py:54
  9.3 8.2 %all-to-all-done = bf16[32,16,128]{2,1,0:T(8,128)(2,1)S(1)} async-done(((bf16[32,16,128]{2,1,0:T(8,128)(2,1)}), bf16[32,16,128]{2,1,0:T(8,128)(2,1)S(1)}, u32[]{:S(2)}, u32[]{:S(2)}) %all-to-all-start) | async-done | bytes 131104 | tf_op jit(solution)/shard_map/all_to_all | solution.py:54
  17.5 0.1 copy.8
  17.6 0.1 reshape.88
  17.6 0.1 fusion.15
  17.7 0.1 fusion.2
  17.9 0.1 add_bitcast_fusion
  17.9 0.1 multiply_clamp_fusion
  18.1 1.7 %clamp_reduce_fusion = f32[256,128]{1,0:T(8,128)S(1)} fusion(f32[120,128]{1,0:T(8,128)S(1)} %min.28, f32[256]{0:T(256)S(1)} %iota_add_fusion), kind=kLoop, calls=%fused_computation | loop fusion | flops 11763712 | bytes 193536 | tf_op jit(solution)/shard_map/reduce_sum | solution.py:61
  19.7 0.1 clamp_reduce_fusion.1
  19.8 0.1 fusion.7
  19.8 0.5 %bitcast_subtract_fusion = (f32[1,128]{1,0:T(1,128)}, f32[1,128]{1,0:T(1,128)}) fusion(f32[128]{0:T(128)S(1)} %fusion.7, f32[128]{0:T(128)S(1)} %clamp_reduce_fusion.1), kind=kLoop, calls=%fused_computation.23 | loop fusion | flops 768 | bytes 2048 | tf_op jit(solution)/shard_map/sub | solution.py:88
  (3 shorter events, 0.0 us)
Async XLA Ops:
  2.0 15.5 %all-to-all-start = ((bf16[32,16,128]{2,1,0:T(8,128)(2,1)}), bf16[32,16,128]{2,1,0:T(8,128)(2,1)S(1)}, u32[]{:S(2)}, u32[]{:S(2)}) async-start(bf16[32,16,128]{2,1,0:T(8,128)(2,1)} %bitcast.18), calls=%async_computation | async-start | bytes 262144 | tf_op jit(solution)/shard_map/all_to_all | solution.py:54

commit v8 on v7

v8 whole, which is shorter than its diff:
```python
import functools

import jax
import jax.numpy as jnp
from jax import lax
from jax.experimental import pallas as pl
from jax.experimental.pallas import tpu as pltpu
from jax.sharding import PartitionSpec as P

WIN = 15
BINS = 256


VALUE_RANGE = 12.8
QUANT_LEVEL = 0.9
SHARPNESS = 32.0
KERNEL_SCALE = 0.25
STEP_SIZE = 2.0


def chunk_kernel(span, cal_own, year_count, region_count, temps_ref, mask_ref, out_ref, stage_ref):
    days_in = temps_ref.shape[0]
    chunk_rows = span + 1
    stage_ref[0:days_in, :] = temps_ref[...].astype(jnp.float32)
    flags = mask_ref[...].astype(jnp.float32)
    stage_ref[days_in : days_in + 1, :] = flags
    is_flag = lax.broadcasted_iota(jnp.int32, (chunk_rows, out_ref.shape[1]), 0) == span
    for year in range(year_count):
        rows = stage_ref[year * cal_own : year * cal_own + chunk_rows, :]
        tile = jnp.where(is_flag, flags, rows).astype(out_ref.dtype)
        for region in range(region_count):
            first = (year * region_count + region) * chunk_rows
            out_ref[first : first + chunk_rows, :] = tile


def gather_windows(temps, flags, span, cal_own):
    year_count, region_count = lax.axis_size("year"), lax.axis_size("region")
    chunk_rows = span + 1
    lon_own = temps.shape[1]
    rows = pl.pallas_call(
        functools.partial(chunk_kernel, span, cal_own, year_count, region_count),
        out_shape=jax.ShapeDtypeStruct((year_count * region_count * chunk_rows, lon_own), temps.dtype),
        scratch_shapes=[pltpu.VMEM((temps.shape[0] + 1, lon_own), jnp.float32)],
    )(temps, flags.reshape(1, lon_own))
    rows = rows.reshape(year_count * region_count, chunk_rows, lon_own)
    return lax.all_to_all(rows, ("year", "region"), 0, 0, tiled=True)


def threshold_kernel(span, cal_own, year_count, region_count, count_all, region_ref, recv_ref, coarse_ref,
                     refined_ref, samples_ref, scaled_ref):
    chunk_rows = span + 1
    lon_own = recv_ref.shape[1]
    width = VALUE_RANGE / BINS
    region = region_ref[0]
    west_region = (region + region_count - 1) % region_count
    east_region = (region + 1) % region_count
    lane = lax.broadcasted_iota(jnp.int32, (chunk_rows, lon_own), 1)

    def block(year, source):
        first = pl.multiple_of((year * region_count + source) * chunk_rows, chunk_rows)
        return recv_ref[pl.ds(first, chunk_rows), :].astype(jnp.float32)

    def neighbours(year):
        center, west, east = block(year, region), block(year, west_region), block(year, east_region)
        to_west = jnp.where(lane == 0, pltpu.roll(west, 1, 1), pltpu.roll(center, 1, 1))
        to_east = jnp.where(lane == lon_own - 1, pltpu.roll(east, lon_own - 1, 1), pltpu.roll(center, lon_own - 1, 1))
        return center, to_west, to_east

    center, to_west, to_east = neighbours(0)
    flag, flag_west, flag_east = center[span:, :], to_west[span:, :], to_east[span:, :]
    same_west = 1.0 - jnp.abs(flag - flag_west)
    same_east = 1.0 - jnp.abs(flag - flag_east)
    norm = 1.0 + same_west + same_east
    for year in range(year_count):
        center, to_west, to_east = neighbours(year)
        mixed = center + same_west * to_west + same_east * to_east
        smooth = (mixed / norm).astype(jnp.bfloat16).astype(jnp.float32)
        samples_ref[year * chunk_rows : (year + 1) * chunk_rows, :] = smooth
    samples_total = year_count * WIN
    upper = lax.broadcasted_iota(jnp.int32, (64, lon_own), 0).astype(jnp.float32) + 1.0
    for j in range(cal_own):
        for year in range(year_count):
            rows = samples_ref[year * chunk_rows + j : year * chunk_rows + j + WIN, :]
            scaled = jnp.clip((rows + 0.5 * VALUE_RANGE) / width, 0.0, BINS - 1.0)
            scaled_ref[year * WIN : (year + 1) * WIN, :] = scaled
        total = jnp.zeros((1, lon_own), jnp.float32)
        for part in range(BINS // 64):
            def add_sample(index, cumulative):
                row = scaled_ref[pl.ds(index, 1), :]
                return cumulative + jnp.clip(upper + float(64 * part) - row, 0.0, 1.0)

            cumulative = lax.fori_loop(0, samples_total, add_sample, jnp.zeros((64, lon_own), jnp.float32))
            ranks = jnp.clip(0.5 + SHARPNESS * (QUANT_LEVEL - cumulative / count_all), 0.0, 1.0)
            total = total + jnp.sum(ranks, axis=0, keepdims=True)
        coarse = -0.5 * VALUE_RANGE + width * total
        cdf = jnp.zeros((1, lon_own), jnp.float32)
        for year in range(year_count):
            rows = samples_ref[year * chunk_rows + j : year * chunk_rows + j + WIN, :]
            kernel = 1.0 / (1.0 + jnp.exp(-((coarse - rows) / KERNEL_SCALE)))
            cdf = cdf + jnp.sum(kernel, axis=0, keepdims=True)
        coarse_ref[j : j + 1, :] = coarse
        refined_ref[j : j + 1, :] = coarse - STEP_SIZE * (cdf / count_all - QUANT_LEVEL)


def shards(daily_temps, land_mask):
    days_in = daily_temps.shape[1]
    lon_own = daily_temps.shape[2]
    year_count = lax.axis_size("year")
    region_count = lax.axis_size("region")
    cal_days = days_in - WIN + 1
    cal_own = cal_days // year_count
    span = WIN + cal_own - 1
    count_all = float(year_count * WIN)
    received = gather_windows(daily_temps[0], land_mask, span, cal_own)
    received = received.reshape(year_count * region_count * (span + 1), lon_own)
    region = lax.axis_index("region").astype(jnp.int32).reshape(1)
    out = jax.ShapeDtypeStruct((cal_own, lon_own), jnp.float32)
    return pl.pallas_call(
        functools.partial(threshold_kernel, span, cal_own, year_count, region_count, count_all),
        out_shape=(out, out),
        in_specs=[pl.BlockSpec(memory_space=pltpu.SMEM), pl.BlockSpec(memory_space=pltpu.VMEM)],
        scratch_shapes=[
            pltpu.VMEM((year_count * (span + 1), lon_own), jnp.float32),
            pltpu.VMEM((year_count * WIN, lon_own), jnp.float32),
        ],
    )(region, received)


def solution(mesh):
    return jax.shard_map(
        shards,
        mesh=mesh,
        in_specs=(P("year", None, "region"), P("region")),
        out_specs=(P("year", "region"), P("year", "region")),
        check_vma=False,
    )
```

time: 20.6 us -> 23.4 us (1.14)
  Pallas kernels: 1.35 us -> 6.3 us
  other arithmetic: 2.63 us -> 0 us
  local copies, waits for them, and re-layouts: 0.2 us -> 0.65 us
    pallas_call x0 -> x1, Pallas kernels: none -> 4.94 us  [shards(): pl.pallas_call(functools.partial(threshold_kernel, span, cal_own, year_co...]
    reduce_sum x3 -> x0, other arithmetic: 1.77 us -> none  [the longest x1 1.66 us: coarse_from_samples(): jnp.sum(jnp.clip(upper[None] - scaled[:, None, :], 0.0, 1.0), axis=0)]
    unnamed x0 -> x2, local copies, waits for them, and re-layouts: none -> 0.65 us
    sub x1 -> x0, other arithmetic: 0.52 us -> none  [shards(): refined = coarse - STEP_SIZE * (cdf / count_all - QUANT_LEVEL)]
where the time goes in v8:
time: 23.4 us; the launch traced here: 23.1 us
  waiting for transfers between devices  8.22 us (35%)
  starting transfers between devices  7.3 us (31%)
  Pallas kernels  6.3 us (27%)
  local copies, waits for them, and re-layouts  0.65 us (3%)
  between operations  0.64 us (3%)
    all_to_all x1, waiting for transfers between devices, gather_windows(): return lax.all_to_all(rows, ('year', 'region'), 0, 0, tiled=True)  8.22 us
    all_to_all x1, starting transfers between devices, gather_windows(): return lax.all_to_all(rows, ('year', 'region'), 0, 0, tiled=True)  7.3 us
    pallas_call x1, Pallas kernels, shards(): pl.pallas_call(functools.partial(threshold_kernel, span, cal_own, year_co...  4.94 us
    pallas_call x1, Pallas kernels, gather_windows(): pl.pallas_call(functools.partial(chunk_kernel, span, cal_own, year_count,...  1.36 us
    unnamed x2, local copies, waits for them, and re-layouts  0.65 us
  transfers between devices with their start and end apart: 1, of which 1 were waited for; matrix products, arithmetic and copies ran while one was open for 0% of the time, Pallas kernels for 0%

profile of v8, /device:TPU:0, one launch (start us, length us, event | category | flops | bytes accessed | tf_op | source)
XLA Modules:
  0.0 23.1 jit_solution(7219424383959848963)
XLA Ops:
  0.6 1.4 %shard_map.41 = bf16[512,128]{1,0:T(8,128)(2,1)} custom-call(bf16[22,128]{1,0:T(8,128)(2,1)} %bitcast.7, s32[1,128]{1,0:T(1,128)} %bitcast.8), custom_call_target="tpu_custom_call" | custom-call | tf_op jit(solution)/shard_map/pallas_call | solution.py:40
  2.0 7.3 %all-to-all-start = ((bf16[32,16,128]{2,1,0:T(8,128)(2,1)}), bf16[32,16,128]{2,1,0:T(8,128)(2,1)S(1)}, u32[]{:S(2)}, u32[]{:S(2)}) async-start(bf16[32,16,128]{2,1,0:T(8,128)(2,1)} %bitcast.6), calls=%async_computation | async-start | bytes 262144 | tf_op jit(solution)/shard_map/all_to_all | solution.py:46
  9.3 8.2 %all-to-all-done = bf16[32,16,128]{2,1,0:T(8,128)(2,1)S(1)} async-done(((bf16[32,16,128]{2,1,0:T(8,128)(2,1)}), bf16[32,16,128]{2,1,0:T(8,128)(2,1)S(1)}, u32[]{:S(2)}, u32[]{:S(2)}) %all-to-all-start) | async-done | bytes 131104 | tf_op jit(solution)/shard_map/all_to_all | solution.py:46
  17.5 0.0 copy-start
  17.5 0.6 %copy-done = bf16[32,16,128]{2,1,0:T(8,128)(2,1)} copy-done((bf16[32,16,128]{2,1,0:T(8,128)(2,1)}, bf16[32,16,128]{2,1,0:T(8,128)(2,1)S(1)}, u32[]{:S(2)}) %copy-start) | copy-done | bytes 131096
  18.2 4.9 %shard_map.42 = (f32[1,128]{1,0:T(1,128)}, f32[1,128]{1,0:T(1,128)}) custom-call(s32[1]{0:T(128)} %bitcast.region_ref, bf16[512,128]{1,0:T(8,128)(2,1)} %bitcast.5), custom_call_target="tpu_custom_call" | custom-call | tf_op jit(solution)/shard_map/pallas_call | solution.py:118
Async XLA Ops:
  2.0 15.5 %all-to-all-start = ((bf16[32,16,128]{2,1,0:T(8,128)(2,1)}), bf16[32,16,128]{2,1,0:T(8,128)(2,1)S(1)}, u32[]{:S(2)}, u32[]{:S(2)}) async-start(bf16[32,16,128]{2,1,0:T(8,128)(2,1)} %bitcast.6), calls=%async_computation | async-start | bytes 262144 | tf_op jit(solution)/shard_map/all_to_all | solution.py:46
  17.5 0.6 %copy-start = (bf16[32,16,128]{2,1,0:T(8,128)(2,1)}, bf16[32,16,128]{2,1,0:T(8,128)(2,1)S(1)}, u32[]{:S(2)}) copy-start(bf16[32,16,128]{2,1,0:T(8,128)(2,1)S(1)} %all-to-all-done) | copy-start | bytes 393220

commit v9 on v7

--- a/solution.py
+++ b/solution.py
@@ -57,8 +57,11 @@
 def coarse_from_samples(samples, count_all, bin_count):
     width = VALUE_RANGE / bin_count
     scaled = jnp.clip((samples + 0.5 * VALUE_RANGE) / width, 0.0, bin_count - 1.0)
-    upper = lax.broadcasted_iota(jnp.float32, (bin_count, 1), 0) + 1.0
-    cumulative = jnp.sum(jnp.clip(upper[None] - scaled[:, None, :], 0.0, 1.0), axis=0)
+    grouped = scaled.reshape(-1, WIN, scaled.shape[-1])
+    points = lax.broadcasted_iota(jnp.float32, (bin_count + 8, 1), 0)
+    partial = jnp.sum(jnp.minimum(grouped[:, :, None, :], points[None, None]), axis=1)
+    floor_sum = jnp.sum(partial, axis=0)
+    cumulative = count_all - (floor_sum[1 : bin_count + 1] - floor_sum[:bin_count])
     ranks = jnp.clip(0.5 + SHARPNESS * (QUANT_LEVEL - cumulative / count_all), 0.0, 1.0)
     return -0.5 * VALUE_RANGE + width * jnp.sum(ranks, axis=0)
 

time: 20.6 us -> 20.3 us (0.985)
  other arithmetic: 2.63 us -> 2.31 us
    reduce_sum x1, other arithmetic: 1.66 us -> 1.34 us  [coarse_from_samples(): floor_sum = jnp.sum(partial, axis=0)]
where the time goes in v9:
time: 20.3 us; the launch traced here: 20 us
  waiting for transfers between devices  8.22 us (40%)
  starting transfers between devices  7.3 us (36%)
  other arithmetic  2.31 us (11%)
  Pallas kernels  1.35 us (7%)
  between operations  0.67 us (3%)
    all_to_all x1, waiting for transfers between devices, gather_windows(): return lax.all_to_all(rows, ('year', 'region'), 0, 0, tiled=True)  8.22 us
    all_to_all x1, starting transfers between devices, gather_windows(): return lax.all_to_all(rows, ('year', 'region'), 0, 0, tiled=True)  7.3 us
    pallas_call x1, Pallas kernels, gather_windows(): pl.pallas_call(functools.partial(chunk_kernel, span, cal_own, year_count,...  1.35 us
    reduce_sum x1, other arithmetic, coarse_from_samples(): floor_sum = jnp.sum(partial, axis=0)  1.34 us
    sub x1, other arithmetic, shards(): refined = coarse - STEP_SIZE * (cdf / count_all - QUANT_LEVEL)  0.52 us
  transfers between devices with their start and end apart: 1, of which 1 were waited for; matrix products, arithmetic and copies ran while one was open for 0% of the time, Pallas kernels for 0%

profile of v9, /device:TPU:0, one launch (start us, length us, event | category | flops | bytes accessed | tf_op | source)
XLA Modules:
  0.0 20.0 jit_solution(3094140618349096738)
XLA Ops:
  0.6 1.3 %shard_map.41 = bf16[512,128]{1,0:T(8,128)(2,1)} custom-call(bf16[22,128]{1,0:T(8,128)(2,1)} %bitcast.20, s32[1,128]{1,0:T(1,128)} %bitcast.22), custom_call_target="tpu_custom_call" | custom-call | tf_op jit(solution)/shard_map/pallas_call | solution.py:48
  2.0 7.3 %all-to-all-start = ((bf16[32,16,128]{2,1,0:T(8,128)(2,1)}), bf16[32,16,128]{2,1,0:T(8,128)(2,1)S(1)}, u32[]{:S(2)}, u32[]{:S(2)}) async-start(bf16[32,16,128]{2,1,0:T(8,128)(2,1)} %bitcast.18), calls=%async_computation | async-start | bytes 262144 | tf_op jit(solution)/shard_map/all_to_all | solution.py:54
  9.3 8.2 %all-to-all-done = bf16[32,16,128]{2,1,0:T(8,128)(2,1)S(1)} async-done(((bf16[32,16,128]{2,1,0:T(8,128)(2,1)}), bf16[32,16,128]{2,1,0:T(8,128)(2,1)S(1)}, u32[]{:S(2)}, u32[]{:S(2)}) %all-to-all-start) | async-done | bytes 131104 | tf_op jit(solution)/shard_map/all_to_all | solution.py:54
  17.5 0.1 copy.7
  17.6 0.1 reshape.73
  17.6 0.1 fusion.22
  17.7 0.1 fusion.9
  17.9 0.1 add_bitcast_fusion
  17.9 0.1 multiply_clamp_fusion
  18.1 1.3 %minimum_reduce_fusion = f32[264,128]{1,0:T(8,128)S(1)} fusion(f32[8,15,128]{2,1,0:T(8,128)S(1)} %get-tuple-element.4), kind=kLoop, calls=%fused_computation | loop fusion | flops 8076288 | bytes 196608 | tf_op jit(solution)/shard_map/reduce_sum | solution.py:63
  19.4 0.1 fusion.6
  19.5 0.1 fusion.14
  19.5 0.5 %bitcast_subtract_fusion = (f32[1,128]{1,0:T(1,128)}, f32[1,128]{1,0:T(1,128)}) fusion(f32[128]{0:T(128)S(1)} %fusion.14, f32[128]{0:T(128)S(1)} %fusion.6), kind=kLoop, calls=%fused_computation.29 | loop fusion | flops 768 | bytes 2048 | tf_op jit(solution)/shard_map/sub | solution.py:91
  (1 shorter events, 0.0 us)
Async XLA Ops:
  2.0 15.5 %all-to-all-start = ((bf16[32,16,128]{2,1,0:T(8,128)(2,1)}), bf16[32,16,128]{2,1,0:T(8,128)(2,1)S(1)}, u32[]{:S(2)}, u32[]{:S(2)}) async-start(bf16[32,16,128]{2,1,0:T(8,128)(2,1)} %bitcast.18), calls=%async_computation | async-start | bytes 262144 | tf_op jit(solution)/shard_map/all_to_all | solution.py:54

commit v10 on v9

--- a/solution.py
+++ b/solution.py
@@ -37,7 +37,7 @@
         rows = stage_ref[year * cal_own : year * cal_own + chunk_rows, :]
         tile = jnp.where(is_flag, flags, rows).astype(out_ref.dtype)
         for region in range(region_count):
-            first = (year * region_count + region) * chunk_rows
+            first = (region * year_count + year) * chunk_rows
             out_ref[first : first + chunk_rows, :] = tile
 
 
@@ -51,7 +51,7 @@
         scratch_shapes=[pltpu.VMEM((temps.shape[0] + 1, lon_own), jnp.float32)],
     )(temps, flags.reshape(1, lon_own))
     rows = rows.reshape(year_count * region_count, chunk_rows, lon_own)
-    return lax.all_to_all(rows, ("year", "region"), 0, 0, tiled=True)
+    return lax.all_to_all(rows, ("region", "year"), 0, 0, tiled=True)
 
 
 def coarse_from_samples(samples, count_all, bin_count):
@@ -76,8 +76,8 @@
     span = WIN + cal_own - 1
     count_all = float(year_count * WIN)
     received = gather_windows(daily_temps[0], land_mask, span, cal_own)
-    received = received.reshape(year_count, region_count, span + 1, lon_own)
-    row = jnp.moveaxis(received, 1, 2).reshape(year_count, span + 1, region_count * lon_own)
+    received = received.reshape(region_count, year_count, span + 1, lon_own)
+    row = jnp.transpose(received, (1, 2, 0, 3)).reshape(year_count, span + 1, region_count * lon_own)
     ring = jnp.concatenate([row[..., -1:], row, row[..., :1]], axis=-1)
     extended = lax.dynamic_slice_in_dim(ring, lax.axis_index("region") * lon_own, lon_own + 2, axis=2)
     extended = extended.astype(jnp.float32)

time: 20.3 us -> 19.8 us (0.975)
  waiting for transfers between devices: 8.22 us -> 7.73 us
    all_to_all x1, waiting for transfers between devices: 8.22 us -> 7.73 us  [gather_windows(): return lax.all_to_all(rows, ('region', 'year'), 0, 0, tiled=True)]
where the time goes in v10:
time: 19.8 us; the launch traced here: 19.6 us
  waiting for transfers between devices  7.73 us (39%)
  starting transfers between devices  7.3 us (37%)
  other arithmetic  2.31 us (12%)
  Pallas kernels  1.35 us (7%)
  between operations  0.66 us (3%)
  local copies, waits for them, and re-layouts  0.25 us (1%)
    all_to_all x1, waiting for transfers between devices, gather_windows(): return lax.all_to_all(rows, ('region', 'year'), 0, 0, tiled=True)  7.73 us
    all_to_all x1, starting transfers between devices, gather_windows(): return lax.all_to_all(rows, ('region', 'year'), 0, 0, tiled=True)  7.3 us
    pallas_call x1, Pallas kernels, gather_windows(): pl.pallas_call(functools.partial(chunk_kernel, span, cal_own, year_count,...  1.35 us
    reduce_sum x1, other arithmetic, coarse_from_samples(): floor_sum = jnp.sum(partial, axis=0)  1.34 us
    sub x1, other arithmetic, shards(): refined = coarse - STEP_SIZE * (cdf / count_all - QUANT_LEVEL)  0.52 us
  transfers between devices with their start and end apart: 1, of which 1 were waited for; matrix products, arithmetic and copies ran while one was open for 0% of the time, Pallas kernels for 0%

profile of v10, /device:TPU:0, one launch (start us, length us, event | category | flops | bytes accessed | tf_op | source)
XLA Modules:
  0.0 19.6 jit_solution(15010680387379459237)
XLA Ops:
  0.6 1.3 %shard_map.41 = bf16[512,128]{1,0:T(8,128)(2,1)} custom-call(bf16[22,128]{1,0:T(8,128)(2,1)} %bitcast.20, s32[1,128]{1,0:T(1,128)} %bitcast.22), custom_call_target="tpu_custom_call" | custom-call | tf_op jit(solution)/shard_map/pallas_call | solution.py:48
  2.0 7.3 %all-to-all-start = ((bf16[32,16,128]{2,1,0:T(8,128)(2,1)}), bf16[32,16,128]{2,1,0:T(8,128)(2,1)S(1)}, u32[]{:S(2)}, u32[]{:S(2)}) async-start(bf16[32,16,128]{2,1,0:T(8,128)(2,1)} %bitcast.18), calls=%async_computation | async-start | bytes 262144 | tf_op jit(solution)/shard_map/all_to_all | solution.py:54
  9.3 7.7 %all-to-all-done = bf16[32,16,128]{2,1,0:T(8,128)(2,1)S(1)} async-done(((bf16[32,16,128]{2,1,0:T(8,128)(2,1)}), bf16[32,16,128]{2,1,0:T(8,128)(2,1)S(1)}, u32[]{:S(2)}, u32[]{:S(2)}) %all-to-all-start) | async-done | bytes 131104 | tf_op jit(solution)/shard_map/all_to_all | solution.py:54
  17.0 0.1 copy.7
  17.1 0.1 reshape.73
  17.2 0.1 fusion.22
  17.3 0.1 fusion.9
  17.4 0.1 add_bitcast_fusion
  17.5 0.1 multiply_clamp_fusion
  17.6 1.3 %minimum_reduce_fusion = f32[264,128]{1,0:T(8,128)S(1)} fusion(f32[8,15,128]{2,1,0:T(8,128)S(1)} %get-tuple-element.4), kind=kLoop, calls=%fused_computation | loop fusion | flops 8076288 | bytes 196608 | tf_op jit(solution)/shard_map/reduce_sum | solution.py:63
  19.0 0.1 fusion.6
  19.0 0.1 fusion.14
  19.1 0.5 %bitcast_subtract_fusion = (f32[1,128]{1,0:T(1,128)}, f32[1,128]{1,0:T(1,128)}) fusion(f32[128]{0:T(128)S(1)} %fusion.14, f32[128]{0:T(128)S(1)} %fusion.6), kind=kLoop, calls=%fused_computation.29 | loop fusion | flops 768 | bytes 2048 | tf_op jit(solution)/shard_map/sub | solution.py:91
  (1 shorter events, 0.0 us)
Async XLA Ops:
  2.0 15.0 %all-to-all-start = ((bf16[32,16,128]{2,1,0:T(8,128)(2,1)}), bf16[32,16,128]{2,1,0:T(8,128)(2,1)S(1)}, u32[]{:S(2)}, u32[]{:S(2)}) async-start(bf16[32,16,128]{2,1,0:T(8,128)(2,1)} %bitcast.18), calls=%async_computation | async-start | bytes 262144 | tf_op jit(solution)/shard_map/all_to_all | solution.py:54

commit v11 on v10

--- a/solution.py
+++ b/solution.py
@@ -77,9 +77,11 @@
     count_all = float(year_count * WIN)
     received = gather_windows(daily_temps[0], land_mask, span, cal_own)
     received = received.reshape(region_count, year_count, span + 1, lon_own)
-    row = jnp.transpose(received, (1, 2, 0, 3)).reshape(year_count, span + 1, region_count * lon_own)
-    ring = jnp.concatenate([row[..., -1:], row, row[..., :1]], axis=-1)
-    extended = lax.dynamic_slice_in_dim(ring, lax.axis_index("region") * lon_own, lon_own + 2, axis=2)
+    region = lax.axis_index("region")
+    center = lax.dynamic_index_in_dim(received, region, 0, keepdims=False)
+    west = lax.dynamic_index_in_dim(received, lax.rem(region + region_count - 1, region_count), 0, keepdims=False)
+    east = lax.dynamic_index_in_dim(received, lax.rem(region + 1, region_count), 0, keepdims=False)
+    extended = jnp.concatenate([west[..., -1:], center, east[..., :1]], axis=-1)
     extended = extended.astype(jnp.float32)
     every_year = smooth_field(extended[:, :span], extended[0, span])
     coarse_rows = []

time: 19.8 us -> 19.7 us (level)
  no operation moved by 1% of the time
where the time goes in v11:
time: 19.7 us; the launch traced here: 19.5 us
  waiting for transfers between devices  7.72 us (39%)
  starting transfers between devices  7.3 us (37%)
  other arithmetic  2.35 us (12%)
  Pallas kernels  1.35 us (7%)
  between operations  0.67 us (3%)
    all_to_all x1, waiting for transfers between devices, gather_windows(): return lax.all_to_all(rows, ('region', 'year'), 0, 0, tiled=True)  7.72 us
    all_to_all x1, starting transfers between devices, gather_windows(): return lax.all_to_all(rows, ('region', 'year'), 0, 0, tiled=True)  7.3 us
    pallas_call x1, Pallas kernels, gather_windows(): pl.pallas_call(functools.partial(chunk_kernel, span, cal_own, year_count,...  1.35 us
    reduce_sum x1, other arithmetic, coarse_from_samples(): floor_sum = jnp.sum(partial, axis=0)  1.34 us
    sub x1, other arithmetic, shards(): refined = coarse - STEP_SIZE * (cdf / count_all - QUANT_LEVEL)  0.52 us
  transfers between devices with their start and end apart: 1, of which 1 were waited for; matrix products, arithmetic and copies ran while one was open for 0% of the time, Pallas kernels for 0%

profile of v11, /device:TPU:0, one launch (start us, length us, event | category | flops | bytes accessed | tf_op | source)
XLA Modules:
  0.0 19.5 jit_solution(10876886910373157448)
XLA Ops:
  0.6 1.3 %shard_map.41 = bf16[512,128]{1,0:T(8,128)(2,1)} custom-call(bf16[22,128]{1,0:T(8,128)(2,1)} %bitcast.26, s32[1,128]{1,0:T(1,128)} %bitcast.28), custom_call_target="tpu_custom_call" | custom-call | tf_op jit(solution)/shard_map/pallas_call | solution.py:48
  2.0 7.3 %all-to-all-start = ((bf16[32,16,128]{2,1,0:T(8,128)(2,1)}), bf16[32,16,128]{2,1,0:T(8,128)(2,1)S(1)}, u32[]{:S(2)}, u32[]{:S(2)}) async-start(bf16[32,16,128]{2,1,0:T(8,128)(2,1)} %bitcast.24), calls=%async_computation | async-start | bytes 262144 | tf_op jit(solution)/shard_map/all_to_all | solution.py:54
  9.3 7.7 %all-to-all-done = bf16[32,16,128]{2,1,0:T(8,128)(2,1)S(1)} async-done(((bf16[32,16,128]{2,1,0:T(8,128)(2,1)}), bf16[32,16,128]{2,1,0:T(8,128)(2,1)S(1)}, u32[]{:S(2)}, u32[]{:S(2)}) %all-to-all-start) | async-done | bytes 131104 | tf_op jit(solution)/shard_map/all_to_all | solution.py:54
  17.0 0.1 slice.52
  17.1 0.1 subtract_bitcast_fusion
  17.2 0.1 maximum_convert_fusion
  17.3 0.1 add_bitcast_fusion
  17.4 0.1 multiply_clamp_fusion
  17.5 1.3 %minimum_reduce_fusion = f32[264,128]{1,0:T(8,128)S(1)} fusion(f32[8,15,128]{2,1,0:T(8,128)S(1)} %get-tuple-element.4), kind=kLoop, calls=%fused_computation | loop fusion | flops 8076288 | bytes 196608 | tf_op jit(solution)/shard_map/reduce_sum | solution.py:63
  18.8 0.1 fusion.6
  18.9 0.1 fusion.11
  19.0 0.5 %bitcast_subtract_fusion = (f32[1,128]{1,0:T(1,128)}, f32[1,128]{1,0:T(1,128)}) fusion(f32[128]{0:T(128)S(1)} %fusion.11, f32[128]{0:T(128)S(1)} %fusion.6), kind=kLoop, calls=%fused_computation.29 | loop fusion | flops 768 | bytes 2048 | tf_op jit(solution)/shard_map/sub | solution.py:93
  (2 shorter events, 0.0 us)
Async XLA Ops:
  2.0 15.0 %all-to-all-start = ((bf16[32,16,128]{2,1,0:T(8,128)(2,1)}), bf16[32,16,128]{2,1,0:T(8,128)(2,1)S(1)}, u32[]{:S(2)}, u32[]{:S(2)}) async-start(bf16[32,16,128]{2,1,0:T(8,128)(2,1)} %bitcast.24), calls=%async_computation | async-start | bytes 262144 | tf_op jit(solution)/shard_map/all_to_all | solution.py:54

commit v12 on v11

--- a/solution.py
+++ b/solution.py
@@ -26,32 +26,13 @@
     return lax.reduce_precision(mixed / (1.0 + same_west + same_east), exponent_bits=8, mantissa_bits=7)
 
 
-def chunk_kernel(span, cal_own, year_count, region_count, temps_ref, mask_ref, out_ref, stage_ref):
-    days_in = temps_ref.shape[0]
-    chunk_rows = span + 1
-    stage_ref[0:days_in, :] = temps_ref[...].astype(jnp.float32)
-    flags = mask_ref[...].astype(jnp.float32)
-    stage_ref[days_in : days_in + 1, :] = flags
-    is_flag = lax.broadcasted_iota(jnp.int32, (chunk_rows, out_ref.shape[1]), 0) == span
-    for year in range(year_count):
-        rows = stage_ref[year * cal_own : year * cal_own + chunk_rows, :]
-        tile = jnp.where(is_flag, flags, rows).astype(out_ref.dtype)
-        for region in range(region_count):
-            first = (region * year_count + year) * chunk_rows
-            out_ref[first : first + chunk_rows, :] = tile
-
-
-def gather_windows(temps, flags, span, cal_own):
+def gather_blocks(temps, flags):
     year_count, region_count = lax.axis_size("year"), lax.axis_size("region")
-    chunk_rows = span + 1
-    lon_own = temps.shape[1]
-    rows = pl.pallas_call(
-        functools.partial(chunk_kernel, span, cal_own, year_count, region_count),
-        out_shape=jax.ShapeDtypeStruct((year_count * region_count * chunk_rows, lon_own), temps.dtype),
-        scratch_shapes=[pltpu.VMEM((temps.shape[0] + 1, lon_own), jnp.float32)],
-    )(temps, flags.reshape(1, lon_own))
-    rows = rows.reshape(year_count * region_count, chunk_rows, lon_own)
-    return lax.all_to_all(rows, ("region", "year"), 0, 0, tiled=True)
+    days_in, lon_own = temps.shape
+    row = lax.broadcasted_iota(jnp.int32, (days_in + 1, lon_own), 0)
+    block = jnp.where(row == days_in, flags.astype(temps.dtype)[None, :], jnp.pad(temps, ((0, 1), (0, 0))))
+    tiled = jnp.broadcast_to(block[None], (region_count * year_count, days_in + 1, lon_own))
+    return lax.all_to_all(tiled, ("region", "year"), 0, 0, tiled=True)
 
 
 def coarse_from_samples(samples, count_all, bin_count):
@@ -75,12 +56,19 @@
     cal_own = cal_days // year_count
     span = WIN + cal_own - 1
     count_all = float(year_count * WIN)
-    received = gather_windows(daily_temps[0], land_mask, span, cal_own)
-    received = received.reshape(region_count, year_count, span + 1, lon_own)
+    received = gather_blocks(daily_temps[0], land_mask)
+    received = received.reshape(region_count, year_count, days_in + 1, lon_own)
     region = lax.axis_index("region")
-    center = lax.dynamic_index_in_dim(received, region, 0, keepdims=False)
-    west = lax.dynamic_index_in_dim(received, lax.rem(region + region_count - 1, region_count), 0, keepdims=False)
-    east = lax.dynamic_index_in_dim(received, lax.rem(region + 1, region_count), 0, keepdims=False)
+    first_day = lax.axis_index("year") * cal_own
+
+    def window(index):
+        picked = lax.dynamic_index_in_dim(received, index, 0, keepdims=False)
+        days = lax.dynamic_slice_in_dim(picked, first_day, span, axis=1)
+        return jnp.concatenate([days, picked[:, days_in:]], axis=1)
+
+    center = window(region)
+    west = window(lax.rem(region + region_count - 1, region_count))
+    east = window(lax.rem(region + 1, region_count))
     extended = jnp.concatenate([west[..., -1:], center, east[..., :1]], axis=-1)
     extended = extended.astype(jnp.float32)
     every_year = smooth_field(extended[:, :span], extended[0, span])

time: 19.7 us -> 21.4 us (1.086)
  other arithmetic: 2.35 us -> 3.82 us
  Pallas kernels: 1.35 us -> 0 us
  waiting for transfers between devices: 7.72 us -> 8.53 us
  local copies, waits for them, and re-layouts: 0.09 us -> 0.79 us
    pallas_call x1 -> x0, Pallas kernels: 1.35 us -> none  [gather_windows(): pl.pallas_call(functools.partial(chunk_kernel, span, cal_own, year_count,...]
    all_to_all x1, waiting for transfers between devices: 7.72 us -> 8.53 us  [gather_blocks(): return lax.all_to_all(tiled, ('region', 'year'), 0, 0, tiled=True)]
    select_n x0 -> x1, other arithmetic: none -> 0.76 us  [gather_blocks(): jnp.where(row == days_in, flags.astype(temps.dtype)[None, :], jnp.pad(tem...]
    broadcast_in_dim x0 -> x1, local copies, waits for them, and re-layouts: none -> 0.7 us  [gather_blocks(): jnp.broadcast_to(block[None], (region_count * year_count, days_in + 1, lo...]
    convert_element_type x0 -> x1, other arithmetic: none -> 0.66 us  [gather_blocks(): flags.astype(temps.dtype)[None, :]]
where the time goes in v12:
time: 21.4 us; the launch traced here: 21.2 us
  waiting for transfers between devices  8.53 us (40%)
  starting transfers between devices  7.3 us (34%)
  other arithmetic  3.82 us (18%)
  local copies, waits for them, and re-layouts  0.79 us (4%)
  between operations  0.72 us (3%)
    all_to_all x1, waiting for transfers between devices, gather_blocks(): return lax.all_to_all(tiled, ('region', 'year'), 0, 0, tiled=True)  8.53 us
    all_to_all x1, starting transfers between devices, gather_blocks(): return lax.all_to_all(tiled, ('region', 'year'), 0, 0, tiled=True)  7.3 us
    reduce_sum x1, other arithmetic, coarse_from_samples(): floor_sum = jnp.sum(partial, axis=0)  1.34 us
    select_n x1, other arithmetic, gather_blocks(): jnp.where(row == days_in, flags.astype(temps.dtype)[None, :], jnp.pad(tem...  0.76 us
    broadcast_in_dim x1, local copies, waits for them, and re-layouts, gather_blocks(): jnp.broadcast_to(block[None], (region_count * year_count, days_in + 1, lo...  0.7 us
    convert_element_type x1, other arithmetic, gather_blocks(): flags.astype(temps.dtype)[None, :]  0.66 us
    sub x1, other arithmetic, shards(): refined = coarse - STEP_SIZE * (cdf / count_all - QUANT_LEVEL)  0.52 us
  transfers between devices with their start and end apart: 1, of which 1 were waited for; matrix products, arithmetic and copies ran while one was open for 0% of the time, Pallas kernels for 0%

profile of v12, /device:TPU:0, one launch (start us, length us, event | category | flops | bytes accessed | tf_op | source)
XLA Modules:
  0.0 21.2 jit_solution(11364879218230071058)
XLA Ops:
  0.6 0.7 %convert_element_type.8 = bf16[128]{0:T(256)(128)(2,1)S(1)} convert(s32[128]{0:T(128)} %param.3) | non-fusion elementwise | flops 128 | bytes 768 | tf_op jit(solution)/shard_map/convert_element_type | solution.py:33
  1.3 0.8 %pad_select_fusion = bf16[23,128]{1,0:T(8,128)(2,1)S(1)} fusion(bf16[22,128]{1,0:T(8,128)(2,1)} %bitcast.26, pred[23]{0:T(512)(128)(4,1)S(1)} %iota_compare_fusion, bf16[128]{0:T(256)(128)(2,1)S(1)} %convert_element_type.8), kind=kLoop, calls=%fused_computation.29 | loop fusion | flops 2944 | bytes 11799 | tf_op jit(solution)/shard_map/jit(_where)/select_n | solution.py:33
  2.1 0.7 %broadcast_in_dim.11 = bf16[32,23,128]{2,1,0:T(8,128)(2,1)} broadcast(bf16[23,128]{1,0:T(8,128)(2,1)S(1)} %pad_select_fusion), dimensions={1,2} | broadcast | bytes 194304 | tf_op jit(solution)/shard_map/broadcast_in_dim | solution.py:34
  2.8 7.3 %all-to-all-start = ((bf16[32,23,128]{2,1,0:T(8,128)(2,1)}), bf16[32,23,128]{2,1,0:T(8,128)(2,1)S(1)}, u32[]{:S(2)}, u32[]{:S(2)}) async-start(bf16[32,23,128]{2,1,0:T(8,128)(2,1)} %broadcast_in_dim.11), calls=%async_computation | async-start | bytes 393216 | tf_op jit(solution)/shard_map/all_to_all | solution.py:35
  10.1 8.5 %all-to-all-done = bf16[32,23,128]{2,1,0:T(8,128)(2,1)S(1)} async-done(((bf16[32,23,128]{2,1,0:T(8,128)(2,1)}), bf16[32,23,128]{2,1,0:T(8,128)(2,1)S(1)}, u32[]{:S(2)}, u32[]{:S(2)}) %all-to-all-start) | async-done | bytes 188448 | tf_op jit(solution)/shard_map/all_to_all | solution.py:35
  18.7 0.1 subtract_bitcast_fusion
  18.8 0.1 fusion.12
  19.0 0.1 add_bitcast_fusion
  19.1 0.1 multiply_clamp_fusion
  19.2 1.3 %minimum_reduce_fusion = f32[264,128]{1,0:T(8,128)S(1)} fusion(f32[8,15,128]{2,1,0:T(8,128)S(1)} %get-tuple-element.4), kind=kLoop, calls=%fused_computation | loop fusion | flops 8076288 | bytes 196608 | tf_op jit(solution)/shard_map/reduce_sum | solution.py:44
  20.5 0.1 fusion.6
  20.6 0.1 fusion.14
  20.6 0.5 %bitcast_subtract_fusion = (f32[1,128]{1,0:T(1,128)}, f32[1,128]{1,0:T(1,128)}) fusion(f32[128]{0:T(128)S(1)} %fusion.14, f32[128]{0:T(128)S(1)} %fusion.6), kind=kLoop, calls=%fused_computation.38 | loop fusion | flops 768 | bytes 2048 | tf_op jit(solution)/shard_map/sub | solution.py:81
  (7 shorter events, 0.1 us)
Async XLA Ops:
  2.8 15.9 %all-to-all-start = ((bf16[32,23,128]{2,1,0:T(8,128)(2,1)}), bf16[32,23,128]{2,1,0:T(8,128)(2,1)S(1)}, u32[]{:S(2)}, u32[]{:S(2)}) async-start(bf16[32,23,128]{2,1,0:T(8,128)(2,1)} %broadcast_in_dim.11), calls=%async_computation | async-start | bytes 393216 | tf_op jit(solution)/shard_map/all_to_all | solution.py:35

commit v13 on v11

--- a/solution.py
+++ b/solution.py
@@ -16,14 +16,6 @@
 SHARPNESS = 32.0
 KERNEL_SCALE = 0.25
 STEP_SIZE = 2.0
-
-
-def smooth_field(extended, flags):
-    center = extended[..., 1:-1]
-    same_west = 1.0 - jnp.abs(flags[1:-1] - flags[:-2])
-    same_east = 1.0 - jnp.abs(flags[1:-1] - flags[2:])
-    mixed = center + same_west * extended[..., :-2] + same_east * extended[..., 2:]
-    return lax.reduce_precision(mixed / (1.0 + same_west + same_east), exponent_bits=8, mantissa_bits=7)
 
 
 def chunk_kernel(span, cal_own, year_count, region_count, temps_ref, mask_ref, out_ref, stage_ref):
@@ -81,9 +73,13 @@
     center = lax.dynamic_index_in_dim(received, region, 0, keepdims=False)
     west = lax.dynamic_index_in_dim(received, lax.rem(region + region_count - 1, region_count), 0, keepdims=False)
     east = lax.dynamic_index_in_dim(received, lax.rem(region + 1, region_count), 0, keepdims=False)
-    extended = jnp.concatenate([west[..., -1:], center, east[..., :1]], axis=-1)
-    extended = extended.astype(jnp.float32)
-    every_year = smooth_field(extended[:, :span], extended[0, span])
+    center = center.astype(jnp.float32)
+    to_west = jnp.concatenate([west[..., -1:].astype(jnp.float32), center[..., :-1]], axis=-1)
+    to_east = jnp.concatenate([center[..., 1:], east[..., :1].astype(jnp.float32)], axis=-1)
+    same_west = 1.0 - jnp.abs(center[0, span] - to_west[0, span])
+    same_east = 1.0 - jnp.abs(center[0, span] - to_east[0, span])
+    mixed = center[:, :span] + same_west * to_west[:, :span] + same_east * to_east[:, :span]
+    every_year = lax.reduce_precision(mixed / (1.0 + same_west + same_east), exponent_bits=8, mantissa_bits=7)
     coarse_rows = []
     refined_rows = []
     for j in range(cal_own):

time: 19.7 us -> 19.7 us (level)
  no operation moved by 1% of the time
where the time goes in v13:
time: 19.7 us; the launch traced here: 19.5 us
  waiting for transfers between devices  7.72 us (39%)
  starting transfers between devices  7.3 us (37%)
  other arithmetic  2.35 us (12%)
  Pallas kernels  1.36 us (7%)
  between operations  0.67 us (3%)
    all_to_all x1, waiting for transfers between devices, gather_windows(): return lax.all_to_all(rows, ('region', 'year'), 0, 0, tiled=True)  7.72 us
    all_to_all x1, starting transfers between devices, gather_windows(): return lax.all_to_all(rows, ('region', 'year'), 0, 0, tiled=True)  7.3 us
    pallas_call x1, Pallas kernels, gather_windows(): pl.pallas_call(functools.partial(chunk_kernel, span, cal_own, year_count,...  1.36 us
    reduce_sum x1, other arithmetic, coarse_from_samples(): floor_sum = jnp.sum(partial, axis=0)  1.34 us
    sub x1, other arithmetic, shards(): refined = coarse - STEP_SIZE * (cdf / count_all - QUANT_LEVEL)  0.52 us
  transfers between devices with their start and end apart: 1, of which 1 were waited for; matrix products, arithmetic and copies ran while one was open for 0% of the time, Pallas kernels for 0%

profile of v13, /device:TPU:0, one launch (start us, length us, event | category | flops | bytes accessed | tf_op | source)
XLA Modules:
  0.0 19.5 jit_solution(1175567118498675021)
XLA Ops:
  0.6 1.4 %shard_map.41 = bf16[512,128]{1,0:T(8,128)(2,1)} custom-call(bf16[22,128]{1,0:T(8,128)(2,1)} %bitcast.23, s32[1,128]{1,0:T(1,128)} %bitcast.25), custom_call_target="tpu_custom_call" | custom-call | tf_op jit(solution)/shard_map/pallas_call | solution.py:40
  2.0 7.3 %all-to-all-start = ((bf16[32,16,128]{2,1,0:T(8,128)(2,1)}), bf16[32,16,128]{2,1,0:T(8,128)(2,1)S(1)}, u32[]{:S(2)}, u32[]{:S(2)}) async-start(bf16[32,16,128]{2,1,0:T(8,128)(2,1)} %bitcast.21), calls=%async_computation | async-start | bytes 262144 | tf_op jit(solution)/shard_map/all_to_all | solution.py:46
  9.3 7.7 %all-to-all-done = bf16[32,16,128]{2,1,0:T(8,128)(2,1)S(1)} async-done(((bf16[32,16,128]{2,1,0:T(8,128)(2,1)}), bf16[32,16,128]{2,1,0:T(8,128)(2,1)S(1)}, u32[]{:S(2)}, u32[]{:S(2)}) %all-to-all-start) | async-done | bytes 131104 | tf_op jit(solution)/shard_map/all_to_all | solution.py:46
  17.0 0.1 fusion.22
  17.1 0.1 slice_convert_fusion
  17.2 0.1 subtract_bitcast_fusion
  17.3 0.1 add_bitcast_fusion
  17.4 0.1 multiply_clamp_fusion
  17.5 1.3 %minimum_reduce_fusion = f32[264,128]{1,0:T(8,128)S(1)} fusion(f32[8,15,128]{2,1,0:T(8,128)S(1)} %get-tuple-element.4), kind=kLoop, calls=%fused_computation | loop fusion | flops 8076288 | bytes 196608 | tf_op jit(solution)/shard_map/reduce_sum | solution.py:55
  18.8 0.1 fusion.6
  18.9 0.1 fusion.13
  19.0 0.5 %bitcast_subtract_fusion = (f32[1,128]{1,0:T(1,128)}, f32[1,128]{1,0:T(1,128)}) fusion(f32[128]{0:T(128)S(1)} %fusion.13, f32[128]{0:T(128)S(1)} %fusion.6), kind=kLoop, calls=%fused_computation.29 | loop fusion | flops 768 | bytes 2048 | tf_op jit(solution)/shard_map/sub | solution.py:89
  (2 shorter events, 0.0 us)
Async XLA Ops:
  2.0 15.0 %all-to-all-start = ((bf16[32,16,128]{2,1,0:T(8,128)(2,1)}), bf16[32,16,128]{2,1,0:T(8,128)(2,1)S(1)}, u32[]{:S(2)}, u32[]{:S(2)}) async-start(bf16[32,16,128]{2,1,0:T(8,128)(2,1)} %bitcast.21), calls=%async_computation | async-start | bytes 262144 | tf_op jit(solution)/shard_map/all_to_all | solution.py:46

commit v14 on v8

v14 whole, which is shorter than its diff:
```python
import functools

import jax
import jax.numpy as jnp
from jax import lax
from jax.experimental import pallas as pl
from jax.experimental.pallas import tpu as pltpu
from jax.sharding import PartitionSpec as P

WIN = 15
BINS = 256


VALUE_RANGE = 12.8
QUANT_LEVEL = 0.9
SHARPNESS = 32.0
KERNEL_SCALE = 0.25
STEP_SIZE = 2.0


def chunk_kernel(span, cal_own, year_count, region_count, temps_ref, mask_ref, out_ref, stage_ref):
    days_in = temps_ref.shape[0]
    chunk_rows = span + 1
    stage_ref[0:days_in, :] = temps_ref[...].astype(jnp.float32)
    flags = mask_ref[...].astype(jnp.float32)
    stage_ref[days_in : days_in + 1, :] = flags
    is_flag = lax.broadcasted_iota(jnp.int32, (chunk_rows, out_ref.shape[1]), 0) == span
    for year in range(year_count):
        rows = stage_ref[year * cal_own : year * cal_own + chunk_rows, :]
        tile = jnp.where(is_flag, flags, rows).astype(out_ref.dtype)
        for region in range(region_count):
            first = (region * year_count + year) * chunk_rows
            out_ref[first : first + chunk_rows, :] = tile


def gather_windows(temps, flags, span, cal_own):
    year_count, region_count = lax.axis_size("year"), lax.axis_size("region")
    chunk_rows = span + 1
    lon_own = temps.shape[1]
    rows = pl.pallas_call(
        functools.partial(chunk_kernel, span, cal_own, year_count, region_count),
        out_shape=jax.ShapeDtypeStruct((year_count * region_count * chunk_rows, lon_own), temps.dtype),
        scratch_shapes=[pltpu.VMEM((temps.shape[0] + 1, lon_own), jnp.float32)],
    )(temps, flags.reshape(1, lon_own))
    rows = rows.reshape(year_count * region_count, chunk_rows, lon_own)
    return lax.all_to_all(rows, ("region", "year"), 0, 0, tiled=True)


def coarse_from_samples(samples, count_all, bin_count):
    width = VALUE_RANGE / bin_count
    scaled = jnp.clip((samples + 0.5 * VALUE_RANGE) / width, 0.0, bin_count - 1.0)
    grouped = scaled.reshape(-1, WIN, scaled.shape[-1])
    points = lax.broadcasted_iota(jnp.float32, (bin_count + 8, 1), 0)
    partial = jnp.sum(jnp.minimum(grouped[:, :, None, :], points[None, None]), axis=1)
    floor_sum = jnp.sum(partial, axis=0)
    cumulative = count_all - (floor_sum[1 : bin_count + 1] - floor_sum[:bin_count])
    ranks = jnp.clip(0.5 + SHARPNESS * (QUANT_LEVEL - cumulative / count_all), 0.0, 1.0)
    return -0.5 * VALUE_RANGE + width * jnp.sum(ranks, axis=0)


def threshold_kernel(span, cal_own, year_count, region_count, count_all, region_ref, recv_ref, coarse_ref,
                     refined_ref, blocks_ref, samples_ref, scaled_ref, floor_ref, sems):
    chunk_rows = span + 1
    rows_per_region = year_count * chunk_rows
    lon_own = recv_ref.shape[1]
    width = VALUE_RANGE / BINS
    region = region_ref[0]
    sources = (region, lax.rem(region + region_count - 1, region_count), lax.rem(region + 1, region_count))
    copies = []
    for slot, source in enumerate(sources):
        first = pl.multiple_of(source * rows_per_region, chunk_rows)
        copy = pltpu.make_async_copy(recv_ref.at[pl.ds(first, rows_per_region)], blocks_ref.at[slot], sems.at[slot])
        copy.start()
        copies.append(copy)
    for copy in copies:
        copy.wait()
    lane = lax.broadcasted_iota(jnp.int32, (chunk_rows, lon_own), 1)

    def neighbours(year):
        rows = slice(year * chunk_rows, (year + 1) * chunk_rows)
        center = blocks_ref[0, rows, :].astype(jnp.float32)
        west = blocks_ref[1, rows, :].astype(jnp.float32)
        east = blocks_ref[2, rows, :].astype(jnp.float32)
        to_west = jnp.where(lane == 0, pltpu.roll(west, 1, 1), pltpu.roll(center, 1, 1))
        to_east = jnp.where(lane == lon_own - 1, pltpu.roll(east, lon_own - 1, 1), pltpu.roll(center, lon_own - 1, 1))
        return center, to_west, to_east

    center, to_west, to_east = neighbours(0)
    flag = center[span:, :]
    same_west = 1.0 - jnp.abs(flag - to_west[span:, :])
    same_east = 1.0 - jnp.abs(flag - to_east[span:, :])
    norm = 1.0 + same_west + same_east
    for year in range(year_count):
        center, to_west, to_east = neighbours(year)
        mixed = center + same_west * to_west + same_east * to_east
        samples_ref[year * chunk_rows : (year + 1) * chunk_rows, :] = (mixed / norm).astype(jnp.bfloat16).astype(jnp.float32)
    samples_total = year_count * WIN
    part_rows = (BINS + 8) // 3
    for j in range(cal_own):
        for year in range(year_count):
            rows = samples_ref[year * chunk_rows + j : year * chunk_rows + j + WIN, :]
            scaled_ref[year * WIN : (year + 1) * WIN, :] = jnp.clip((rows + 0.5 * VALUE_RANGE) / width, 0.0, BINS - 1.0)
        for part in range(3):
            points = lax.broadcasted_iota(jnp.int32, (part_rows, lon_own), 0).astype(jnp.float32) + float(part * part_rows)
            total = jnp.zeros((part_rows, lon_own), jnp.float32)
            for index in range(samples_total):
                total = total + jnp.minimum(scaled_ref[index : index + 1, :], points)
            floor_ref[part * part_rows : (part + 1) * part_rows, :] = total
        cumulative = count_all - (floor_ref[1 : BINS + 1, :] - floor_ref[0:BINS, :])
        ranks = jnp.clip(0.5 + SHARPNESS * (QUANT_LEVEL - cumulative / count_all), 0.0, 1.0)
        coarse = -0.5 * VALUE_RANGE + width * jnp.sum(ranks, axis=0, keepdims=True)
        cdf = jnp.zeros((1, lon_own), jnp.float32)
        for year in range(year_count):
            rows = samples_ref[year * chunk_rows + j : year * chunk_rows + j + WIN, :]
            cdf = cdf + jnp.sum(1.0 / (1.0 + jnp.exp(-((coarse - rows) / KERNEL_SCALE))), axis=0, keepdims=True)
        coarse_ref[j : j + 1, :] = coarse
        refined_ref[j : j + 1, :] = coarse - STEP_SIZE * (cdf / count_all - QUANT_LEVEL)


def shards(daily_temps, land_mask):
    days_in = daily_temps.shape[1]
    lon_own = daily_temps.shape[2]
    year_count = lax.axis_size("year")
    region_count = lax.axis_size("region")
    cal_days = days_in - WIN + 1
    cal_own = cal_days // year_count
    span = WIN + cal_own - 1
    count_all = float(year_count * WIN)
    received = gather_windows(daily_temps[0], land_mask, span, cal_own)
    received = received.reshape(region_count * year_count * (span + 1), lon_own)
    region = lax.axis_index("region").astype(jnp.int32).reshape(1)
    out = jax.ShapeDtypeStruct((cal_own, lon_own), jnp.float32)
    return pl.pallas_call(
        functools.partial(threshold_kernel, span, cal_own, year_count, region_count, count_all),
        out_shape=(out, out),
        in_specs=[pl.BlockSpec(memory_space=pltpu.SMEM), pl.BlockSpec(memory_space=pl.ANY)],
        scratch_shapes=[
            pltpu.VMEM((3, year_count * (span + 1), lon_own), jnp.bfloat16),
            pltpu.VMEM((year_count * (span + 1), lon_own), jnp.float32),
            pltpu.VMEM((year_count * WIN, lon_own), jnp.float32),
            pltpu.VMEM(((BINS + 8) // 3 * 3, lon_own), jnp.float32),
            pltpu.SemaphoreType.DMA((3,)),
        ],
    )(region, received)


def solution(mesh):
    return jax.shard_map(
        shards,
        mesh=mesh,
        in_specs=(P("year", None, "region"), P("region")),
        out_specs=(P("year", "region"), P("year", "region")),
        check_vma=False,
    )
```

time: 23.4 us -> 21.4 us (0.915)
  Pallas kernels: 6.3 us -> 4.82 us
  waiting for transfers between devices: 8.22 us -> 7.74 us
    pallas_call x1, Pallas kernels: 4.94 us -> 3.46 us  [shards(): pl.pallas_call(functools.partial(threshold_kernel, span, cal_own, year_co...]
    all_to_all x1, waiting for transfers between devices: 8.22 us -> 7.74 us  [gather_windows(): return lax.all_to_all(rows, ('region', 'year'), 0, 0, tiled=True)]
where the time goes in v14:
time: 21.4 us; the launch traced here: 21.1 us
  waiting for transfers between devices  7.74 us (36%)
  starting transfers between devices  7.3 us (34%)
  Pallas kernels  4.82 us (23%)
  local copies, waits for them, and re-layouts  0.65 us (3%)
  between operations  0.64 us (3%)
    all_to_all x1, waiting for transfers between devices, gather_windows(): return lax.all_to_all(rows, ('region', 'year'), 0, 0, tiled=True)  7.74 us
    all_to_all x1, starting transfers between devices, gather_windows(): return lax.all_to_all(rows, ('region', 'year'), 0, 0, tiled=True)  7.3 us
    pallas_call x1, Pallas kernels, shards(): pl.pallas_call(functools.partial(threshold_kernel, span, cal_own, year_co...  3.46 us
    pallas_call x1, Pallas kernels, gather_windows(): pl.pallas_call(functools.partial(chunk_kernel, span, cal_own, year_count,...  1.36 us
    unnamed x2, local copies, waits for them, and re-layouts  0.65 us
  transfers between devices with their start and end apart: 1, of which 1 were waited for; matrix products, arithmetic and copies ran while one was open for 0% of the time, Pallas kernels for 0%

profile of v14, /device:TPU:0, one launch (start us, length us, event | category | flops | bytes accessed | tf_op | source)
XLA Modules:
  0.0 21.1 jit_solution(396956122661020679)
XLA Ops:
  0.6 1.4 %shard_map.41 = bf16[512,128]{1,0:T(8,128)(2,1)} custom-call(bf16[22,128]{1,0:T(8,128)(2,1)} %bitcast.7, s32[1,128]{1,0:T(1,128)} %bitcast.8), custom_call_target="tpu_custom_call" | custom-call | tf_op jit(solution)/shard_map/pallas_call | solution.py:40
  2.0 7.3 %all-to-all-start = ((bf16[32,16,128]{2,1,0:T(8,128)(2,1)}), bf16[32,16,128]{2,1,0:T(8,128)(2,1)S(1)}, u32[]{:S(2)}, u32[]{:S(2)}) async-start(bf16[32,16,128]{2,1,0:T(8,128)(2,1)} %bitcast.6), calls=%async_computation | async-start | bytes 262144 | tf_op jit(solution)/shard_map/all_to_all | solution.py:46
  9.3 7.7 %all-to-all-done = bf16[32,16,128]{2,1,0:T(8,128)(2,1)S(1)} async-done(((bf16[32,16,128]{2,1,0:T(8,128)(2,1)}), bf16[32,16,128]{2,1,0:T(8,128)(2,1)S(1)}, u32[]{:S(2)}, u32[]{:S(2)}) %all-to-all-start) | async-done | bytes 131104 | tf_op jit(solution)/shard_map/all_to_all | solution.py:46
  17.0 0.0 copy-start
  17.0 0.6 %copy-done = bf16[32,16,128]{2,1,0:T(8,128)(2,1)} copy-done((bf16[32,16,128]{2,1,0:T(8,128)(2,1)}, bf16[32,16,128]{2,1,0:T(8,128)(2,1)S(1)}, u32[]{:S(2)}) %copy-start) | copy-done | bytes 131096
  17.7 3.5 %shard_map.42 = (f32[1,128]{1,0:T(1,128)}, f32[1,128]{1,0:T(1,128)}) custom-call(s32[1]{0:T(128)} %bitcast.region_ref, bf16[512,128]{1,0:T(8,128)(2,1)} %bitcast.5), custom_call_target="tpu_custom_call" | custom-call | tf_op jit(solution)/shard_map/pallas_call | solution.py:133
Async XLA Ops:
  2.0 15.0 %all-to-all-start = ((bf16[32,16,128]{2,1,0:T(8,128)(2,1)}), bf16[32,16,128]{2,1,0:T(8,128)(2,1)S(1)}, u32[]{:S(2)}, u32[]{:S(2)}) async-start(bf16[32,16,128]{2,1,0:T(8,128)(2,1)} %bitcast.6), calls=%async_computation | async-start | bytes 262144 | tf_op jit(solution)/shard_map/all_to_all | solution.py:46
  17.0 0.6 %copy-start = (bf16[32,16,128]{2,1,0:T(8,128)(2,1)}, bf16[32,16,128]{2,1,0:T(8,128)(2,1)S(1)}, u32[]{:S(2)}) copy-start(bf16[32,16,128]{2,1,0:T(8,128)(2,1)S(1)} %all-to-all-done) | copy-start | bytes 393220

commit v15 on v13

--- a/solution.py
+++ b/solution.py
@@ -49,13 +49,24 @@
 def coarse_from_samples(samples, count_all, bin_count):
     width = VALUE_RANGE / bin_count
     scaled = jnp.clip((samples + 0.5 * VALUE_RANGE) / width, 0.0, bin_count - 1.0)
-    grouped = scaled.reshape(-1, WIN, scaled.shape[-1])
-    points = lax.broadcasted_iota(jnp.float32, (bin_count + 8, 1), 0)
-    partial = jnp.sum(jnp.minimum(grouped[:, :, None, :], points[None, None]), axis=1)
-    floor_sum = jnp.sum(partial, axis=0)
-    cumulative = count_all - (floor_sum[1 : bin_count + 1] - floor_sum[:bin_count])
-    ranks = jnp.clip(0.5 + SHARPNESS * (QUANT_LEVEL - cumulative / count_all), 0.0, 1.0)
-    return -0.5 * VALUE_RANGE + width * jnp.sum(ranks, axis=0)
+    low = count_all * (QUANT_LEVEL - 0.5 / SHARPNESS)
+    high = count_all * (QUANT_LEVEL + 0.5 / SHARPNESS)
+    block = 8
+
+    def running(points):
+        return jnp.sum(jnp.clip(points[None] + 1.0 - scaled[:, None, :], 0.0, 1.0), axis=0)
+
+    ends = lax.broadcasted_iota(jnp.int32, (bin_count // block, 1), 0).astype(jnp.float32) * block + (block - 1)
+    at_ends = running(ends)
+    full_low = jnp.sum(jnp.where(at_ends <= low, 1.0, 0.0), axis=0)
+    full_high = jnp.sum(jnp.where(at_ends < high, 1.0, 0.0), axis=0)
+    offsets = lax.broadcasted_iota(jnp.int32, (block, 1), 0).astype(jnp.float32)
+    inside = running(jnp.concatenate([full_low[None] * block + offsets, full_high[None] * block + offsets], axis=0))
+    first_low = full_low * block + jnp.sum(jnp.where(inside[:block] <= low, 1.0, 0.0), axis=0)
+    first_high = full_high * block + jnp.sum(jnp.where(inside[block:] < high, 1.0, 0.0), axis=0)
+    between = jnp.sum(jnp.maximum(first_high - scaled, 0.0) - jnp.maximum(first_low - scaled, 0.0), axis=0)
+    ranks = first_low + (first_high - first_low) * (0.5 + SHARPNESS * QUANT_LEVEL) - (SHARPNESS / count_all) * between
+    return -0.5 * VALUE_RANGE + width * ranks
 
 
 def shards(daily_temps, land_mask):

time: 19.7 us -> 19 us (0.964)
  other arithmetic: 2.35 us -> 1.63 us
    reduce_sum x2 -> x5, other arithmetic: 1.4 us -> 0.57 us  [the longest x2 0.48 us: running(): jnp.sum(jnp.clip(points[None] + 1.0 - scaled[:, None, :], 0.0, 1.0), axis=0)]
where the time goes in v15:
time: 19 us; the launch traced here: 18.8 us
  waiting for transfers between devices  7.7 us (41%)
  starting transfers between devices  7.3 us (38%)
  other arithmetic  1.63 us (9%)
  Pallas kernels  1.35 us (7%)
  between operations  0.7 us (4%)
    all_to_all x1, waiting for transfers between devices, gather_windows(): return lax.all_to_all(rows, ('region', 'year'), 0, 0, tiled=True)  7.7 us
    all_to_all x1, starting transfers between devices, gather_windows(): return lax.all_to_all(rows, ('region', 'year'), 0, 0, tiled=True)  7.3 us
    pallas_call x1, Pallas kernels, gather_windows(): pl.pallas_call(functools.partial(chunk_kernel, span, cal_own, year_count,...  1.35 us
    sub x1, other arithmetic, shards(): refined = coarse - STEP_SIZE * (cdf / count_all - QUANT_LEVEL)  0.52 us
    reduce_sum x2, other arithmetic, running(): jnp.sum(jnp.clip(points[None] + 1.0 - scaled[:, None, :], 0.0, 1.0), axis=0)  0.48 us
  transfers between devices with their start and end apart: 1, of which 1 were waited for; matrix products, arithmetic and copies ran while one was open for 0% of the time, Pallas kernels for 0%

profile of v15, /device:TPU:0, one launch (start us, length us, event | category | flops | bytes accessed | tf_op | source)
XLA Modules:
  0.0 18.8 jit_solution(5958196152981462633)
XLA Ops:
  0.6 1.3 %shard_map.41 = bf16[512,128]{1,0:T(8,128)(2,1)} custom-call(bf16[22,128]{1,0:T(8,128)(2,1)} %bitcast.39, s32[1,128]{1,0:T(1,128)} %bitcast.41), custom_call_target="tpu_custom_call" | custom-call | tf_op jit(solution)/shard_map/pallas_call | solution.py:40
  2.0 7.3 %all-to-all-start = ((bf16[32,16,128]{2,1,0:T(8,128)(2,1)}), bf16[32,16,128]{2,1,0:T(8,128)(2,1)S(1)}, u32[]{:S(2)}, u32[]{:S(2)}) async-start(bf16[32,16,128]{2,1,0:T(8,128)(2,1)} %bitcast.37), calls=%async_computation | async-start | bytes 262144 | tf_op jit(solution)/shard_map/all_to_all | solution.py:46
  9.3 7.7 %all-to-all-done = bf16[32,16,128]{2,1,0:T(8,128)(2,1)S(1)} async-done(((bf16[32,16,128]{2,1,0:T(8,128)(2,1)}), bf16[32,16,128]{2,1,0:T(8,128)(2,1)S(1)}, u32[]{:S(2)}, u32[]{:S(2)}) %all-to-all-start) | async-done | bytes 131104 | tf_op jit(solution)/shard_map/all_to_all | solution.py:46
  17.0 0.1 fusion.20
  17.1 0.1 slice_convert_fusion
  17.2 0.1 subtract_bitcast_fusion
  17.3 0.1 add_bitcast_fusion
  17.4 0.1 multiply_clamp_fusion
  17.5 0.3 %clamp_reduce_fusion = f32[32,128]{1,0:T(8,128)S(1)} fusion(f32[120,128]{1,0:T(8,128)S(1)} %min.28, f32[32]{0:T(128)S(1)} %multiply_add_fusion.1), kind=kLoop, calls=%fused_computation | loop fusion | flops 1470464 | bytes 77952 | tf_op jit(solution)/shard_map/reduce_sum | solution.py:57
  17.9 0.1 broadcast_add_fusion.1
  17.9 0.2 clamp_reduce_fusion.1
  18.2 0.1 fusion.6
  18.2 0.5 %bitcast_subtract_fusion = (f32[1,128]{1,0:T(1,128)}, f32[1,128]{1,0:T(1,128)}) fusion(f32[128]{0:T(128)S(1)} %fusion.6, f32[128]{0:T(128)S(1)} %subtract_reduce_fusion, f32[128]{0:T(128)S(1)} %fusion.15, f32[128]{0:T(128)S(1)} %fusion.14), kind=kLoop, calls=%fused_computation.32 | loop fusion | flops 1408 | bytes 3072 | tf_op jit(solution)/shard_map/sub | solution.py:100
  (13 shorter events, 0.1 us)
Async XLA Ops:
  2.0 15.0 %all-to-all-start = ((bf16[32,16,128]{2,1,0:T(8,128)(2,1)}), bf16[32,16,128]{2,1,0:T(8,128)(2,1)S(1)}, u32[]{:S(2)}, u32[]{:S(2)}) async-start(bf16[32,16,128]{2,1,0:T(8,128)(2,1)} %bitcast.37), calls=%async_computation | async-start | bytes 262144 | tf_op jit(solution)/shard_map/all_to_all | solution.py:46

commit v16 on v15

--- a/solution.py
+++ b/solution.py
@@ -18,7 +18,13 @@
 STEP_SIZE = 2.0
 
 
-def chunk_kernel(span, cal_own, year_count, region_count, temps_ref, mask_ref, out_ref, stage_ref):
+def chunk_kernel(span, cal_own, year_count, region_count, temps_hbm, mask_hbm, out_hbm, temps_ref, mask_ref,
+                 out_ref, stage_ref, sems):
+    loads = [pltpu.make_async_copy(temps_hbm, temps_ref, sems.at[0]), pltpu.make_async_copy(mask_hbm, mask_ref, sems.at[1])]
+    for load in loads:
+        load.start()
+    for load in loads:
+        load.wait()
     days_in = temps_ref.shape[0]
     chunk_rows = span + 1
     stage_ref[0:days_in, :] = temps_ref[...].astype(jnp.float32)
@@ -31,16 +37,28 @@
         for region in range(region_count):
             first = (region * year_count + year) * chunk_rows
             out_ref[first : first + chunk_rows, :] = tile
+    store = pltpu.make_async_copy(out_ref, out_hbm, sems.at[2])
+    store.start()
+    store.wait()
 
 
 def gather_windows(temps, flags, span, cal_own):
     year_count, region_count = lax.axis_size("year"), lax.axis_size("region")
     chunk_rows = span + 1
     lon_own = temps.shape[1]
+    total_rows = year_count * region_count * chunk_rows
     rows = pl.pallas_call(
         functools.partial(chunk_kernel, span, cal_own, year_count, region_count),
-        out_shape=jax.ShapeDtypeStruct((year_count * region_count * chunk_rows, lon_own), temps.dtype),
-        scratch_shapes=[pltpu.VMEM((temps.shape[0] + 1, lon_own), jnp.float32)],
+        out_shape=jax.ShapeDtypeStruct((total_rows, lon_own), temps.dtype),
+        in_specs=[pl.BlockSpec(memory_space=pl.ANY)] * 2,
+        out_specs=pl.BlockSpec(memory_space=pl.ANY),
+        scratch_shapes=[
+            pltpu.VMEM(temps.shape, temps.dtype),
+            pltpu.VMEM((1, lon_own), flags.dtype),
+            pltpu.VMEM((total_rows, lon_own), temps.dtype),
+            pltpu.VMEM((temps.shape[0] + 1, lon_own), jnp.float32),
+            pltpu.SemaphoreType.DMA((3,)),
+        ],
     )(temps, flags.reshape(1, lon_own))
     rows = rows.reshape(year_count * region_count, chunk_rows, lon_own)
     return lax.all_to_all(rows, ("region", "year"), 0, 0, tiled=True)

time: 19 us -> 19 us (level)
  no operation moved by 1% of the time
where the time goes in v16:
time: 19 us; the launch traced here: 18.8 us
  waiting for transfers between devices  7.7 us (41%)
  starting transfers between devices  7.3 us (38%)
  other arithmetic  1.63 us (9%)
  Pallas kernels  1.37 us (7%)
  between operations  0.71 us (4%)
    all_to_all x1, waiting for transfers between devices, gather_windows(): return lax.all_to_all(rows, ('region', 'year'), 0, 0, tiled=True)  7.7 us
    all_to_all x1, starting transfers between devices, gather_windows(): return lax.all_to_all(rows, ('region', 'year'), 0, 0, tiled=True)  7.3 us
    pallas_call x1, Pallas kernels, gather_windows(): pl.pallas_call(functools.partial(chunk_kernel, span, cal_own, year_count,...  1.37 us
    sub x1, other arithmetic, shards(): refined = coarse - STEP_SIZE * (cdf / count_all - QUANT_LEVEL)  0.52 us
    reduce_sum x2, other arithmetic, running(): jnp.sum(jnp.clip(points[None] + 1.0 - scaled[:, None, :], 0.0, 1.0), axis=0)  0.48 us
  transfers between devices with their start and end apart: 1, of which 1 were waited for; matrix products, arithmetic and copies ran while one was open for 0% of the time, Pallas kernels for 0%

profile of v16, /device:TPU:0, one launch (start us, length us, event | category | flops | bytes accessed | tf_op | source)
XLA Modules:
  0.0 18.8 jit_solution(4552120138738790416)
XLA Ops:
  0.6 1.4 %shard_map.41 = bf16[512,128]{1,0:T(8,128)(2,1)} custom-call(bf16[22,128]{1,0:T(8,128)(2,1)} %bitcast.39, s32[1,128]{1,0:T(1,128)} %bitcast.41), custom_call_target="tpu_custom_call" | custom-call | tf_op jit(solution)/shard_map/pallas_call | solution.py:50
  2.0 7.3 %all-to-all-start = ((bf16[32,16,128]{2,1,0:T(8,128)(2,1)}), bf16[32,16,128]{2,1,0:T(8,128)(2,1)S(1)}, u32[]{:S(2)}, u32[]{:S(2)}) async-start(bf16[32,16,128]{2,1,0:T(8,128)(2,1)} %bitcast.37), calls=%async_computation | async-start | bytes 262144 | tf_op jit(solution)/shard_map/all_to_all | solution.py:64
  9.4 7.7 %all-to-all-done = bf16[32,16,128]{2,1,0:T(8,128)(2,1)S(1)} async-done(((bf16[32,16,128]{2,1,0:T(8,128)(2,1)}), bf16[32,16,128]{2,1,0:T(8,128)(2,1)S(1)}, u32[]{:S(2)}, u32[]{:S(2)}) %all-to-all-start) | async-done | bytes 131104 | tf_op jit(solution)/shard_map/all_to_all | solution.py:64
  17.1 0.1 fusion.20
  17.2 0.1 slice_convert_fusion
  17.2 0.1 subtract_bitcast_fusion
  17.3 0.1 add_bitcast_fusion
  17.4 0.1 multiply_clamp_fusion
  17.5 0.3 %clamp_reduce_fusion = f32[32,128]{1,0:T(8,128)S(1)} fusion(f32[120,128]{1,0:T(8,128)S(1)} %min.28, f32[32]{0:T(128)S(1)} %multiply_add_fusion.1), kind=kLoop, calls=%fused_computation | loop fusion | flops 1470464 | bytes 77952 | tf_op jit(solution)/shard_map/reduce_sum | solution.py:75
  17.9 0.1 broadcast_add_fusion.1
  18.0 0.2 clamp_reduce_fusion.1
  18.2 0.1 fusion.6
  18.3 0.5 %bitcast_subtract_fusion = (f32[1,128]{1,0:T(1,128)}, f32[1,128]{1,0:T(1,128)}) fusion(f32[128]{0:T(128)S(1)} %fusion.6, f32[128]{0:T(128)S(1)} %subtract_reduce_fusion, f32[128]{0:T(128)S(1)} %fusion.15, f32[128]{0:T(128)S(1)} %fusion.14), kind=kLoop, calls=%fused_computation.32 | loop fusion | flops 1408 | bytes 3072 | tf_op jit(solution)/shard_map/sub | solution.py:118
  (13 shorter events, 0.1 us)
Async XLA Ops:
  2.0 15.1 %all-to-all-start = ((bf16[32,16,128]{2,1,0:T(8,128)(2,1)}), bf16[32,16,128]{2,1,0:T(8,128)(2,1)S(1)}, u32[]{:S(2)}, u32[]{:S(2)}) async-start(bf16[32,16,128]{2,1,0:T(8,128)(2,1)} %bitcast.37), calls=%async_computation | async-start | bytes 262144 | tf_op jit(solution)/shard_map/all_to_all | solution.py:64

commit v17 on v15

--- a/solution.py
+++ b/solution.py
@@ -51,19 +51,24 @@
     scaled = jnp.clip((samples + 0.5 * VALUE_RANGE) / width, 0.0, bin_count - 1.0)
     low = count_all * (QUANT_LEVEL - 0.5 / SHARPNESS)
     high = count_all * (QUANT_LEVEL + 0.5 / SHARPNESS)
-    block = 8
 
     def running(points):
         return jnp.sum(jnp.clip(points[None] + 1.0 - scaled[:, None, :], 0.0, 1.0), axis=0)
 
-    ends = lax.broadcasted_iota(jnp.int32, (bin_count // block, 1), 0).astype(jnp.float32) * block + (block - 1)
-    at_ends = running(ends)
-    full_low = jnp.sum(jnp.where(at_ends <= low, 1.0, 0.0), axis=0)
-    full_high = jnp.sum(jnp.where(at_ends < high, 1.0, 0.0), axis=0)
-    offsets = lax.broadcasted_iota(jnp.int32, (block, 1), 0).astype(jnp.float32)
-    inside = running(jnp.concatenate([full_low[None] * block + offsets, full_high[None] * block + offsets], axis=0))
-    first_low = full_low * block + jnp.sum(jnp.where(inside[:block] <= low, 1.0, 0.0), axis=0)
-    first_high = full_high * block + jnp.sum(jnp.where(inside[block:] < high, 1.0, 0.0), axis=0)
+    def counts(values, bound, inclusive):
+        return jnp.sum(jnp.where(values <= bound if inclusive else values < bound, 1.0, 0.0), axis=0)
+
+    sizes = (32, 4, 1)
+    steps = lax.broadcasted_iota(jnp.int32, (bin_count // sizes[0], 1), 0).astype(jnp.float32)
+    at_ends = running(steps * sizes[0] + (sizes[0] - 1))
+    first_low = sizes[0] * counts(at_ends, low, True)
+    first_high = sizes[0] * counts(at_ends, high, False)
+    for parent, size in zip(sizes[:-1], sizes[1:]):
+        parts = parent // size
+        steps = lax.broadcasted_iota(jnp.int32, (parts, 1), 0).astype(jnp.float32) * size + (size - 1)
+        at_ends = running(jnp.concatenate([first_low[None] + steps, first_high[None] + steps], axis=0))
+        first_low = first_low + size * counts(at_ends[:parts], low, True)
+        first_high = first_high + size * counts(at_ends[parts:], high, False)
     between = jnp.sum(jnp.maximum(first_high - scaled, 0.0) - jnp.maximum(first_low - scaled, 0.0), axis=0)
     ranks = first_low + (first_high - first_low) * (0.5 + SHARPNESS * QUANT_LEVEL) - (SHARPNESS / count_all) * between
     return -0.5 * VALUE_RANGE + width * ranks

time: 19 us -> 19.2 us (1.011)
    reduce_sum x2 -> x3, other arithmetic: 0.48 us -> 0.49 us  [running(): jnp.sum(jnp.clip(points[None] + 1.0 - scaled[:, None, :], 0.0, 1.0), axis=0)]
where the time goes in v17:
time: 19.2 us; the launch traced here: 18.9 us
  waiting for transfers between devices  7.69 us (40%)
  starting transfers between devices  7.3 us (38%)
  other arithmetic  1.76 us (9%)
  Pallas kernels  1.35 us (7%)
  between operations  0.71 us (4%)
    all_to_all x1, waiting for transfers between devices, gather_windows(): return lax.all_to_all(rows, ('region', 'year'), 0, 0, tiled=True)  7.69 us
    all_to_all x1, starting transfers between devices, gather_windows(): return lax.all_to_all(rows, ('region', 'year'), 0, 0, tiled=True)  7.3 us
    pallas_call x1, Pallas kernels, gather_windows(): pl.pallas_call(functools.partial(chunk_kernel, span, cal_own, year_count,...  1.35 us
    sub x1, other arithmetic, shards(): refined = coarse - STEP_SIZE * (cdf / count_all - QUANT_LEVEL)  0.52 us
    reduce_sum x3, other arithmetic, running(): jnp.sum(jnp.clip(points[None] + 1.0 - scaled[:, None, :], 0.0, 1.0), axis=0)  0.49 us
  transfers between devices with their start and end apart: 1, of which 1 were waited for; matrix products, arithmetic and copies ran while one was open for 0% of the time, Pallas kernels for 0%

profile of v17, /device:TPU:0, one launch (start us, length us, event | category | flops | bytes accessed | tf_op | source)
XLA Modules:
  0.0 18.9 jit_solution(12624889403017416175)
XLA Ops:
  0.6 1.3 %shard_map.41 = bf16[512,128]{1,0:T(8,128)(2,1)} custom-call(bf16[22,128]{1,0:T(8,128)(2,1)} %bitcast.39, s32[1,128]{1,0:T(1,128)} %bitcast.41), custom_call_target="tpu_custom_call" | custom-call | tf_op jit(solution)/shard_map/pallas_call | solution.py:40
  2.0 7.3 %all-to-all-start = ((bf16[32,16,128]{2,1,0:T(8,128)(2,1)}), bf16[32,16,128]{2,1,0:T(8,128)(2,1)S(1)}, u32[]{:S(2)}, u32[]{:S(2)}) async-start(bf16[32,16,128]{2,1,0:T(8,128)(2,1)} %bitcast.37), calls=%async_computation | async-start | bytes 262144 | tf_op jit(solution)/shard_map/all_to_all | solution.py:46
  9.3 7.7 %all-to-all-done = bf16[32,16,128]{2,1,0:T(8,128)(2,1)S(1)} async-done(((bf16[32,16,128]{2,1,0:T(8,128)(2,1)}), bf16[32,16,128]{2,1,0:T(8,128)(2,1)S(1)}, u32[]{:S(2)}, u32[]{:S(2)}) %all-to-all-start) | async-done | bytes 131104 | tf_op jit(solution)/shard_map/all_to_all | solution.py:46
  17.0 0.1 fusion.18
  17.1 0.1 slice_convert_fusion
  17.2 0.1 subtract_bitcast_fusion
  17.3 0.1 add_bitcast_fusion
  17.4 0.1 multiply_clamp_fusion
  17.5 0.2 %clamp_reduce_fusion.2 = f32[8,128]{1,0:T(8,128)S(1)} fusion(f32[120,128]{1,0:T(8,128)S(1)} %min.32, f32[8]{0:T(128)S(1)} %multiply_add_fusion.4), kind=kLoop, calls=%fused_computation.2 | loop fusion | flops 367616 | bytes 65568 | tf_op jit(solution)/shard_map/reduce_sum | solution.py:56
  17.7 0.1 broadcast_add_fusion.1
  17.8 0.2 clamp_reduce_fusion
  18.0 0.1 broadcast_add_fusion.3
  18.1 0.1 clamp_reduce_fusion.1
  18.3 0.1 fusion.6
  18.4 0.5 %bitcast_subtract_fusion = (f32[1,128]{1,0:T(1,128)}, f32[1,128]{1,0:T(1,128)}) fusion(f32[128]{0:T(128)S(1)} %fusion.6, f32[128]{0:T(128)S(1)} %subtract_reduce_fusion, f32[128]{0:T(128)S(1)} %add.318, f32[128]{0:T(128)S(1)} %add.316), kind=kLoop, calls=%fused_computation.40 | loop fusion | flops 1408 | bytes 3072 | tf_op jit(solution)/shard_map/sub | solution.py:105
  (18 shorter events, 0.2 us)
Async XLA Ops:
  2.0 15.0 %all-to-all-start = ((bf16[32,16,128]{2,1,0:T(8,128)(2,1)}), bf16[32,16,128]{2,1,0:T(8,128)(2,1)S(1)}, u32[]{:S(2)}, u32[]{:S(2)}) async-start(bf16[32,16,128]{2,1,0:T(8,128)(2,1)} %bitcast.37), calls=%async_computation | async-start | bytes 262144 | tf_op jit(solution)/shard_map/all_to_all | solution.py:46

commit v18 on v15

--- a/solution.py
+++ b/solution.py
@@ -87,8 +87,11 @@
     center = center.astype(jnp.float32)
     to_west = jnp.concatenate([west[..., -1:].astype(jnp.float32), center[..., :-1]], axis=-1)
     to_east = jnp.concatenate([center[..., 1:], east[..., :1].astype(jnp.float32)], axis=-1)
-    same_west = 1.0 - jnp.abs(center[0, span] - to_west[0, span])
-    same_east = 1.0 - jnp.abs(center[0, span] - to_east[0, span])
+    flags = land_mask.astype(jnp.float32)
+    flag_west = jnp.concatenate([west[0, span, -1:].astype(jnp.float32), flags[:-1]])
+    flag_east = jnp.concatenate([flags[1:], east[0, span, :1].astype(jnp.float32)])
+    same_west = 1.0 - jnp.abs(flags - flag_west)
+    same_east = 1.0 - jnp.abs(flags - flag_east)
     mixed = center[:, :span] + same_west * to_west[:, :span] + same_east * to_east[:, :span]
     every_year = lax.reduce_precision(mixed / (1.0 + same_west + same_east), exponent_bits=8, mantissa_bits=7)
     coarse_rows = []

time: 19 us -> 21.4 us (1.13)
  between operations: 0.7 us -> 2.04 us
  local copies, waits for them, and re-layouts: 0.09 us -> 1.26 us
    slice x1 -> x4, local copies, waits for them, and re-layouts: 0.08 us -> 1.25 us  [the longest x1 0.58 us: shards(): west[0, span, -1:].astype(jnp.float32)]
where the time goes in v18:
time: 21.4 us; the launch traced here: 21.2 us
  waiting for transfers between devices  7.6 us (36%)
  starting transfers between devices  7.3 us (34%)
  between operations  2.04 us (10%)
  other arithmetic  1.63 us (8%)
  Pallas kernels  1.35 us (6%)
  local copies, waits for them, and re-layouts  1.26 us (6%)
    all_to_all x1, waiting for transfers between devices, gather_windows(): return lax.all_to_all(rows, ('region', 'year'), 0, 0, tiled=True)  7.6 us
    all_to_all x1, starting transfers between devices, gather_windows(): return lax.all_to_all(rows, ('region', 'year'), 0, 0, tiled=True)  7.3 us
    pallas_call x1, Pallas kernels, gather_windows(): pl.pallas_call(functools.partial(chunk_kernel, span, cal_own, year_count,...  1.35 us
    slice x1, local copies, waits for them, and re-layouts, shards(): west[0, span, -1:].astype(jnp.float32)  0.58 us
    sub x1, other arithmetic, shards(): refined = coarse - STEP_SIZE * (cdf / count_all - QUANT_LEVEL)  0.52 us
    slice x1, local copies, waits for them, and re-layouts, shards(): east[0, span, :1].astype(jnp.float32)  0.51 us
    reduce_sum x2, other arithmetic, running(): jnp.sum(jnp.clip(points[None] + 1.0 - scaled[:, None, :], 0.0, 1.0), axis=0)  0.48 us
  transfers between devices with their start and end apart: 1, of which 1 were waited for; matrix products, arithmetic and copies ran while one was open for 0% of the time, Pallas kernels for 0%

profile of v18, /device:TPU:0, one launch (start us, length us, event | category | flops | bytes accessed | tf_op | source)
XLA Modules:
  0.0 21.2 jit_solution(488578600546595186)
XLA Ops:
  0.6 1.3 %shard_map.41 = bf16[512,128]{1,0:T(8,128)(2,1)} custom-call(bf16[22,128]{1,0:T(8,128)(2,1)} %bitcast.38, s32[1,128]{1,0:T(1,128)} %bitcast.39), custom_call_target="tpu_custom_call" | custom-call | tf_op jit(solution)/shard_map/pallas_call | solution.py:40
  2.0 0.0 copy-start
  2.0 7.3 %all-to-all-start = ((bf16[32,16,128]{2,1,0:T(8,128)(2,1)}), bf16[32,16,128]{2,1,0:T(8,128)(2,1)S(1)}, u32[]{:S(2)}, u32[]{:S(2)}) async-start(bf16[32,16,128]{2,1,0:T(8,128)(2,1)} %bitcast.36), calls=%async_computation | async-start | bytes 262144 | tf_op jit(solution)/shard_map/all_to_all | solution.py:46
  9.3 0.0 copy-done
  9.4 0.1 fusion.21
  9.4 7.6 %all-to-all-done = bf16[32,16,128]{2,1,0:T(8,128)(2,1)S(1)} async-done(((bf16[32,16,128]{2,1,0:T(8,128)(2,1)}), bf16[32,16,128]{2,1,0:T(8,128)(2,1)S(1)}, u32[]{:S(2)}, u32[]{:S(2)}) %all-to-all-start) | async-done | bytes 131104 | tf_op jit(solution)/shard_map/all_to_all | solution.py:46
  17.0 0.6 %slice.53 = bf16[1,1,1]{2,1,0:T(2,128)(2,1)} slice(bf16[8,16,128]{2,1,0:T(8,128)(2,1)S(1)} %get-tuple-element.16), slice={[0:1], [15:16], [127:128]} | slice | bytes 4 | tf_op jit(solution)/shard_map/slice | solution.py:91
  17.6 0.1 slice_convert_fusion
  17.7 0.5 %slice.56 = bf16[1,1,1]{2,1,0:T(2,128)(2,1)} slice(bf16[8,16,128]{2,1,0:T(8,128)(2,1)S(1)} %get-tuple-element.15), slice={[0:1], [15:16], [0:1]} | slice | bytes 4 | tf_op jit(solution)/shard_map/slice | solution.py:92
  18.2 0.1 fusion.20
  19.6 0.1 broadcast_subtract_fusion
  19.7 0.1 subtract_add_fusion
  19.8 0.1 multiply_clamp_fusion
  19.9 0.3 %clamp_reduce_fusion = f32[32,128]{1,0:T(8,128)S(1)} fusion(f32[120,128]{1,0:T(8,128)S(1)} %min.28, f32[32]{0:T(128)S(1)} %multiply_add_fusion.1), kind=kLoop, calls=%fused_computation | loop fusion | flops 1470464 | bytes 77952 | tf_op jit(solution)/shard_map/reduce_sum | solution.py:57
  20.3 0.1 broadcast_add_fusion.1
  20.3 0.2 clamp_reduce_fusion.1
  20.6 0.1 fusion.6
  20.6 0.5 %bitcast_subtract_fusion = (f32[1,128]{1,0:T(1,128)}, f32[1,128]{1,0:T(1,128)}) fusion(f32[128]{0:T(128)S(1)} %fusion.6, f32[128]{0:T(128)S(1)} %subtract_reduce_fusion, f32[128]{0:T(128)S(1)} %fusion.15, f32[128]{0:T(128)S(1)} %fusion.14), kind=kLoop, calls=%fused_computation.32 | loop fusion | flops 1408 | bytes 3072 | tf_op jit(solution)/shard_map/sub | solution.py:103
  (14 shorter events, 0.2 us)
Async XLA Ops:
  2.0 7.3 %copy-start = (s32[128]{0:T(128)S(1)}, s32[128]{0:T(128)}, u32[]{:S(2)}) copy-start(s32[128]{0:T(128)} %param.3) | copy-start | bytes 1540
  2.0 15.0 %all-to-all-start = ((bf16[32,16,128]{2,1,0:T(8,128)(2,1)}), bf16[32,16,128]{2,1,0:T(8,128)(2,1)S(1)}, u32[]{:S(2)}, u32[]{:S(2)}) async-start(bf16[32,16,128]{2,1,0:T(8,128)(2,1)} %bitcast.36), calls=%async_computation | async-start | bytes 262144 | tf_op jit(solution)/shard_map/all_to_all | solution.py:46

commit v19 on v15

--- a/solution.py
+++ b/solution.py
@@ -51,7 +51,7 @@
     scaled = jnp.clip((samples + 0.5 * VALUE_RANGE) / width, 0.0, bin_count - 1.0)
     low = count_all * (QUANT_LEVEL - 0.5 / SHARPNESS)
     high = count_all * (QUANT_LEVEL + 0.5 / SHARPNESS)
-    block = 8
+    block = 16
 
     def running(points):
         return jnp.sum(jnp.clip(points[None] + 1.0 - scaled[:, None, :], 0.0, 1.0), axis=0)

time: 19 us -> 19 us (level)
  no operation moved by 1% of the time
where the time goes in v19:
time: 19 us; the launch traced here: 18.8 us
  waiting for transfers between devices  7.7 us (41%)
  starting transfers between devices  7.3 us (38%)
  other arithmetic  1.64 us (9%)
  Pallas kernels  1.35 us (7%)
  between operations  0.7 us (4%)
    all_to_all x1, waiting for transfers between devices, gather_windows(): return lax.all_to_all(rows, ('region', 'year'), 0, 0, tiled=True)  7.7 us
    all_to_all x1, starting transfers between devices, gather_windows(): return lax.all_to_all(rows, ('region', 'year'), 0, 0, tiled=True)  7.3 us
    pallas_call x1, Pallas kernels, gather_windows(): pl.pallas_call(functools.partial(chunk_kernel, span, cal_own, year_count,...  1.35 us
    sub x1, other arithmetic, shards(): refined = coarse - STEP_SIZE * (cdf / count_all - QUANT_LEVEL)  0.52 us
    reduce_sum x2, other arithmetic, running(): jnp.sum(jnp.clip(points[None] + 1.0 - scaled[:, None, :], 0.0, 1.0), axis=0)  0.49 us
  transfers between devices with their start and end apart: 1, of which 1 were waited for; matrix products, arithmetic and copies ran while one was open for 0% of the time, Pallas kernels for 0%

profile of v19, /device:TPU:0, one launch (start us, length us, event | category | flops | bytes accessed | tf_op | source)
XLA Modules:
  0.0 18.8 jit_solution(14563792653710091848)
XLA Ops:
  0.6 1.3 %shard_map.41 = bf16[512,128]{1,0:T(8,128)(2,1)} custom-call(bf16[22,128]{1,0:T(8,128)(2,1)} %bitcast.39, s32[1,128]{1,0:T(1,128)} %bitcast.41), custom_call_target="tpu_custom_call" | custom-call | tf_op jit(solution)/shard_map/pallas_call | solution.py:40
  2.0 7.3 %all-to-all-start = ((bf16[32,16,128]{2,1,0:T(8,128)(2,1)}), bf16[32,16,128]{2,1,0:T(8,128)(2,1)S(1)}, u32[]{:S(2)}, u32[]{:S(2)}) async-start(bf16[32,16,128]{2,1,0:T(8,128)(2,1)} %bitcast.37), calls=%async_computation | async-start | bytes 262144 | tf_op jit(solution)/shard_map/all_to_all | solution.py:46
  9.3 7.7 %all-to-all-done = bf16[32,16,128]{2,1,0:T(8,128)(2,1)S(1)} async-done(((bf16[32,16,128]{2,1,0:T(8,128)(2,1)}), bf16[32,16,128]{2,1,0:T(8,128)(2,1)S(1)}, u32[]{:S(2)}, u32[]{:S(2)}) %all-to-all-start) | async-done | bytes 131104 | tf_op jit(solution)/shard_map/all_to_all | solution.py:46
  17.0 0.1 fusion.20
  17.1 0.1 slice_convert_fusion
  17.2 0.1 subtract_bitcast_fusion
  17.3 0.1 add_bitcast_fusion
  17.4 0.1 multiply_clamp_fusion
  17.5 0.2 %clamp_reduce_fusion.1 = f32[16,128]{1,0:T(8,128)S(1)} fusion(f32[120,128]{1,0:T(8,128)S(1)} %min.28, f32[16]{0:T(128)S(1)} %multiply_add_fusion.1), kind=kLoop, calls=%fused_computation.1 | loop fusion | flops 735232 | bytes 69696 | tf_op jit(solution)/shard_map/reduce_sum | solution.py:57
  17.8 0.1 broadcast_add_fusion.1
  17.8 0.3 %clamp_reduce_fusion = f32[32,128]{1,0:T(8,128)S(1)} fusion(f32[120,128]{1,0:T(8,128)S(1)} %min.28, f32[32,128]{1,0:T(8,128)S(1)} %maximum_add_fusion), kind=kLoop, calls=%fused_computation | loop fusion | flops 1470464 | bytes 94208 | tf_op jit(solution)/shard_map/reduce_sum | solution.py:57
  18.2 0.1 fusion.6
  18.2 0.5 %bitcast_subtract_fusion = (f32[1,128]{1,0:T(1,128)}, f32[1,128]{1,0:T(1,128)}) fusion(f32[128]{0:T(128)S(1)} %fusion.6, f32[128]{0:T(128)S(1)} %subtract_reduce_fusion, f32[128]{0:T(128)S(1)} %fusion.15, f32[128]{0:T(128)S(1)} %fusion.14), kind=kLoop, calls=%fused_computation.32 | loop fusion | flops 1408 | bytes 3072 | tf_op jit(solution)/shard_map/sub | solution.py:100
  (13 shorter events, 0.1 us)
Async XLA Ops:
  2.0 15.0 %all-to-all-start = ((bf16[32,16,128]{2,1,0:T(8,128)(2,1)}), bf16[32,16,128]{2,1,0:T(8,128)(2,1)S(1)}, u32[]{:S(2)}, u32[]{:S(2)}) async-start(bf16[32,16,128]{2,1,0:T(8,128)(2,1)} %bitcast.37), calls=%async_computation | async-start | bytes 262144 | tf_op jit(solution)/shard_map/all_to_all | solution.py:46

commit v20 on v15

--- a/solution.py
+++ b/solution.py
@@ -29,7 +29,7 @@
         rows = stage_ref[year * cal_own : year * cal_own + chunk_rows, :]
         tile = jnp.where(is_flag, flags, rows).astype(out_ref.dtype)
         for region in range(region_count):
-            first = (region * year_count + year) * chunk_rows
+            first = (year * region_count + region) * chunk_rows
             out_ref[first : first + chunk_rows, :] = tile
 
 
@@ -43,7 +43,7 @@
         scratch_shapes=[pltpu.VMEM((temps.shape[0] + 1, lon_own), jnp.float32)],
     )(temps, flags.reshape(1, lon_own))
     rows = rows.reshape(year_count * region_count, chunk_rows, lon_own)
-    return lax.all_to_all(rows, ("region", "year"), 0, 0, tiled=True)
+    return lax.all_to_all(rows, ("year", "region"), 0, 0, tiled=True)
 
 
 def coarse_from_samples(samples, count_all, bin_count):
@@ -79,7 +79,7 @@
     span = WIN + cal_own - 1
     count_all = float(year_count * WIN)
     received = gather_windows(daily_temps[0], land_mask, span, cal_own)
-    received = received.reshape(region_count, year_count, span + 1, lon_own)
+    received = jnp.swapaxes(received.reshape(year_count, region_count, span + 1, lon_own), 0, 1)
     region = lax.axis_index("region")
     center = lax.dynamic_index_in_dim(received, region, 0, keepdims=False)
     west = lax.dynamic_index_in_dim(received, lax.rem(region + region_count - 1, region_count), 0, keepdims=False)

time: 19 us -> 19.5 us (1.026)
  waiting for transfers between devices: 7.7 us -> 8.19 us
    all_to_all x1, waiting for transfers between devices: 7.7 us -> 8.19 us  [gather_windows(): return lax.all_to_all(rows, ('year', 'region'), 0, 0, tiled=True)]
where the time goes in v20:
time: 19.5 us; the launch traced here: 19.3 us
  waiting for transfers between devices  8.19 us (42%)
  starting transfers between devices  7.3 us (37%)
  other arithmetic  1.64 us (8%)
  Pallas kernels  1.35 us (7%)
  between operations  0.7 us (4%)
    all_to_all x1, waiting for transfers between devices, gather_windows(): return lax.all_to_all(rows, ('year', 'region'), 0, 0, tiled=True)  8.19 us
    all_to_all x1, starting transfers between devices, gather_windows(): return lax.all_to_all(rows, ('year', 'region'), 0, 0, tiled=True)  7.3 us
    pallas_call x1, Pallas kernels, gather_windows(): pl.pallas_call(functools.partial(chunk_kernel, span, cal_own, year_count,...  1.35 us
    sub x1, other arithmetic, shards(): refined = coarse - STEP_SIZE * (cdf / count_all - QUANT_LEVEL)  0.52 us
    reduce_sum x2, other arithmetic, running(): jnp.sum(jnp.clip(points[None] + 1.0 - scaled[:, None, :], 0.0, 1.0), axis=0)  0.48 us
  transfers between devices with their start and end apart: 1, of which 1 were waited for; matrix products, arithmetic and copies ran while one was open for 0% of the time, Pallas kernels for 0%

profile of v20, /device:TPU:0, one launch (start us, length us, event | category | flops | bytes accessed | tf_op | source)
XLA Modules:
  0.0 19.3 jit_solution(1398874796106247773)
XLA Ops:
  0.6 1.3 %shard_map.41 = bf16[512,128]{1,0:T(8,128)(2,1)} custom-call(bf16[22,128]{1,0:T(8,128)(2,1)} %bitcast.39, s32[1,128]{1,0:T(1,128)} %bitcast.41), custom_call_target="tpu_custom_call" | custom-call | tf_op jit(solution)/shard_map/pallas_call | solution.py:40
  2.0 7.3 %all-to-all-start = ((bf16[32,16,128]{2,1,0:T(8,128)(2,1)}), bf16[32,16,128]{2,1,0:T(8,128)(2,1)S(1)}, u32[]{:S(2)}, u32[]{:S(2)}) async-start(bf16[32,16,128]{2,1,0:T(8,128)(2,1)} %bitcast.37), calls=%async_computation | async-start | bytes 262144 | tf_op jit(solution)/shard_map/all_to_all | solution.py:46
  9.3 8.2 %all-to-all-done = bf16[32,16,128]{2,1,0:T(8,128)(2,1)S(1)} async-done(((bf16[32,16,128]{2,1,0:T(8,128)(2,1)}), bf16[32,16,128]{2,1,0:T(8,128)(2,1)S(1)}, u32[]{:S(2)}, u32[]{:S(2)}) %all-to-all-start) | async-done | bytes 131104 | tf_op jit(solution)/shard_map/all_to_all | solution.py:46
  17.5 0.1 fusion.20
  17.6 0.1 slice_convert_fusion
  17.7 0.1 subtract_bitcast_fusion
  17.8 0.1 add_bitcast_fusion
  17.9 0.1 multiply_clamp_fusion
  18.0 0.3 %clamp_reduce_fusion = f32[32,128]{1,0:T(8,128)S(1)} fusion(f32[120,128]{1,0:T(8,128)S(1)} %min.28, f32[32]{0:T(128)S(1)} %multiply_add_fusion.1), kind=kLoop, calls=%fused_computation | loop fusion | flops 1470464 | bytes 77952 | tf_op jit(solution)/shard_map/reduce_sum | solution.py:57
  18.4 0.1 broadcast_add_fusion.1
  18.4 0.2 clamp_reduce_fusion.1
  18.7 0.1 fusion.6
  18.7 0.5 %bitcast_subtract_fusion = (f32[1,128]{1,0:T(1,128)}, f32[1,128]{1,0:T(1,128)}) fusion(f32[128]{0:T(128)S(1)} %fusion.6, f32[128]{0:T(128)S(1)} %subtract_reduce_fusion, f32[128]{0:T(128)S(1)} %fusion.15, f32[128]{0:T(128)S(1)} %fusion.14), kind=kLoop, calls=%fused_computation.32 | loop fusion | flops 1408 | bytes 3072 | tf_op jit(solution)/shard_map/sub | solution.py:100
  (13 shorter events, 0.2 us)
Async XLA Ops:
  2.0 15.5 %all-to-all-start = ((bf16[32,16,128]{2,1,0:T(8,128)(2,1)}), bf16[32,16,128]{2,1,0:T(8,128)(2,1)S(1)}, u32[]{:S(2)}, u32[]{:S(2)}) async-start(bf16[32,16,128]{2,1,0:T(8,128)(2,1)} %bitcast.37), calls=%async_computation | async-start | bytes 262144 | tf_op jit(solution)/shard_map/all_to_all | solution.py:46

commit v21 on v15

--- a/solution.py
+++ b/solution.py
@@ -18,19 +18,26 @@
 STEP_SIZE = 2.0
 
 
-def chunk_kernel(span, cal_own, year_count, region_count, temps_ref, mask_ref, out_ref, stage_ref):
+def chunk_kernel(span, cal_own, year_count, region_count, temps_ref, mask_ref, out_hbm, stage_ref, tiles_ref, sems):
     days_in = temps_ref.shape[0]
     chunk_rows = span + 1
     stage_ref[0:days_in, :] = temps_ref[...].astype(jnp.float32)
     flags = mask_ref[...].astype(jnp.float32)
     stage_ref[days_in : days_in + 1, :] = flags
-    is_flag = lax.broadcasted_iota(jnp.int32, (chunk_rows, out_ref.shape[1]), 0) == span
+    is_flag = lax.broadcasted_iota(jnp.int32, (chunk_rows, tiles_ref.shape[2]), 0) == span
+    copies = []
     for year in range(year_count):
         rows = stage_ref[year * cal_own : year * cal_own + chunk_rows, :]
-        tile = jnp.where(is_flag, flags, rows).astype(out_ref.dtype)
+        tiles_ref[year] = jnp.where(is_flag, flags, rows).astype(tiles_ref.dtype)
         for region in range(region_count):
             first = (region * year_count + year) * chunk_rows
-            out_ref[first : first + chunk_rows, :] = tile
+            copy = pltpu.make_async_copy(
+                tiles_ref.at[year], out_hbm.at[pl.ds(first, chunk_rows)], sems.at[year * region_count + region]
+            )
+            copy.start()
+            copies.append(copy)
+    for copy in copies:
+        copy.wait()
 
 
 def gather_windows(temps, flags, span, cal_own):
@@ -40,7 +47,12 @@
     rows = pl.pallas_call(
         functools.partial(chunk_kernel, span, cal_own, year_count, region_count),
         out_shape=jax.ShapeDtypeStruct((year_count * region_count * chunk_rows, lon_own), temps.dtype),
-        scratch_shapes=[pltpu.VMEM((temps.shape[0] + 1, lon_own), jnp.float32)],
+        out_specs=pl.BlockSpec(memory_space=pl.ANY),
+        scratch_shapes=[
+            pltpu.VMEM((temps.shape[0] + 1, lon_own), jnp.float32),
+            pltpu.VMEM((year_count, chunk_rows, lon_own), temps.dtype),
+            pltpu.SemaphoreType.DMA((year_count * region_count,)),
+        ],
     )(temps, flags.reshape(1, lon_own))
     rows = rows.reshape(year_count * region_count, chunk_rows, lon_own)
     return lax.all_to_all(rows, ("region", "year"), 0, 0, tiled=True)

time: 19 us -> 19.4 us (1.021)
  Pallas kernels: 1.35 us -> 1.69 us
    pallas_call x1, Pallas kernels: 1.35 us -> 1.69 us  [gather_windows(): pl.pallas_call(functools.partial(chunk_kernel, span, cal_own, year_count,...]
where the time goes in v21:
time: 19.4 us; the launch traced here: 19.1 us
  waiting for transfers between devices  7.7 us (40%)
  starting transfers between devices  7.3 us (38%)
  Pallas kernels  1.69 us (9%)
  other arithmetic  1.63 us (8%)
  between operations  0.71 us (4%)
    all_to_all x1, waiting for transfers between devices, gather_windows(): return lax.all_to_all(rows, ('region', 'year'), 0, 0, tiled=True)  7.7 us
    all_to_all x1, starting transfers between devices, gather_windows(): return lax.all_to_all(rows, ('region', 'year'), 0, 0, tiled=True)  7.3 us
    pallas_call x1, Pallas kernels, gather_windows(): pl.pallas_call(functools.partial(chunk_kernel, span, cal_own, year_count,...  1.69 us
    sub x1, other arithmetic, shards(): refined = coarse - STEP_SIZE * (cdf / count_all - QUANT_LEVEL)  0.52 us
    reduce_sum x2, other arithmetic, running(): jnp.sum(jnp.clip(points[None] + 1.0 - scaled[:, None, :], 0.0, 1.0), axis=0)  0.48 us
  transfers between devices with their start and end apart: 1, of which 1 were waited for; matrix products, arithmetic and copies ran while one was open for 0% of the time, Pallas kernels for 0%

profile of v21, /device:TPU:0, one launch (start us, length us, event | category | flops | bytes accessed | tf_op | source)
XLA Modules:
  0.0 19.1 jit_solution(1962522658493650256)
XLA Ops:
  0.6 1.7 %shard_map.41 = bf16[512,128]{1,0:T(8,128)(2,1)} custom-call(bf16[22,128]{1,0:T(8,128)(2,1)} %bitcast.39, s32[1,128]{1,0:T(1,128)} %bitcast.41), custom_call_target="tpu_custom_call" | custom-call | tf_op jit(solution)/shard_map/pallas_call | solution.py:47
  2.3 7.3 %all-to-all-start = ((bf16[32,16,128]{2,1,0:T(8,128)(2,1)}), bf16[32,16,128]{2,1,0:T(8,128)(2,1)S(1)}, u32[]{:S(2)}, u32[]{:S(2)}) async-start(bf16[32,16,128]{2,1,0:T(8,128)(2,1)} %bitcast.37), calls=%async_computation | async-start | bytes 262144 | tf_op jit(solution)/shard_map/all_to_all | solution.py:58
  9.7 7.7 %all-to-all-done = bf16[32,16,128]{2,1,0:T(8,128)(2,1)S(1)} async-done(((bf16[32,16,128]{2,1,0:T(8,128)(2,1)}), bf16[32,16,128]{2,1,0:T(8,128)(2,1)S(1)}, u32[]{:S(2)}, u32[]{:S(2)}) %all-to-all-start) | async-done | bytes 131104 | tf_op jit(solution)/shard_map/all_to_all | solution.py:58
  17.4 0.1 fusion.20
  17.5 0.1 slice_convert_fusion
  17.6 0.1 subtract_bitcast_fusion
  17.6 0.1 add_bitcast_fusion
  17.7 0.1 multiply_clamp_fusion
  17.9 0.3 %clamp_reduce_fusion = f32[32,128]{1,0:T(8,128)S(1)} fusion(f32[120,128]{1,0:T(8,128)S(1)} %min.28, f32[32]{0:T(128)S(1)} %multiply_add_fusion.1), kind=kLoop, calls=%fused_computation | loop fusion | flops 1470464 | bytes 77952 | tf_op jit(solution)/shard_map/reduce_sum | solution.py:69
  18.2 0.1 broadcast_add_fusion.1
  18.3 0.2 clamp_reduce_fusion.1
  18.5 0.1 fusion.6
  18.6 0.5 %bitcast_subtract_fusion = (f32[1,128]{1,0:T(1,128)}, f32[1,128]{1,0:T(1,128)}) fusion(f32[128]{0:T(128)S(1)} %fusion.6, f32[128]{0:T(128)S(1)} %subtract_reduce_fusion, f32[128]{0:T(128)S(1)} %fusion.15, f32[128]{0:T(128)S(1)} %fusion.14), kind=kLoop, calls=%fused_computation.32 | loop fusion | flops 1408 | bytes 3072 | tf_op jit(solution)/shard_map/sub | solution.py:112
  (13 shorter events, 0.1 us)
Async XLA Ops:
  2.3 15.1 %all-to-all-start = ((bf16[32,16,128]{2,1,0:T(8,128)(2,1)}), bf16[32,16,128]{2,1,0:T(8,128)(2,1)S(1)}, u32[]{:S(2)}, u32[]{:S(2)}) async-start(bf16[32,16,128]{2,1,0:T(8,128)(2,1)} %bitcast.37), calls=%async_computation | async-start | bytes 262144 | tf_op jit(solution)/shard_map/all_to_all | solution.py:58
